TPU v7x, 128 devices: a whole 4x4x4 slice. The times are simulated.
128 devices in a mesh: segment: 2 (over core), tensor: 4 (over x), batch: 16 (over z, y).
Axes of the slice: x: 4, y: 4, z: 4, core: 2. Of those that a mesh axis runs over, the one named last changes fastest.
Arguments:
- hidden: bfloat16 [3, 128, 16384], P(None, 'tensor', 'batch'), may hold values from -6 to 6
- norm_gain: bfloat16 [2, 16384], P('segment', 'batch'), may hold values from 0.25 to 1.75
- w_query: bfloat16 [2, 16384, 8192], P('segment', 'batch', 'tensor'), may hold values from -0.046875 to 0.046875
- key_value_weight: bfloat16 [2, 16384, 2048], P('segment', 'batch', 'tensor'), may hold values from -0.046875 to 0.046875
- w_out: bfloat16 [2, 8192, 16384], P('segment', 'tensor', 'batch'), may hold values from -0.0625 to 0.0625
- key_value_cache: bfloat16 [2, 32, 8, 256, 256], P('segment', 'batch', 'tensor'), may hold values from -6 to 6
- owner_slot: int32 [32], replicated, may hold values from 0 to 31, each once
- accepted: int32 [3, 32], replicated, may hold values from 1 to 4
Outputs:
- layer_outputs: bfloat16 [2, 3, 128, 16384], P('segment', None, 'tensor', 'batch')
- new_cache: bfloat16 [2, 32, 8, 12, 256], P('segment', 'batch', 'tensor')
Inputs may be any that keep to these rules, and one draw needn't show every extreme that they name: `owner_slot`: each slot is held by exactly one request; slot s belongs to index s // 2 of batch.
All inputs are finite; a program needn't handle non-finite values.
Results may differ from a plain program's by a relative error of at most 0.0095.
Values may be sent and summed in bfloat16 or wider, within the bound.
No kernel may reach another device: no remote copies, remote signals or barrier semaphores. Data moves between devices by JAX's collectives and lax.ppermute only.
A program may use at most 64 MiB of HBM per device.

v0:
```python
import jax
import jax.numpy as jnp
from jax import lax
from jax.sharding import PartitionSpec as P

MODEL_WIDTH = 16384
HEAD_SIZE = 128
DRAFT_BLOCK = 4
DECODE_ROUNDS = 3
GROUP_HEADS = 8


BATCH_INNER = 4


def shifted(x, axis, fn):
    n = lax.axis_size(axis)
    return lax.ppermute(x, axis, [(i, fn(i, n)) for i in range(n)])


def along_tensor(x, k):
    return shifted(x, "tensor", lambda i, n: (i + k) % n)


def along_y(x, k):
    m = BATCH_INNER
    return shifted(x, "batch", lambda i, n: (i // m) * m + (i % m + k) % m)


def along_z(x, k):
    m = BATCH_INNER
    return shifted(x, "batch", lambda i, n: ((i // m + k) % (n // m)) * m + i % m)


def spread(blocks, pos, send):
    m = blocks.shape[0]
    out = [lax.dynamic_index_in_dim(blocks, pos, 0, keepdims=False)]
    for k in range(1, m):
        piece = lax.dynamic_index_in_dim(blocks, (pos + k) % m, 0, keepdims=False)
        out.append(send(piece, k))
    return out


def gather_from(x, pos, m, send):
    out = [x] + [send(x, k) for k in range(1, m)]
    order = (pos - jnp.arange(m)) % m
    return jnp.take(jnp.stack(out), order, axis=0)


def passed_along(block, axis, distance):
    devices = range(lax.axis_size(axis))
    route = [(i - distance, i) for i in devices if i - distance in devices]
    return lax.ppermute(block, axis, route)


def shards(
    hidden, norm_gain, w_query, key_value_weight, w_out, key_value_cache, owner_slot, accepted
):
    f32, bf16 = jnp.float32, jnp.bfloat16
    rounds, rows_local, width_local = hidden.shape
    n_segment = lax.axis_size("segment")
    segment = lax.axis_index("segment")
    tensor = lax.axis_index("tensor")
    group = lax.axis_index("batch")
    requests = owner_slot.shape[0]
    rows_total = requests * DRAFT_BLOCK
    slots_local = key_value_cache.shape[1]
    kv_local = key_value_cache.shape[2]
    query_cols = w_query.shape[2]
    kv_cols = key_value_weight.shape[2]
    block = rounds * DRAFT_BLOCK
    own_rows = slots_local * block
    req_local = rows_local // DRAFT_BLOCK
    scale = HEAD_SIZE ** (-0.5)
    gain = norm_gain[0].astype(f32)
    cache_local = key_value_cache[0]

    onehot = (owner_slot[None, :] == jnp.arange(requests)[:, None]).astype(jnp.int32)
    inverse = jnp.sum(onehot * jnp.arange(requests)[None, :], axis=1)
    acc_slot = jnp.sum(onehot[None] * accepted[:, None, :], axis=2)
    acc_own = lax.dynamic_slice_in_dim(acc_slot, group * slots_local, slots_local, 1)

    rr = jnp.arange(rounds)
    jj = jnp.arange(DRAFT_BLOCK)
    sort_index = (
        rr[None, :, None] * rows_total + inverse[:, None, None] * DRAFT_BLOCK + jj[None, None, :]
    ).reshape(-1)
    own_req = tensor * req_local + jnp.arange(req_local)
    own_index = (
        owner_slot[own_req][None, :, None] * block + rr[:, None, None] * DRAFT_BLOCK + jj[None, None, :]
    ).reshape(-1)

    pos = jnp.arange(block)
    r2 = pos // DRAFT_BLOCK
    place = pos % DRAFT_BLOCK
    acc_pos = acc_own[r2, :].T
    earlier = (r2[None, None, None, :] < rr[None, :, None, None]) & (
        place[None, None, None, :] < acc_pos[:, None, None, :]
    )
    same = (r2[None, :] == rr[:, None])[:, None, :] & (place[None, None, :] <= jj[None, :, None])
    valid = earlier | same[None]
    keep = place[None, :] < acc_pos

    n_tensor = lax.axis_size("tensor")
    n_y = BATCH_INNER
    n_z = lax.axis_size("batch") // n_y
    z_pos = group // n_y
    y_pos = group % n_y

    back_index = (
        owner_slot[None, :, None] * block + rr[:, None, None] * DRAFT_BLOCK + jj[None, None, :]
    ).reshape(-1)

    def layer(x_sorted, last):
        xf = x_sorted.astype(f32)
        sq = jnp.sum(xf * xf, axis=1, keepdims=True)
        sq_hi = sq.astype(bf16)
        sq_lo = (sq - sq_hi.astype(f32)).astype(bf16)
        xg = (xf * gain[None, :]).astype(bf16)
        first = jnp.dot(xg, w_query[0], preferred_element_type=f32)
        second = jnp.dot(xg, key_value_weight[0], preferred_element_type=f32)
        proj = jnp.concatenate([first.astype(bf16), second.astype(bf16), sq_hi, sq_lo], axis=1)
        cols = proj.shape[1]
        blocks = proj.reshape(n_z, n_y, own_rows, cols)
        cut = (cols // 2) // 128 * 128
        first_y = blocks[..., :cut].transpose(1, 0, 2, 3)
        first_z = blocks[..., cut:]
        part_a = sum(r.astype(f32) for r in spread(first_y, y_pos, along_y))
        part_b = sum(r.astype(f32) for r in spread(first_z, z_pos, along_z))
        total_a = sum(spread(part_a, z_pos, along_z))
        total_b = sum(spread(part_b, y_pos, along_y))
        total = jnp.concatenate([total_a, total_b], axis=1)
        total_sq = total[:, query_cols + kv_cols] + total[:, query_cols + kv_cols + 1]
        inv = lax.rsqrt(total_sq / MODEL_WIDTH + 1e-05)[:, None]
        query = (total[:, :query_cols] * inv).astype(bf16)
        keyval = (total[:, query_cols : query_cols + kv_cols] * inv).astype(bf16)
        query_heads = query.reshape(
            slots_local, rounds, DRAFT_BLOCK, kv_local, GROUP_HEADS, HEAD_SIZE
        )
        fresh = keyval.reshape(slots_local, block, kv_local, 2 * HEAD_SIZE).transpose(0, 2, 1, 3)
        s_cache = jnp.einsum(
            "srjhgd,shld->shgrjl", query_heads, cache_local[..., :HEAD_SIZE],
            preferred_element_type=f32,
        ) * scale
        s_fresh = jnp.einsum(
            "srjhgd,shld->shgrjl", query_heads, fresh[..., :HEAD_SIZE],
            preferred_element_type=f32,
        ) * scale
        s_fresh = jnp.where(valid[:, None, None], s_fresh, -1e30)
        scores = jnp.concatenate([s_cache, s_fresh], axis=-1)
        weights = jax.nn.softmax(scores, axis=-1).astype(bf16)
        values = jnp.concatenate([cache_local[..., HEAD_SIZE:], fresh[..., HEAD_SIZE:]], axis=2)
        attended = jnp.einsum(
            "shgrjl,shld->srjhgd", weights, values, preferred_element_type=f32
        )
        attended = attended.astype(bf16).reshape(own_rows, query_cols)
        by_z = gather_from(attended, z_pos, n_z, along_z)
        by_zy = gather_from(by_z, y_pos, n_y, along_y)
        gathered = by_zy.transpose(1, 0, 2, 3).reshape(-1, query_cols)
        partial = jnp.dot(gathered, w_out[0], preferred_element_type=f32)
        ext_new = jnp.where(keep[:, None, :, None], fresh, jnp.zeros_like(fresh))
        if last:
            natural = jnp.take(partial.astype(bf16), back_index, axis=0)
            pieces = natural.reshape(rounds, n_tensor, rows_local, width_local).transpose(1, 0, 2, 3)
            mine = sum(r.astype(f32) for r in spread(pieces, tensor, along_tensor))
            x_own = jnp.take(xf, own_index, axis=0).reshape(rounds, rows_local, width_local)
            return None, (x_own + mine).astype(bf16), ext_new
        quarter = partial.shape[0] // n_tensor
        pieces = partial.astype(bf16).reshape(n_tensor, quarter, width_local)
        mine = sum(r.astype(f32) for r in spread(pieces, tensor, along_tensor))
        x_mine = lax.dynamic_index_in_dim(
            xf.reshape(n_tensor, quarter, width_local), tensor, 0, keepdims=False
        )
        x_mine = (x_mine + mine).astype(bf16)
        x_new = gather_from(x_mine, tensor, n_tensor, along_tensor).reshape(-1, width_local)
        rec_new = jnp.take(x_new, own_index, axis=0).reshape(rounds, rows_local, width_local)
        return x_new, rec_new, ext_new

    rows_all = gather_from(hidden, tensor, n_tensor, along_tensor)
    rows_all = rows_all.transpose(1, 0, 2, 3).reshape(-1, width_local)
    x = jnp.take(rows_all, sort_index, axis=0)
    record = None
    ext = None
    for step in range(n_segment):
        x_new, rec_new, ext_new = layer(x, step + 1 == n_segment)
        if step == 0:
            record, ext = rec_new, ext_new
        else:
            active = segment == step
            record = jnp.where(active, rec_new, record)
            ext = jnp.where(active, ext_new, ext)
        if step + 1 < n_segment:
            x = passed_along(x_new, "segment", 1)
    return (record[None], ext[None])


def solution(mesh):
    in_specs = (
        P(None, "tensor", "batch"),
        P("segment", "batch"),
        P("segment", "batch", "tensor"),
        P("segment", "batch", "tensor"),
        P("segment", "tensor", "batch"),
        P("segment", "batch", "tensor", None, None),
        P(),
        P(),
    )
    out_specs = (P("segment", None, "tensor", "batch"), P("segment", "batch", "tensor", None, None))
    return jax.shard_map(shards, mesh=mesh, in_specs=in_specs, out_specs=out_specs, check_vma=False)
```

profile of v0, /device:TPU:0, one launch (start us, length us, event | category | flops | bytes accessed | tf_op | source)
XLA Modules:
  0.0 233.3 jit_solution(16708702370408987090)
XLA Ops:
  19.5 4.1 %fusion.8 = bf16[384,2048]{1,0:T(8,128)(2,1)S(1)} fusion(bf16[1,1024,2048]{2,1,0:T(8,128)(2,1)} %param.16, f32[1024]{0:T(1024)S(1)} %bitcast.311, bf16[384,1024]{1,0:T(8,128)(2,1)S(1)} %gather_fusion.6, pred[384]{0:T(512)(128)(4,1)S(1)} %get-tuple-element.60), kind=kOutput, calls=%fused_computation.20 | convolution fusion | flops 1612972032 | bytes 6558080 | tf_op jit(solution)/shard_map/dot_general | solution.py:120
  25.6 3.2 %collective-permute-start.10 = (bf16[4,24,1280]{2,1,0:T(8,128)(2,1)}, bf16[4,24,1280]{2,1,0:T(8,128)(2,1)}, u32[]{:S(2)}, u32[]{:S(2)}) collective-permute-start(bf16[4,24,1280]{2,1,0:T(8,128)(2,1)} %get-tuple-element.28), channel_id=1, source_target_pairs={{0,2},{1,3},{2,0},{3,1},{4,6},{5,7},{6,4},{7,5},{8,10},{9,11},{10,... | collective-permute-start | bytes 737288 | tf_op jit(solution)/shard_map/ppermute | solution.py:18
  33.3 3.9 %concatenate.36 = bf16[4,4,24,2562]{3,2,1,0:T(8,128)(2,1)} concatenate(bf16[4,4,24,2048]{3,2,1,0:T(8,128)(2,1)S(1)} %bitcast.269, bf16[4,4,24,512]{3,2,1,0:T(8,128)(2,1)} %bitcast.295, bf16[4,4,24,1]{3,2,1,0:T(8,128)(2,1)S(1)} %copy.78, bf16[4,4,24,1]{3,2,1,0:T(8,128)(2,1)} %copy.79), dimensions={3} | concatenate | bytes 3935232 | tf_op jit(solution)/shard_map/concatenate | solution.py:122
  40.6 3.6 %collective-permute-start.4 = (bf16[4,24,1282]{2,1,0:T(8,128)(2,1)S(1)}, bf16[4,24,1282]{2,1,0:T(8,128)(2,1)S(1)}, u32[]{:S(2)}, u32[]{:S(2)}) collective-permute-start(bf16[4,24,1282]{2,1,0:T(8,128)(2,1)S(1)} %get-tuple-element.22), channel_id=1, source_target_pairs={{0,8},{1,9},{2,10},{3,11},{4,12},{5,13},{6,14},{7,15},{8,0},{9,1},... | collective-permute-start | bytes 738440 | tf_op jit(solution)/shard_map/ppermute | solution.py:18
  52.1 5.1 %collective-permute-done.4 = bf16[4,24,1282]{2,1,0:T(8,128)(2,1)S(1)} collective-permute-done((bf16[4,24,1282]{2,1,0:T(8,128)(2,1)S(1)}, bf16[4,24,1282]{2,1,0:T(8,128)(2,1)S(1)}, u32[]{:S(2)}, u32[]{:S(2)}) %collective-permute-start.4) | collective-permute-done | bytes 246176 | tf_op jit(solution)/shard_map/ppermute | solution.py:18
  77.1 3.6 %collective-permute-start.19 = (bf16[4,24,2048]{2,1,0:T(8,128)(2,1)S(1)}, bf16[4,24,2048]{2,1,0:T(8,128)(2,1)S(1)}, u32[]{:S(2)}, u32[]{:S(2)}) collective-permute-start(bf16[4,24,2048]{2,1,0:T(8,128)(2,1)S(1)} %broadcast_select_fusion.2), channel_id=1, source_target_pairs={{0,2},{1,3},{2,0},{3,1},{4,6},{5,7},{6,4},{7,5},{8,10},{9,11},{10,... | collective-permute-start | bytes 1179656 | tf_op jit(solution)/shard_map/ppermute | solution.py:18
  81.0 7.3 %collective-permute-done.18 = bf16[4,24,2048]{2,1,0:T(8,128)(2,1)S(1)} collective-permute-done((bf16[4,24,2048]{2,1,0:T(8,128)(2,1)S(1)}, bf16[4,24,2048]{2,1,0:T(8,128)(2,1)S(1)}, u32[]{:S(2)}, u32[]{:S(2)}) %collective-permute-start.18) | collective-permute-done | bytes 393248 | tf_op jit(solution)/shard_map/ppermute | solution.py:18
  88.2 8.0 %collective-permute-done.19 = bf16[4,24,2048]{2,1,0:T(8,128)(2,1)S(1)} collective-permute-done((bf16[4,24,2048]{2,1,0:T(8,128)(2,1)S(1)}, bf16[4,24,2048]{2,1,0:T(8,128)(2,1)S(1)}, u32[]{:S(2)}, u32[]{:S(2)}) %collective-permute-start.19) | collective-permute-done | bytes 393248 | tf_op jit(solution)/shard_map/ppermute | solution.py:18
  106.6 5.2 %collective-permute-done.21 = bf16[96,1024]{1,0:T(8,128)(2,1)S(1)} collective-permute-done((bf16[96,1024]{1,0:T(8,128)(2,1)S(1)}, bf16[96,1024]{1,0:T(8,128)(2,1)S(1)}, u32[]{:S(2)}, u32[]{:S(2)}) %collective-permute-start.21) | collective-permute-done | bytes 196640 | tf_op jit(solution)/shard_map/ppermute | solution.py:18
  114.8 3.7 %collective-permute-start.25 = (bf16[96,1024]{1,0:T(8,128)(2,1)S(1)}, bf16[96,1024]{1,0:T(8,128)(2,1)S(1)}, u32[]{:S(2)}, u32[]{:S(2)}) collective-permute-start(bf16[96,1024]{1,0:T(8,128)(2,1)S(1)} %fusion.49), channel_id=1, source_target_pairs={{0,32},{16,48},{32,0},{48,16},{1,33},{17,49},{33,1},{49,17},{2,34}... | collective-permute-start | bytes 589832 | tf_op jit(solution)/shard_map/ppermute | solution.py:18
  118.5 3.4 %collective-permute-done.24 = bf16[96,1024]{1,0:T(8,128)(2,1)S(1)} collective-permute-done((bf16[96,1024]{1,0:T(8,128)(2,1)S(1)}, bf16[96,1024]{1,0:T(8,128)(2,1)S(1)}, u32[]{:S(2)}, u32[]{:S(2)}) %collective-permute-start.24) | collective-permute-done | bytes 196640 | tf_op jit(solution)/shard_map/ppermute | solution.py:18
  121.9 5.0 %collective-permute-done.25 = bf16[96,1024]{1,0:T(8,128)(2,1)S(1)} collective-permute-done((bf16[96,1024]{1,0:T(8,128)(2,1)S(1)}, bf16[96,1024]{1,0:T(8,128)(2,1)S(1)}, u32[]{:S(2)}, u32[]{:S(2)}) %collective-permute-start.25) | collective-permute-done | bytes 196640 | tf_op jit(solution)/shard_map/ppermute | solution.py:18
  133.0 4.2 %fusion.11 = bf16[384,2048]{1,0:T(8,128)(2,1)S(1)} fusion(bf16[1,1024,2048]{2,1,0:T(8,128)(2,1)} %param.16, bf16[384,1024]{1,0:T(8,128)(2,1)} %copy-done.4, f32[1024]{0:T(1024)S(1)} %bitcast.313), kind=kOutput, calls=%fused_computation.21 | convolution fusion | flops 1612578816 | bytes 6557696 | tf_op jit(solution)/shard_map/dot_general | solution.py:120
  140.0 3.9 %concatenate.42 = bf16[4,4,24,2562]{3,2,1,0:T(8,128)(2,1)} concatenate(bf16[4,4,24,2048]{3,2,1,0:T(8,128)(2,1)S(1)} %bitcast.271, bf16[4,4,24,512]{3,2,1,0:T(8,128)(2,1)} %bitcast.296, bf16[4,4,24,1]{3,2,1,0:T(8,128)(2,1)S(1)} %copy.87, bf16[4,4,24,1]{3,2,1,0:T(8,128)(2,1)} %copy.88), dimensions={3} | concatenate | bytes 3935232 | tf_op jit(solution)/shard_map/concatenate | solution.py:122
  147.2 4.1 %collective-permute-start.35 = (bf16[4,24,1280]{2,1,0:T(8,128)(2,1)S(1)}, bf16[4,24,1280]{2,1,0:T(8,128)(2,1)S(1)}, u32[]{:S(2)}, u32[]{:S(2)}) collective-permute-start(bf16[4,24,1280]{2,1,0:T(8,128)(2,1)S(1)} %get-tuple-element.25), channel_id=1, source_target_pairs={{0,2},{1,3},{2,0},{3,1},{4,6},{5,7},{6,4},{7,5},{8,10},{9,11},{10,... | collective-permute-start | bytes 737288 | tf_op jit(solution)/shard_map/ppermute | solution.py:18
  151.5 3.8 %collective-permute-start.29 = (bf16[4,24,1282]{2,1,0:T(8,128)(2,1)S(1)}, bf16[4,24,1282]{2,1,0:T(8,128)(2,1)S(1)}, u32[]{:S(2)}, u32[]{:S(2)}) collective-permute-start(bf16[4,24,1282]{2,1,0:T(8,128)(2,1)S(1)} %get-tuple-element.19), channel_id=1, source_target_pairs={{0,8},{1,9},{2,10},{3,11},{4,12},{5,13},{6,14},{7,15},{8,0},{9,1},... | collective-permute-start | bytes 738440 | tf_op jit(solution)/shard_map/ppermute | solution.py:18
  158.5 4.1 %collective-permute-done.35 = bf16[4,24,1280]{2,1,0:T(8,128)(2,1)S(1)} collective-permute-done((bf16[4,24,1280]{2,1,0:T(8,128)(2,1)S(1)}, bf16[4,24,1280]{2,1,0:T(8,128)(2,1)S(1)}, u32[]{:S(2)}, u32[]{:S(2)}) %collective-permute-start.35) | collective-permute-done | bytes 245792 | tf_op jit(solution)/shard_map/ppermute | solution.py:18
  163.1 3.8 %collective-permute-start.38 = (f32[24,1280]{1,0:T(8,128)S(1)}, f32[24,1280]{1,0:T(8,128)S(1)}, u32[]{:S(2)}, u32[]{:S(2)}) collective-permute-start(f32[24,1280]{1,0:T(8,128)S(1)} %get-tuple-element.43), channel_id=1, source_target_pairs={{0,8},{1,9},{2,10},{3,11},{4,12},{5,13},{6,14},{7,15},{8,0},{9,1},... | collective-permute-start | bytes 368648 | tf_op jit(solution)/shard_map/ppermute | solution.py:18
  167.5 3.2 %collective-permute-start.31 = (f32[24,1282]{1,0:T(8,128)S(1)}, f32[24,1282]{1,0:T(8,128)S(1)}, u32[]{:S(2)}, u32[]{:S(2)}) collective-permute-start(f32[24,1282]{1,0:T(8,128)S(1)} %get-tuple-element.35), channel_id=1, source_target_pairs={{0,1},{1,2},{2,3},{3,0},{4,5},{5,6},{6,7},{7,4},{8,9},{9,10},{10,1... | collective-permute-start | bytes 369224 | tf_op jit(solution)/shard_map/ppermute | solution.py:18
  181.1 3.3 %collective-permute-start.41 = (bf16[24,2048]{1,0:T(8,128)(2,1)}, bf16[24,2048]{1,0:T(8,128)(2,1)}, u32[]{:S(2)}, u32[]{:S(2)}) collective-permute-start(bf16[24,2048]{1,0:T(8,128)(2,1)} %reshape.637), channel_id=1, source_target_pairs={{0,8},{1,9},{2,10},{3,11},{4,12},{5,13},{6,14},{7,15},{8,0},{9,1},... | collective-permute-start | bytes 294920 | tf_op jit(solution)/shard_map/ppermute | solution.py:18
  197.2 6.3 %collective-permute-done.43 = bf16[4,24,2048]{2,1,0:T(8,128)(2,1)S(1)} collective-permute-done((bf16[4,24,2048]{2,1,0:T(8,128)(2,1)S(1)}, bf16[4,24,2048]{2,1,0:T(8,128)(2,1)S(1)}, u32[]{:S(2)}, u32[]{:S(2)}) %collective-permute-start.43) | collective-permute-done | bytes 393248 | tf_op jit(solution)/shard_map/ppermute | solution.py:18
  203.5 8.1 %collective-permute-done.44 = bf16[4,24,2048]{2,1,0:T(8,128)(2,1)S(1)} collective-permute-done((bf16[4,24,2048]{2,1,0:T(8,128)(2,1)S(1)}, bf16[4,24,2048]{2,1,0:T(8,128)(2,1)S(1)}, u32[]{:S(2)}, u32[]{:S(2)}) %collective-permute-start.44) | collective-permute-done | bytes 393248 | tf_op jit(solution)/shard_map/ppermute | solution.py:18
  220.8 4.1 %collective-permute-start.47 = (bf16[3,32,1024]{2,1,0:T(8,128)(2,1)S(1)}, bf16[3,32,1024]{2,1,0:T(8,128)(2,1)S(1)}, u32[]{:S(2)}, u32[]{:S(2)}) collective-permute-start(bf16[3,32,1024]{2,1,0:T(8,128)(2,1)S(1)} %get-tuple-element.31), channel_id=1, source_target_pairs={{0,32},{16,48},{32,0},{48,16},{1,33},{17,49},{33,1},{49,17},{2,34}... | collective-permute-start | bytes 589832 | tf_op jit(solution)/shard_map/ppermute | solution.py:18
  225.6 3.8 %collective-permute-done.46 = bf16[3,32,1024]{2,1,0:T(8,128)(2,1)S(1)} collective-permute-done((bf16[3,32,1024]{2,1,0:T(8,128)(2,1)S(1)}, bf16[3,32,1024]{2,1,0:T(8,128)(2,1)S(1)}, u32[]{:S(2)}, u32[]{:S(2)}) %collective-permute-start.46) | collective-permute-done | bytes 196640 | tf_op jit(solution)/shard_map/ppermute | solution.py:18
  (302 shorter events, 122.7 us)
Async XLA Ops:
  0.7 15.4 %collective-permute-start = (bf16[3,32,1024]{2,1,0:T(8,128)(2,1)}, bf16[3,32,1024]{2,1,0:T(8,128)(2,1)S(1)}, u32[]{:S(2)}, u32[]{:S(2)}) collective-permute-start(bf16[3,32,1024]{2,1,0:T(8,128)(2,1)} %param.14), channel_id=1, source_target_pairs={{0,16},{16,32},{32,48},{48,0},{1,17},{17,33},{33,49},{49,1},{2,18}... | collective-permute-start | bytes 589832 | tf_op jit(solution)/shard_map/ppermute | solution.py:18
  2.3 13.8 %collective-permute-start.1 = (bf16[3,32,1024]{2,1,0:T(8,128)(2,1)}, bf16[3,32,1024]{2,1,0:T(8,128)(2,1)S(1)}, u32[]{:S(2)}, u32[]{:S(2)}) collective-permute-start(bf16[3,32,1024]{2,1,0:T(8,128)(2,1)} %param.14), channel_id=1, source_target_pairs={{0,32},{16,48},{32,0},{48,16},{1,33},{17,49},{33,1},{49,17},{2,34}... | collective-permute-start | bytes 589832 | tf_op jit(solution)/shard_map/ppermute | solution.py:18
  5.1 11.0 %collective-permute-start.2 = (bf16[3,32,1024]{2,1,0:T(8,128)(2,1)}, bf16[3,32,1024]{2,1,0:T(8,128)(2,1)S(1)}, u32[]{:S(2)}, u32[]{:S(2)}) collective-permute-start(bf16[3,32,1024]{2,1,0:T(8,128)(2,1)} %param.14), channel_id=1, source_target_pairs={{0,48},{16,0},{32,16},{48,32},{1,49},{17,1},{33,17},{49,33},{2,50}... | collective-permute-start | bytes 589832 | tf_op jit(solution)/shard_map/ppermute | solution.py:18
  25.6 18.6 %collective-permute-start.10 = (bf16[4,24,1280]{2,1,0:T(8,128)(2,1)}, bf16[4,24,1280]{2,1,0:T(8,128)(2,1)}, u32[]{:S(2)}, u32[]{:S(2)}) collective-permute-start(bf16[4,24,1280]{2,1,0:T(8,128)(2,1)} %get-tuple-element.28), channel_id=1, source_target_pairs={{0,2},{1,3},{2,0},{3,1},{4,6},{5,7},{6,4},{7,5},{8,10},{9,11},{10,... | collective-permute-start | bytes 737288 | tf_op jit(solution)/shard_map/ppermute | solution.py:18
  28.8 16.5 %collective-permute-start.11 = (bf16[4,24,1280]{2,1,0:T(8,128)(2,1)}, bf16[4,24,1280]{2,1,0:T(8,128)(2,1)}, u32[]{:S(2)}, u32[]{:S(2)}) collective-permute-start(bf16[4,24,1280]{2,1,0:T(8,128)(2,1)} %get-tuple-element.27), channel_id=1, source_target_pairs={{0,3},{1,0},{2,1},{3,2},{4,7},{5,4},{6,5},{7,6},{8,11},{9,8},{10,9... | collective-permute-start | bytes 737288 | tf_op jit(solution)/shard_map/ppermute | solution.py:18
  29.8 15.4 %collective-permute-start.9 = (bf16[4,24,1280]{2,1,0:T(8,128)(2,1)}, bf16[4,24,1280]{2,1,0:T(8,128)(2,1)}, u32[]{:S(2)}, u32[]{:S(2)}) collective-permute-start(bf16[4,24,1280]{2,1,0:T(8,128)(2,1)} %get-tuple-element.26), channel_id=1, source_target_pairs={{0,1},{1,2},{2,3},{3,0},{4,5},{5,6},{6,7},{7,4},{8,9},{9,10},{10,1... | collective-permute-start | bytes 737288 | tf_op jit(solution)/shard_map/ppermute | solution.py:18
  38.7 11.8 %collective-permute-start.3 = (bf16[4,24,1282]{2,1,0:T(8,128)(2,1)S(1)}, bf16[4,24,1282]{2,1,0:T(8,128)(2,1)S(1)}, u32[]{:S(2)}, u32[]{:S(2)}) collective-permute-start(bf16[4,24,1282]{2,1,0:T(8,128)(2,1)S(1)} %get-tuple-element.20), channel_id=1, source_target_pairs={{0,4},{1,5},{2,6},{3,7},{4,8},{5,9},{6,10},{7,11},{8,12},{9,13},{1... | collective-permute-start | bytes 738440 | tf_op jit(solution)/shard_map/ppermute | solution.py:18
  40.6 16.5 %collective-permute-start.4 = (bf16[4,24,1282]{2,1,0:T(8,128)(2,1)S(1)}, bf16[4,24,1282]{2,1,0:T(8,128)(2,1)S(1)}, u32[]{:S(2)}, u32[]{:S(2)}) collective-permute-start(bf16[4,24,1282]{2,1,0:T(8,128)(2,1)S(1)} %get-tuple-element.22), channel_id=1, source_target_pairs={{0,8},{1,9},{2,10},{3,11},{4,12},{5,13},{6,14},{7,15},{8,0},{9,1},... | collective-permute-start | bytes 738440 | tf_op jit(solution)/shard_map/ppermute | solution.py:18
  44.2 12.9 %collective-permute-start.5 = (bf16[4,24,1282]{2,1,0:T(8,128)(2,1)S(1)}, bf16[4,24,1282]{2,1,0:T(8,128)(2,1)S(1)}, u32[]{:S(2)}, u32[]{:S(2)}) collective-permute-start(bf16[4,24,1282]{2,1,0:T(8,128)(2,1)S(1)} %get-tuple-element.21), channel_id=1, source_target_pairs={{0,12},{1,13},{2,14},{3,15},{4,0},{5,1},{6,2},{7,3},{8,4},{9,5},{1... | collective-permute-start | bytes 738440 | tf_op jit(solution)/shard_map/ppermute | solution.py:18
  46.7 14.5 %collective-permute-start.12 = (f32[24,1280]{1,0:T(8,128)S(1)}, f32[24,1280]{1,0:T(8,128)S(1)}, u32[]{:S(2)}, u32[]{:S(2)}) collective-permute-start(f32[24,1280]{1,0:T(8,128)S(1)} %get-tuple-element.44), channel_id=1, source_target_pairs={{0,4},{1,5},{2,6},{3,7},{4,8},{5,9},{6,10},{7,11},{8,12},{9,13},{1... | collective-permute-start | bytes 368648 | tf_op jit(solution)/shard_map/ppermute | solution.py:18
  47.8 13.4 %collective-permute-start.13 = (f32[24,1280]{1,0:T(8,128)S(1)}, f32[24,1280]{1,0:T(8,128)S(1)}, u32[]{:S(2)}, u32[]{:S(2)}) collective-permute-start(f32[24,1280]{1,0:T(8,128)S(1)} %get-tuple-element.46), channel_id=1, source_target_pairs={{0,8},{1,9},{2,10},{3,11},{4,12},{5,13},{6,14},{7,15},{8,0},{9,1},... | collective-permute-start | bytes 368648 | tf_op jit(solution)/shard_map/ppermute | solution.py:18
  76.6 11.6 %collective-permute-start.18 = (bf16[4,24,2048]{2,1,0:T(8,128)(2,1)S(1)}, bf16[4,24,2048]{2,1,0:T(8,128)(2,1)S(1)}, u32[]{:S(2)}, u32[]{:S(2)}) collective-permute-start(bf16[4,24,2048]{2,1,0:T(8,128)(2,1)S(1)} %broadcast_select_fusion.2), channel_id=1, source_target_pairs={{0,1},{1,2},{2,3},{3,0},{4,5},{5,6},{6,7},{7,4},{8,9},{9,10},{10,1... | collective-permute-start | bytes 1179656 | tf_op jit(solution)/shard_map/ppermute | solution.py:18
  77.1 19.1 %collective-permute-start.19 = (bf16[4,24,2048]{2,1,0:T(8,128)(2,1)S(1)}, bf16[4,24,2048]{2,1,0:T(8,128)(2,1)S(1)}, u32[]{:S(2)}, u32[]{:S(2)}) collective-permute-start(bf16[4,24,2048]{2,1,0:T(8,128)(2,1)S(1)} %broadcast_select_fusion.2), channel_id=1, source_target_pairs={{0,2},{1,3},{2,0},{3,1},{4,6},{5,7},{6,4},{7,5},{8,10},{9,11},{10,... | collective-permute-start | bytes 1179656 | tf_op jit(solution)/shard_map/ppermute | solution.py:18
  80.6 15.6 %collective-permute-start.20 = (bf16[4,24,2048]{2,1,0:T(8,128)(2,1)S(1)}, bf16[4,24,2048]{2,1,0:T(8,128)(2,1)S(1)}, u32[]{:S(2)}, u32[]{:S(2)}) collective-permute-start(bf16[4,24,2048]{2,1,0:T(8,128)(2,1)S(1)} %broadcast_select_fusion.2), channel_id=1, source_target_pairs={{0,3},{1,0},{2,1},{3,2},{4,7},{5,4},{6,5},{7,6},{8,11},{9,8},{10,9... | collective-permute-start | bytes 1179656 | tf_op jit(solution)/shard_map/ppermute | solution.py:18
  114.8 12.1 %collective-permute-start.25 = (bf16[96,1024]{1,0:T(8,128)(2,1)S(1)}, bf16[96,1024]{1,0:T(8,128)(2,1)S(1)}, u32[]{:S(2)}, u32[]{:S(2)}) collective-permute-start(bf16[96,1024]{1,0:T(8,128)(2,1)S(1)} %fusion.49), channel_id=1, source_target_pairs={{0,32},{16,48},{32,0},{48,16},{1,33},{17,49},{33,1},{49,17},{2,34}... | collective-permute-start | bytes 589832 | tf_op jit(solution)/shard_map/ppermute | solution.py:18
  147.2 15.4 %collective-permute-start.35 = (bf16[4,24,1280]{2,1,0:T(8,128)(2,1)S(1)}, bf16[4,24,1280]{2,1,0:T(8,128)(2,1)S(1)}, u32[]{:S(2)}, u32[]{:S(2)}) collective-permute-start(bf16[4,24,1280]{2,1,0:T(8,128)(2,1)S(1)} %get-tuple-element.25), channel_id=1, source_target_pairs={{0,2},{1,3},{2,0},{3,1},{4,6},{5,7},{6,4},{7,5},{8,10},{9,11},{10,... | collective-permute-start | bytes 737288 | tf_op jit(solution)/shard_map/ppermute | solution.py:18
  151.3 11.3 %collective-permute-start.36 = (bf16[4,24,1280]{2,1,0:T(8,128)(2,1)S(1)}, bf16[4,24,1280]{2,1,0:T(8,128)(2,1)S(1)}, u32[]{:S(2)}, u32[]{:S(2)}) collective-permute-start(bf16[4,24,1280]{2,1,0:T(8,128)(2,1)S(1)} %get-tuple-element.24), channel_id=1, source_target_pairs={{0,3},{1,0},{2,1},{3,2},{4,7},{5,4},{6,5},{7,6},{8,11},{9,8},{10,9... | collective-permute-start | bytes 737288 | tf_op jit(solution)/shard_map/ppermute | solution.py:18
  151.4 15.5 %collective-permute-start.28 = (bf16[4,24,1282]{2,1,0:T(8,128)(2,1)S(1)}, bf16[4,24,1282]{2,1,0:T(8,128)(2,1)S(1)}, u32[]{:S(2)}, u32[]{:S(2)}) collective-permute-start(bf16[4,24,1282]{2,1,0:T(8,128)(2,1)S(1)} %get-tuple-element.17), channel_id=1, source_target_pairs={{0,4},{1,5},{2,6},{3,7},{4,8},{5,9},{6,10},{7,11},{8,12},{9,13},{1... | collective-permute-start | bytes 738440 | tf_op jit(solution)/shard_map/ppermute | solution.py:18
  151.5 15.8 %collective-permute-start.29 = (bf16[4,24,1282]{2,1,0:T(8,128)(2,1)S(1)}, bf16[4,24,1282]{2,1,0:T(8,128)(2,1)S(1)}, u32[]{:S(2)}, u32[]{:S(2)}) collective-permute-start(bf16[4,24,1282]{2,1,0:T(8,128)(2,1)S(1)} %get-tuple-element.19), channel_id=1, source_target_pairs={{0,8},{1,9},{2,10},{3,11},{4,12},{5,13},{6,14},{7,15},{8,0},{9,1},... | collective-permute-start | bytes 738440 | tf_op jit(solution)/shard_map/ppermute | solution.py:18
  156.1 11.2 %collective-permute-start.30 = (bf16[4,24,1282]{2,1,0:T(8,128)(2,1)S(1)}, bf16[4,24,1282]{2,1,0:T(8,128)(2,1)S(1)}, u32[]{:S(2)}, u32[]{:S(2)}) collective-permute-start(bf16[4,24,1282]{2,1,0:T(8,128)(2,1)S(1)} %get-tuple-element.18), channel_id=1, source_target_pairs={{0,12},{1,13},{2,14},{3,15},{4,0},{5,1},{6,2},{7,3},{8,4},{9,5},{1... | collective-permute-start | bytes 738440 | tf_op jit(solution)/shard_map/ppermute | solution.py:18
  191.2 12.3 %collective-permute-start.43 = (bf16[4,24,2048]{2,1,0:T(8,128)(2,1)S(1)}, bf16[4,24,2048]{2,1,0:T(8,128)(2,1)S(1)}, u32[]{:S(2)}, u32[]{:S(2)}) collective-permute-start(bf16[4,24,2048]{2,1,0:T(8,128)(2,1)S(1)} %broadcast_select_fusion.1), channel_id=1, source_target_pairs={{0,1},{1,2},{2,3},{3,0},{4,5},{5,6},{6,7},{7,4},{8,9},{9,10},{10,1... | collective-permute-start | bytes 1179656 | tf_op jit(solution)/shard_map/ppermute | solution.py:18
  193.4 18.2 %collective-permute-start.44 = (bf16[4,24,2048]{2,1,0:T(8,128)(2,1)S(1)}, bf16[4,24,2048]{2,1,0:T(8,128)(2,1)S(1)}, u32[]{:S(2)}, u32[]{:S(2)}) collective-permute-start(bf16[4,24,2048]{2,1,0:T(8,128)(2,1)S(1)} %broadcast_select_fusion.1), channel_id=1, source_target_pairs={{0,2},{1,3},{2,0},{3,1},{4,6},{5,7},{6,4},{7,5},{8,10},{9,11},{10,... | collective-permute-start | bytes 1179656 | tf_op jit(solution)/shard_map/ppermute | solution.py:18
  195.9 15.7 %collective-permute-start.45 = (bf16[4,24,2048]{2,1,0:T(8,128)(2,1)S(1)}, bf16[4,24,2048]{2,1,0:T(8,128)(2,1)S(1)}, u32[]{:S(2)}, u32[]{:S(2)}) collective-permute-start(bf16[4,24,2048]{2,1,0:T(8,128)(2,1)S(1)} %broadcast_select_fusion.1), channel_id=1, source_target_pairs={{0,3},{1,0},{2,1},{3,2},{4,7},{5,4},{6,5},{7,6},{8,11},{9,8},{10,9... | collective-permute-start | bytes 1179656 | tf_op jit(solution)/shard_map/ppermute | solution.py:18
  220.8 11.6 %collective-permute-start.47 = (bf16[3,32,1024]{2,1,0:T(8,128)(2,1)S(1)}, bf16[3,32,1024]{2,1,0:T(8,128)(2,1)S(1)}, u32[]{:S(2)}, u32[]{:S(2)}) collective-permute-start(bf16[3,32,1024]{2,1,0:T(8,128)(2,1)S(1)} %get-tuple-element.31), channel_id=1, source_target_pairs={{0,32},{16,48},{32,0},{48,16},{1,33},{17,49},{33,1},{49,17},{2,34}... | collective-permute-start | bytes 589832 | tf_op jit(solution)/shard_map/ppermute | solution.py:18
  (61 other events, 626.5 us)
where the time goes:
time: 235 us; the launch traced here: 233 us
  starting transfers between devices  79.9 us (34%)
  waiting for transfers between devices  78.5 us (33%)
  local copies, waits for them, and re-layouts  38.8 us (17%)
  other arithmetic  18 us (8%)
  matrix products  16.4 us (7%)
    ppermute x48, starting transfers between devices, shifted(): return lax.ppermute(x, axis, [(i, fn(i, n)) for i in range(n)])  78.5 us
    ppermute x48, waiting for transfers between devices, shifted(): return lax.ppermute(x, axis, [(i, fn(i, n)) for i in range(n)])  78.5 us
    dot_general x2, matrix products, layer(): first = jnp.dot(xg, w_query[0], preferred_element_type=f32)  8.33 us
    concatenate x2, local copies, waits for them, and re-layouts, layer(): jnp.concatenate([first.astype(bf16), second.astype(bf16), sq_hi, sq_lo],...  7.89 us
    gather x6, local copies, waits for them, and re-layouts, gather_from(): return jnp.take(jnp.stack(out), order, axis=0)  6.28 us
    unnamed x75, local copies, waits for them, and re-layouts  4.74 us
  transfers between devices with their start and end apart: 49, of which 27 were waited for; matrix products, arithmetic and copies ran while one was open for 11% of the time, Pallas kernels for 0%

commit v1 on v0

--- a/solution.py
+++ b/solution.py
@@ -117,17 +117,16 @@
         sq_hi = sq.astype(bf16)
         sq_lo = (sq - sq_hi.astype(f32)).astype(bf16)
         xg = (xf * gain[None, :]).astype(bf16)
-        first = jnp.dot(xg, w_query[0], preferred_element_type=f32)
+        cut = (query_cols // 2 + kv_cols // 2) // 128 * 128
+        first_half = jnp.dot(xg, w_query[0, :, :cut], preferred_element_type=f32).astype(bf16)
+        rest = jnp.dot(xg, w_query[0, :, cut:], preferred_element_type=f32)
         second = jnp.dot(xg, key_value_weight[0], preferred_element_type=f32)
-        proj = jnp.concatenate([first.astype(bf16), second.astype(bf16), sq_hi, sq_lo], axis=1)
-        cols = proj.shape[1]
-        blocks = proj.reshape(n_z, n_y, own_rows, cols)
-        cut = (cols // 2) // 128 * 128
-        first_y = blocks[..., :cut].transpose(1, 0, 2, 3)
-        first_z = blocks[..., cut:]
-        part_a = sum(r.astype(f32) for r in spread(first_y, y_pos, along_y))
+        rest = jnp.concatenate([rest.astype(bf16), second.astype(bf16), sq_hi, sq_lo], axis=1)
+        first_y = first_half.reshape(n_z, n_y, own_rows, cut).transpose(1, 0, 2, 3)
+        first_z = rest.reshape(n_z, n_y, own_rows, rest.shape[1])
+        part_a = sum(r.astype(f32) for r in spread(first_y, y_pos, along_y)).astype(bf16)
         part_b = sum(r.astype(f32) for r in spread(first_z, z_pos, along_z))
-        total_a = sum(spread(part_a, z_pos, along_z))
+        total_a = sum(r.astype(f32) for r in spread(part_a, z_pos, along_z))
         total_b = sum(spread(part_b, y_pos, along_y))
         total = jnp.concatenate([total_a, total_b], axis=1)
         total_sq = total[:, query_cols + kv_cols] + total[:, query_cols + kv_cols + 1]

time: 235 us -> 215 us (0.915)
  waiting for transfers between devices: 78.5 us -> 70.5 us
  local copies, waits for them, and re-layouts: 38.8 us -> 32 us
  starting transfers between devices: 79.9 us -> 73.2 us
    ppermute x48, waiting for transfers between devices: 78.5 us -> 70.1 us  [shifted(): return lax.ppermute(x, axis, [(i, fn(i, n)) for i in range(n)])]
    ppermute x48, starting transfers between devices: 78.5 us -> 71.8 us  [shifted(): return lax.ppermute(x, axis, [(i, fn(i, n)) for i in range(n)])]
    slice x4 -> x0, local copies, waits for them, and re-layouts: 3.85 us -> none  [the longest x2 2.72 us: layer(): first_z = blocks[..., cut:]]
    concatenate x2, local copies, waits for them, and re-layouts: 7.89 us -> 4.14 us  [layer(): jnp.concatenate([rest.astype(bf16), second.astype(bf16), sq_hi, sq_lo], a...]
    convert_element_type x0 -> x2, other arithmetic: none -> 2.87 us  [layer(): sum((r.astype(f32) for r in spread(first_y, y_pos, along_y))).astype(bf16)]
    unnamed x75 -> x67, local copies, waits for them, and re-layouts: 4.74 us -> 2.61 us
    dot_general x2 -> x4, matrix products: 8.33 us -> 8.74 us  [the longest x2 4.57 us: layer(): rest = jnp.dot(xg, w_query[0, :, cut:], preferred_element_type=f32)]
  transfers between devices with their start and end apart: 49 -> 49, of which waited for: 27 -> 28; matrix products, arithmetic and copies ran while one was open for 11% -> 13% of each run, Pallas kernels for 0% -> 0%
where the time goes in v1:
time: 215 us; the launch traced here: 214 us
  starting transfers between devices  73.2 us (34%)
  waiting for transfers between devices  70.5 us (33%)
  local copies, waits for them, and re-layouts  32 us (15%)
  other arithmetic  19.9 us (9%)
  matrix products  16.9 us (8%)
    ppermute x48, starting transfers between devices, shifted(): return lax.ppermute(x, axis, [(i, fn(i, n)) for i in range(n)])  71.8 us
    ppermute x48, waiting for transfers between devices, shifted(): return lax.ppermute(x, axis, [(i, fn(i, n)) for i in range(n)])  70.1 us
    gather x6, local copies, waits for them, and re-layouts, gather_from(): return jnp.take(jnp.stack(out), order, axis=0)  6.24 us
    dot_general x2, matrix products, layer(): rest = jnp.dot(xg, w_query[0, :, cut:], preferred_element_type=f32)  4.57 us
  transfers between devices with their start and end apart: 49, of which 28 were waited for; matrix products, arithmetic and copies ran while one was open for 13% of the time, Pallas kernels for 0%

profile of v1, /device:TPU:0, one launch (start us, length us, event | category | flops | bytes accessed | tf_op | source)
XLA Modules:
  0.0 214.0 jit_solution(11037115809610403153)
XLA Ops:
  19.9 2.4 %fusion.20 = bf16[384,768]{1,0:T(8,128)(2,1)S(1)} fusion(bf16[1,1024,2048]{2,1,0:T(8,128)(2,1)} %param.16, f32[1024]{0:T(1024)S(1)} %bitcast.318, bf16[384,1024]{1,0:T(8,128)(2,1)S(1)} %gather_fusion.6, pred[384]{0:T(512)(128)(4,1)S(1)} %get-tuple-element.60), kind=kOutput, calls=%fused_computation.38 | convolution fusion | flops 605847552 | bytes 2953600 | tf_op jit(solution)/shard_map/dot_general | solution.py:122
  48.6 3.5 %collective-permute-start.13 = (bf16[24,1280]{1,0:T(8,128)(2,1)S(1)}, bf16[24,1280]{1,0:T(8,128)(2,1)S(1)}, u32[]{:S(2)}, u32[]{:S(2)}) collective-permute-start(bf16[24,1280]{1,0:T(8,128)(2,1)S(1)} %get-tuple-element.46), channel_id=1, source_target_pairs={{0,8},{1,9},{2,10},{3,11},{4,12},{5,13},{6,14},{7,15},{8,0},{9,1},... | collective-permute-start | bytes 184328 | tf_op jit(solution)/shard_map/ppermute | solution.py:18
  53.6 2.6 %collective-permute-start.8 = (f32[24,1282]{1,0:T(8,128)S(1)}, f32[24,1282]{1,0:T(8,128)S(1)}, u32[]{:S(2)}, u32[]{:S(2)}) collective-permute-start(f32[24,1282]{1,0:T(8,128)S(1)} %get-tuple-element.39), channel_id=1, source_target_pairs={{0,3},{1,0},{2,1},{3,2},{4,7},{5,4},{6,5},{7,6},{8,11},{9,8},{10,9... | collective-permute-start | bytes 369224 | tf_op jit(solution)/shard_map/ppermute | solution.py:18
  56.6 2.5 %collective-permute-done.6 = f32[24,1282]{1,0:T(8,128)S(1)} collective-permute-done((f32[24,1282]{1,0:T(8,128)S(1)}, f32[24,1282]{1,0:T(8,128)S(1)}, u32[]{:S(2)}, u32[]{:S(2)}) %collective-permute-start.6) | collective-permute-done | bytes 123104 | tf_op jit(solution)/shard_map/ppermute | solution.py:18
  60.1 2.5 %collective-permute-done.7 = f32[24,1282]{1,0:T(8,128)S(1)} collective-permute-done((f32[24,1282]{1,0:T(8,128)S(1)}, f32[24,1282]{1,0:T(8,128)S(1)}, u32[]{:S(2)}, u32[]{:S(2)}) %collective-permute-start.7) | collective-permute-done | bytes 123104 | tf_op jit(solution)/shard_map/ppermute | solution.py:18
  69.1 3.1 %collective-permute-done.16 = bf16[24,2048]{1,0:T(8,128)(2,1)S(1)} collective-permute-done((bf16[24,2048]{1,0:T(8,128)(2,1)S(1)}, bf16[24,2048]{1,0:T(8,128)(2,1)S(1)}, u32[]{:S(2)}, u32[]{:S(2)}) %collective-permute-start.16) | collective-permute-done | bytes 98336 | tf_op jit(solution)/shard_map/ppermute | solution.py:18
  78.4 5.6 %collective-permute-done.19 = bf16[4,24,2048]{2,1,0:T(8,128)(2,1)S(1)} collective-permute-done((bf16[4,24,2048]{2,1,0:T(8,128)(2,1)S(1)}, bf16[4,24,2048]{2,1,0:T(8,128)(2,1)S(1)}, u32[]{:S(2)}, u32[]{:S(2)}) %collective-permute-start.19) | collective-permute-done | bytes 393248 | tf_op jit(solution)/shard_map/ppermute | solution.py:18
  84.0 4.0 %collective-permute-done.18 = bf16[4,24,2048]{2,1,0:T(8,128)(2,1)S(1)} collective-permute-done((bf16[4,24,2048]{2,1,0:T(8,128)(2,1)S(1)}, bf16[4,24,2048]{2,1,0:T(8,128)(2,1)S(1)}, u32[]{:S(2)}, u32[]{:S(2)}) %collective-permute-start.18) | collective-permute-done | bytes 393248 | tf_op jit(solution)/shard_map/ppermute | solution.py:18
  95.5 2.5 %collective-permute-start.23 = (bf16[96,1024]{1,0:T(8,128)(2,1)S(1)}, bf16[96,1024]{1,0:T(8,128)(2,1)S(1)}, u32[]{:S(2)}, u32[]{:S(2)}) collective-permute-start(bf16[96,1024]{1,0:T(8,128)(2,1)S(1)} %get-tuple-element.33), channel_id=1, source_target_pairs={{0,48},{16,0},{32,16},{48,32},{1,49},{17,1},{33,17},{49,33},{2,50}... | collective-permute-start | bytes 589832 | tf_op jit(solution)/shard_map/ppermute | solution.py:18
  98.6 7.4 %collective-permute-done.21 = bf16[96,1024]{1,0:T(8,128)(2,1)S(1)} collective-permute-done((bf16[96,1024]{1,0:T(8,128)(2,1)S(1)}, bf16[96,1024]{1,0:T(8,128)(2,1)S(1)}, u32[]{:S(2)}, u32[]{:S(2)}) %collective-permute-start.21) | collective-permute-done | bytes 196640 | tf_op jit(solution)/shard_map/ppermute | solution.py:18
  110.3 4.4 %collective-permute-done.26 = bf16[96,1024]{1,0:T(8,128)(2,1)S(1)} collective-permute-done((bf16[96,1024]{1,0:T(8,128)(2,1)S(1)}, bf16[96,1024]{1,0:T(8,128)(2,1)S(1)}, u32[]{:S(2)}, u32[]{:S(2)}) %collective-permute-start.26) | collective-permute-done | bytes 196640 | tf_op jit(solution)/shard_map/ppermute | solution.py:18
  124.5 2.9 %convolution_convert_fusion = bf16[384,1280]{1,0:T(8,128)(2,1)S(1)} fusion(bf16[1,1024,2048]{2,1,0:T(8,128)(2,1)} %param.16, bf16[384,1024]{1,0:T(8,128)(2,1)S(1)} %collective-permute-done.27, f32[1024]{0:T(1024)S(1)} %bitcast.321), kind=kOutput, calls=%fused_computation.16 | convolution fusion | flops 1008304128 | bytes 4395008 | tf_op jit(solution)/shard_map/dot_general | solution.py:121
  128.8 2.8 %collective-permute-start.36 = (bf16[4,24,1280]{2,1,0:T(8,128)(2,1)}, bf16[4,24,1280]{2,1,0:T(8,128)(2,1)}, u32[]{:S(2)}, u32[]{:S(2)}) collective-permute-start(bf16[4,24,1280]{2,1,0:T(8,128)(2,1)} %get-tuple-element.24), channel_id=1, source_target_pairs={{0,3},{1,0},{2,1},{3,2},{4,7},{5,4},{6,5},{7,6},{8,11},{9,8},{10,9... | collective-permute-start | bytes 737288 | tf_op jit(solution)/shard_map/ppermute | solution.py:18
  137.4 3.2 %collective-permute-start.30 = (bf16[4,24,1282]{2,1,0:T(8,128)(2,1)S(1)}, bf16[4,24,1282]{2,1,0:T(8,128)(2,1)S(1)}, u32[]{:S(2)}, u32[]{:S(2)}) collective-permute-start(bf16[4,24,1282]{2,1,0:T(8,128)(2,1)S(1)} %get-tuple-element.18), channel_id=1, source_target_pairs={{0,12},{1,13},{2,14},{3,15},{4,0},{5,1},{6,2},{7,3},{8,4},{9,5},{1... | collective-permute-start | bytes 738440 | tf_op jit(solution)/shard_map/ppermute | solution.py:18
  140.6 2.8 %collective-permute-done.34 = bf16[4,24,1280]{2,1,0:T(8,128)(2,1)} collective-permute-done((bf16[4,24,1280]{2,1,0:T(8,128)(2,1)}, bf16[4,24,1280]{2,1,0:T(8,128)(2,1)}, u32[]{:S(2)}, u32[]{:S(2)}) %collective-permute-start.34) | collective-permute-done | bytes 245792 | tf_op jit(solution)/shard_map/ppermute | solution.py:18
  146.2 3.2 %collective-permute-start.39 = (bf16[24,1280]{1,0:T(8,128)(2,1)S(1)}, bf16[24,1280]{1,0:T(8,128)(2,1)S(1)}, u32[]{:S(2)}, u32[]{:S(2)}) collective-permute-start(bf16[24,1280]{1,0:T(8,128)(2,1)S(1)} %get-tuple-element.42), channel_id=1, source_target_pairs={{0,12},{1,13},{2,14},{3,15},{4,0},{5,1},{6,2},{7,3},{8,4},{9,5},{1... | collective-permute-start | bytes 184328 | tf_op jit(solution)/shard_map/ppermute | solution.py:18
  150.7 3.1 %collective-permute-done.30 = bf16[4,24,1282]{2,1,0:T(8,128)(2,1)S(1)} collective-permute-done((bf16[4,24,1282]{2,1,0:T(8,128)(2,1)S(1)}, bf16[4,24,1282]{2,1,0:T(8,128)(2,1)S(1)}, u32[]{:S(2)}, u32[]{:S(2)}) %collective-permute-start.30) | collective-permute-done | bytes 246176 | tf_op jit(solution)/shard_map/ppermute | solution.py:18
  155.0 2.6 %collective-permute-start.33 = (f32[24,1282]{1,0:T(8,128)S(1)}, f32[24,1282]{1,0:T(8,128)S(1)}, u32[]{:S(2)}, u32[]{:S(2)}) collective-permute-start(f32[24,1282]{1,0:T(8,128)S(1)} %get-tuple-element.36), channel_id=1, source_target_pairs={{0,3},{1,0},{2,1},{3,2},{4,7},{5,4},{6,5},{7,6},{8,11},{9,8},{10,9... | collective-permute-start | bytes 369224 | tf_op jit(solution)/shard_map/ppermute | solution.py:18
  166.6 3.4 %collective-permute-start.42 = (bf16[24,2048]{1,0:T(8,128)(2,1)}, bf16[24,2048]{1,0:T(8,128)(2,1)}, u32[]{:S(2)}, u32[]{:S(2)}) collective-permute-start(bf16[24,2048]{1,0:T(8,128)(2,1)} %reshape.649), channel_id=1, source_target_pairs={{0,12},{1,13},{2,14},{3,15},{4,0},{5,1},{6,2},{7,3},{8,4},{9,5},{1... | collective-permute-start | bytes 294920 | tf_op jit(solution)/shard_map/ppermute | solution.py:18
  181.1 2.9 %collective-permute-start.45 = (bf16[4,24,2048]{2,1,0:T(8,128)(2,1)S(1)}, bf16[4,24,2048]{2,1,0:T(8,128)(2,1)S(1)}, u32[]{:S(2)}, u32[]{:S(2)}) collective-permute-start(bf16[4,24,2048]{2,1,0:T(8,128)(2,1)S(1)} %broadcast_select_fusion.1), channel_id=1, source_target_pairs={{0,3},{1,0},{2,1},{3,2},{4,7},{5,4},{6,5},{7,6},{8,11},{9,8},{10,9... | collective-permute-start | bytes 1179656 | tf_op jit(solution)/shard_map/ppermute | solution.py:18
  184.1 5.5 %collective-permute-done.44 = bf16[4,24,2048]{2,1,0:T(8,128)(2,1)S(1)} collective-permute-done((bf16[4,24,2048]{2,1,0:T(8,128)(2,1)S(1)}, bf16[4,24,2048]{2,1,0:T(8,128)(2,1)S(1)}, u32[]{:S(2)}, u32[]{:S(2)}) %collective-permute-start.44) | collective-permute-done | bytes 393248 | tf_op jit(solution)/shard_map/ppermute | solution.py:18
  189.6 4.1 %collective-permute-done.43 = bf16[4,24,2048]{2,1,0:T(8,128)(2,1)S(1)} collective-permute-done((bf16[4,24,2048]{2,1,0:T(8,128)(2,1)S(1)}, bf16[4,24,2048]{2,1,0:T(8,128)(2,1)S(1)}, u32[]{:S(2)}, u32[]{:S(2)}) %collective-permute-start.43) | collective-permute-done | bytes 393248 | tf_op jit(solution)/shard_map/ppermute | solution.py:18
  202.7 3.2 %collective-permute-start.48 = (bf16[3,32,1024]{2,1,0:T(8,128)(2,1)S(1)}, bf16[3,32,1024]{2,1,0:T(8,128)(2,1)S(1)}, u32[]{:S(2)}, u32[]{:S(2)}) collective-permute-start(bf16[3,32,1024]{2,1,0:T(8,128)(2,1)S(1)} %get-tuple-element.30), channel_id=1, source_target_pairs={{0,48},{16,0},{32,16},{48,32},{1,49},{17,1},{33,17},{49,33},{2,50}... | collective-permute-start | bytes 589832 | tf_op jit(solution)/shard_map/ppermute | solution.py:18
  206.7 3.8 %collective-permute-done.46 = bf16[3,32,1024]{2,1,0:T(8,128)(2,1)S(1)} collective-permute-done((bf16[3,32,1024]{2,1,0:T(8,128)(2,1)S(1)}, bf16[3,32,1024]{2,1,0:T(8,128)(2,1)S(1)}, u32[]{:S(2)}, u32[]{:S(2)}) %collective-permute-start.46) | collective-permute-done | bytes 196640 | tf_op jit(solution)/shard_map/ppermute | solution.py:18
  (292 shorter events, 128.5 us)
Async XLA Ops:
  0.7 15.9 %collective-permute-start = (bf16[3,32,1024]{2,1,0:T(8,128)(2,1)}, bf16[3,32,1024]{2,1,0:T(8,128)(2,1)S(1)}, u32[]{:S(2)}, u32[]{:S(2)}) collective-permute-start(bf16[3,32,1024]{2,1,0:T(8,128)(2,1)} %param.14), channel_id=1, source_target_pairs={{0,16},{16,32},{32,48},{48,0},{1,17},{17,33},{33,49},{49,1},{2,18}... | collective-permute-start | bytes 589832 | tf_op jit(solution)/shard_map/ppermute | solution.py:18
  2.3 14.2 %collective-permute-start.2 = (bf16[3,32,1024]{2,1,0:T(8,128)(2,1)}, bf16[3,32,1024]{2,1,0:T(8,128)(2,1)S(1)}, u32[]{:S(2)}, u32[]{:S(2)}) collective-permute-start(bf16[3,32,1024]{2,1,0:T(8,128)(2,1)} %param.14), channel_id=1, source_target_pairs={{0,48},{16,0},{32,16},{48,32},{1,49},{17,1},{33,17},{49,33},{2,50}... | collective-permute-start | bytes 589832 | tf_op jit(solution)/shard_map/ppermute | solution.py:18
  4.0 12.6 %collective-permute-start.1 = (bf16[3,32,1024]{2,1,0:T(8,128)(2,1)}, bf16[3,32,1024]{2,1,0:T(8,128)(2,1)S(1)}, u32[]{:S(2)}, u32[]{:S(2)}) collective-permute-start(bf16[3,32,1024]{2,1,0:T(8,128)(2,1)} %param.14), channel_id=1, source_target_pairs={{0,32},{16,48},{32,0},{48,16},{1,33},{17,49},{33,1},{49,17},{2,34}... | collective-permute-start | bytes 589832 | tf_op jit(solution)/shard_map/ppermute | solution.py:18
  28.1 11.6 %collective-permute-start.9 = (bf16[4,24,1280]{2,1,0:T(8,128)(2,1)}, bf16[4,24,1280]{2,1,0:T(8,128)(2,1)}, u32[]{:S(2)}, u32[]{:S(2)}) collective-permute-start(bf16[4,24,1280]{2,1,0:T(8,128)(2,1)} %get-tuple-element.26), channel_id=1, source_target_pairs={{0,1},{1,2},{2,3},{3,0},{4,5},{5,6},{6,7},{7,4},{8,9},{9,10},{10,1... | collective-permute-start | bytes 737288 | tf_op jit(solution)/shard_map/ppermute | solution.py:18
  29.6 11.8 %collective-permute-start.11 = (bf16[4,24,1280]{2,1,0:T(8,128)(2,1)}, bf16[4,24,1280]{2,1,0:T(8,128)(2,1)}, u32[]{:S(2)}, u32[]{:S(2)}) collective-permute-start(bf16[4,24,1280]{2,1,0:T(8,128)(2,1)} %get-tuple-element.27), channel_id=1, source_target_pairs={{0,3},{1,0},{2,1},{3,2},{4,7},{5,4},{6,5},{7,6},{8,11},{9,8},{10,9... | collective-permute-start | bytes 737288 | tf_op jit(solution)/shard_map/ppermute | solution.py:18
  31.3 11.7 %collective-permute-start.10 = (bf16[4,24,1280]{2,1,0:T(8,128)(2,1)}, bf16[4,24,1280]{2,1,0:T(8,128)(2,1)}, u32[]{:S(2)}, u32[]{:S(2)}) collective-permute-start(bf16[4,24,1280]{2,1,0:T(8,128)(2,1)} %get-tuple-element.28), channel_id=1, source_target_pairs={{0,2},{1,3},{2,0},{3,1},{4,6},{5,7},{6,4},{7,5},{8,10},{9,11},{10,... | collective-permute-start | bytes 737288 | tf_op jit(solution)/shard_map/ppermute | solution.py:18
  35.4 13.2 %collective-permute-start.3 = (bf16[4,24,1282]{2,1,0:T(8,128)(2,1)S(1)}, bf16[4,24,1282]{2,1,0:T(8,128)(2,1)S(1)}, u32[]{:S(2)}, u32[]{:S(2)}) collective-permute-start(bf16[4,24,1282]{2,1,0:T(8,128)(2,1)S(1)} %get-tuple-element.20), channel_id=1, source_target_pairs={{0,4},{1,5},{2,6},{3,7},{4,8},{5,9},{6,10},{7,11},{8,12},{9,13},{1... | collective-permute-start | bytes 738440 | tf_op jit(solution)/shard_map/ppermute | solution.py:18
  37.4 14.6 %collective-permute-start.5 = (bf16[4,24,1282]{2,1,0:T(8,128)(2,1)S(1)}, bf16[4,24,1282]{2,1,0:T(8,128)(2,1)S(1)}, u32[]{:S(2)}, u32[]{:S(2)}) collective-permute-start(bf16[4,24,1282]{2,1,0:T(8,128)(2,1)S(1)} %get-tuple-element.21), channel_id=1, source_target_pairs={{0,12},{1,13},{2,14},{3,15},{4,0},{5,1},{6,2},{7,3},{8,4},{9,5},{1... | collective-permute-start | bytes 738440 | tf_op jit(solution)/shard_map/ppermute | solution.py:18
  39.6 13.0 %collective-permute-start.4 = (bf16[4,24,1282]{2,1,0:T(8,128)(2,1)S(1)}, bf16[4,24,1282]{2,1,0:T(8,128)(2,1)S(1)}, u32[]{:S(2)}, u32[]{:S(2)}) collective-permute-start(bf16[4,24,1282]{2,1,0:T(8,128)(2,1)S(1)} %get-tuple-element.22), channel_id=1, source_target_pairs={{0,8},{1,9},{2,10},{3,11},{4,12},{5,13},{6,14},{7,15},{8,0},{9,1},... | collective-permute-start | bytes 738440 | tf_op jit(solution)/shard_map/ppermute | solution.py:18
  44.4 11.7 %collective-permute-start.12 = (bf16[24,1280]{1,0:T(8,128)(2,1)S(1)}, bf16[24,1280]{1,0:T(8,128)(2,1)S(1)}, u32[]{:S(2)}, u32[]{:S(2)}) collective-permute-start(bf16[24,1280]{1,0:T(8,128)(2,1)S(1)} %get-tuple-element.44), channel_id=1, source_target_pairs={{0,4},{1,5},{2,6},{3,7},{4,8},{5,9},{6,10},{7,11},{8,12},{9,13},{1... | collective-permute-start | bytes 184328 | tf_op jit(solution)/shard_map/ppermute | solution.py:18
  75.0 13.0 %collective-permute-start.18 = (bf16[4,24,2048]{2,1,0:T(8,128)(2,1)S(1)}, bf16[4,24,2048]{2,1,0:T(8,128)(2,1)S(1)}, u32[]{:S(2)}, u32[]{:S(2)}) collective-permute-start(bf16[4,24,2048]{2,1,0:T(8,128)(2,1)S(1)} %broadcast_select_fusion.2), channel_id=1, source_target_pairs={{0,1},{1,2},{2,3},{3,0},{4,5},{5,6},{6,7},{7,4},{8,9},{9,10},{10,1... | collective-permute-start | bytes 1179656 | tf_op jit(solution)/shard_map/ppermute | solution.py:18
  76.4 11.7 %collective-permute-start.20 = (bf16[4,24,2048]{2,1,0:T(8,128)(2,1)S(1)}, bf16[4,24,2048]{2,1,0:T(8,128)(2,1)S(1)}, u32[]{:S(2)}, u32[]{:S(2)}) collective-permute-start(bf16[4,24,2048]{2,1,0:T(8,128)(2,1)S(1)} %broadcast_select_fusion.2), channel_id=1, source_target_pairs={{0,3},{1,0},{2,1},{3,2},{4,7},{5,4},{6,5},{7,6},{8,11},{9,8},{10,9... | collective-permute-start | bytes 1179656 | tf_op jit(solution)/shard_map/ppermute | solution.py:18
  94.6 11.4 %collective-permute-start.21 = (bf16[96,1024]{1,0:T(8,128)(2,1)S(1)}, bf16[96,1024]{1,0:T(8,128)(2,1)S(1)}, u32[]{:S(2)}, u32[]{:S(2)}) collective-permute-start(bf16[96,1024]{1,0:T(8,128)(2,1)S(1)} %get-tuple-element.32), channel_id=1, source_target_pairs={{0,16},{16,32},{32,48},{48,0},{1,17},{17,33},{33,49},{49,1},{2,18}... | collective-permute-start | bytes 589832 | tf_op jit(solution)/shard_map/ppermute | solution.py:18
  128.4 15.0 %collective-permute-start.34 = (bf16[4,24,1280]{2,1,0:T(8,128)(2,1)}, bf16[4,24,1280]{2,1,0:T(8,128)(2,1)}, u32[]{:S(2)}, u32[]{:S(2)}) collective-permute-start(bf16[4,24,1280]{2,1,0:T(8,128)(2,1)} %get-tuple-element.23), channel_id=1, source_target_pairs={{0,1},{1,2},{2,3},{3,0},{4,5},{5,6},{6,7},{7,4},{8,9},{9,10},{10,1... | collective-permute-start | bytes 737288 | tf_op jit(solution)/shard_map/ppermute | solution.py:18
  128.8 15.6 %collective-permute-start.36 = (bf16[4,24,1280]{2,1,0:T(8,128)(2,1)}, bf16[4,24,1280]{2,1,0:T(8,128)(2,1)}, u32[]{:S(2)}, u32[]{:S(2)}) collective-permute-start(bf16[4,24,1280]{2,1,0:T(8,128)(2,1)} %get-tuple-element.24), channel_id=1, source_target_pairs={{0,3},{1,0},{2,1},{3,2},{4,7},{5,4},{6,5},{7,6},{8,11},{9,8},{10,9... | collective-permute-start | bytes 737288 | tf_op jit(solution)/shard_map/ppermute | solution.py:18
  131.6 12.8 %collective-permute-start.35 = (bf16[4,24,1280]{2,1,0:T(8,128)(2,1)}, bf16[4,24,1280]{2,1,0:T(8,128)(2,1)}, u32[]{:S(2)}, u32[]{:S(2)}) collective-permute-start(bf16[4,24,1280]{2,1,0:T(8,128)(2,1)} %get-tuple-element.25), channel_id=1, source_target_pairs={{0,2},{1,3},{2,0},{3,1},{4,6},{5,7},{6,4},{7,5},{8,10},{9,11},{10,... | collective-permute-start | bytes 737288 | tf_op jit(solution)/shard_map/ppermute | solution.py:18
  137.3 12.1 %collective-permute-start.28 = (bf16[4,24,1282]{2,1,0:T(8,128)(2,1)S(1)}, bf16[4,24,1282]{2,1,0:T(8,128)(2,1)S(1)}, u32[]{:S(2)}, u32[]{:S(2)}) collective-permute-start(bf16[4,24,1282]{2,1,0:T(8,128)(2,1)S(1)} %get-tuple-element.17), channel_id=1, source_target_pairs={{0,4},{1,5},{2,6},{3,7},{4,8},{5,9},{6,10},{7,11},{8,12},{9,13},{1... | collective-permute-start | bytes 738440 | tf_op jit(solution)/shard_map/ppermute | solution.py:18
  137.4 16.5 %collective-permute-start.30 = (bf16[4,24,1282]{2,1,0:T(8,128)(2,1)S(1)}, bf16[4,24,1282]{2,1,0:T(8,128)(2,1)S(1)}, u32[]{:S(2)}, u32[]{:S(2)}) collective-permute-start(bf16[4,24,1282]{2,1,0:T(8,128)(2,1)S(1)} %get-tuple-element.18), channel_id=1, source_target_pairs={{0,12},{1,13},{2,14},{3,15},{4,0},{5,1},{6,2},{7,3},{8,4},{9,5},{1... | collective-permute-start | bytes 738440 | tf_op jit(solution)/shard_map/ppermute | solution.py:18
  143.4 10.8 %collective-permute-start.29 = (bf16[4,24,1282]{2,1,0:T(8,128)(2,1)S(1)}, bf16[4,24,1282]{2,1,0:T(8,128)(2,1)S(1)}, u32[]{:S(2)}, u32[]{:S(2)}) collective-permute-start(bf16[4,24,1282]{2,1,0:T(8,128)(2,1)S(1)} %get-tuple-element.19), channel_id=1, source_target_pairs={{0,8},{1,9},{2,10},{3,11},{4,12},{5,13},{6,14},{7,15},{8,0},{9,1},... | collective-permute-start | bytes 738440 | tf_op jit(solution)/shard_map/ppermute | solution.py:18
  145.9 11.8 %collective-permute-start.37 = (bf16[24,1280]{1,0:T(8,128)(2,1)S(1)}, bf16[24,1280]{1,0:T(8,128)(2,1)S(1)}, u32[]{:S(2)}, u32[]{:S(2)}) collective-permute-start(bf16[24,1280]{1,0:T(8,128)(2,1)S(1)} %get-tuple-element.41), channel_id=1, source_target_pairs={{0,4},{1,5},{2,6},{3,7},{4,8},{5,9},{6,10},{7,11},{8,12},{9,13},{1... | collective-permute-start | bytes 184328 | tf_op jit(solution)/shard_map/ppermute | solution.py:18
  146.2 13.3 %collective-permute-start.39 = (bf16[24,1280]{1,0:T(8,128)(2,1)S(1)}, bf16[24,1280]{1,0:T(8,128)(2,1)S(1)}, u32[]{:S(2)}, u32[]{:S(2)}) collective-permute-start(bf16[24,1280]{1,0:T(8,128)(2,1)S(1)} %get-tuple-element.42), channel_id=1, source_target_pairs={{0,12},{1,13},{2,14},{3,15},{4,0},{5,1},{6,2},{7,3},{8,4},{9,5},{1... | collective-permute-start | bytes 184328 | tf_op jit(solution)/shard_map/ppermute | solution.py:18
  179.0 10.6 %collective-permute-start.44 = (bf16[4,24,2048]{2,1,0:T(8,128)(2,1)S(1)}, bf16[4,24,2048]{2,1,0:T(8,128)(2,1)S(1)}, u32[]{:S(2)}, u32[]{:S(2)}) collective-permute-start(bf16[4,24,2048]{2,1,0:T(8,128)(2,1)S(1)} %broadcast_select_fusion.1), channel_id=1, source_target_pairs={{0,2},{1,3},{2,0},{3,1},{4,6},{5,7},{6,4},{7,5},{8,10},{9,11},{10,... | collective-permute-start | bytes 1179656 | tf_op jit(solution)/shard_map/ppermute | solution.py:18
  180.8 12.9 %collective-permute-start.43 = (bf16[4,24,2048]{2,1,0:T(8,128)(2,1)S(1)}, bf16[4,24,2048]{2,1,0:T(8,128)(2,1)S(1)}, u32[]{:S(2)}, u32[]{:S(2)}) collective-permute-start(bf16[4,24,2048]{2,1,0:T(8,128)(2,1)S(1)} %broadcast_select_fusion.1), channel_id=1, source_target_pairs={{0,1},{1,2},{2,3},{3,0},{4,5},{5,6},{6,7},{7,4},{8,9},{9,10},{10,1... | collective-permute-start | bytes 1179656 | tf_op jit(solution)/shard_map/ppermute | solution.py:18
  181.1 12.5 %collective-permute-start.45 = (bf16[4,24,2048]{2,1,0:T(8,128)(2,1)S(1)}, bf16[4,24,2048]{2,1,0:T(8,128)(2,1)S(1)}, u32[]{:S(2)}, u32[]{:S(2)}) collective-permute-start(bf16[4,24,2048]{2,1,0:T(8,128)(2,1)S(1)} %broadcast_select_fusion.1), channel_id=1, source_target_pairs={{0,3},{1,0},{2,1},{3,2},{4,7},{5,4},{6,5},{7,6},{8,11},{9,8},{10,9... | collective-permute-start | bytes 1179656 | tf_op jit(solution)/shard_map/ppermute | solution.py:18
  (57 other events, 600.9 us)

commit v2 on v1

--- a/solution.py
+++ b/solution.py
@@ -110,6 +110,12 @@
     back_index = (
         owner_slot[None, :, None] * block + rr[:, None, None] * DRAFT_BLOCK + jj[None, None, :]
     ).reshape(-1)
+
+    def arrived_at(s):
+        b = s // own_rows
+        shift_y = (y_pos - b % n_y) % n_y
+        shift_z = (z_pos - b // n_y) % n_z
+        return (shift_y * n_z + shift_z) * own_rows + s % own_rows
 
     def layer(x_sorted, last):
         xf = x_sorted.astype(f32)
@@ -153,19 +159,20 @@
             "shgrjl,shld->srjhgd", weights, values, preferred_element_type=f32
         )
         attended = attended.astype(bf16).reshape(own_rows, query_cols)
-        by_z = gather_from(attended, z_pos, n_z, along_z)
-        by_zy = gather_from(by_z, y_pos, n_y, along_y)
-        gathered = by_zy.transpose(1, 0, 2, 3).reshape(-1, query_cols)
-        partial = jnp.dot(gathered, w_out[0], preferred_element_type=f32)
+        by_z = jnp.stack([attended] + [along_z(attended, k) for k in range(1, n_z)])
+        by_zy = jnp.stack([by_z] + [along_y(by_z, k) for k in range(1, n_y)])
+        gathered = by_zy.reshape(-1, query_cols)
+        partial = jnp.dot(gathered, w_out[0], preferred_element_type=f32).astype(bf16)
         ext_new = jnp.where(keep[:, None, :, None], fresh, jnp.zeros_like(fresh))
         if last:
-            natural = jnp.take(partial.astype(bf16), back_index, axis=0)
+            natural = jnp.take(partial, arrived_at(back_index), axis=0)
             pieces = natural.reshape(rounds, n_tensor, rows_local, width_local).transpose(1, 0, 2, 3)
             mine = sum(r.astype(f32) for r in spread(pieces, tensor, along_tensor))
             x_own = jnp.take(xf, own_index, axis=0).reshape(rounds, rows_local, width_local)
             return None, (x_own + mine).astype(bf16), ext_new
         quarter = partial.shape[0] // n_tensor
-        pieces = partial.astype(bf16).reshape(n_tensor, quarter, width_local)
+        in_order = jnp.take(partial, arrived_at(jnp.arange(partial.shape[0])), axis=0)
+        pieces = in_order.reshape(n_tensor, quarter, width_local)
         mine = sum(r.astype(f32) for r in spread(pieces, tensor, along_tensor))
         x_mine = lax.dynamic_index_in_dim(
             xf.reshape(n_tensor, quarter, width_local), tensor, 0, keepdims=False

time: 215 us -> 210 us (0.977)
  local copies, waits for them, and re-layouts: 32 us -> 26 us
  matrix products: 16.9 us -> 21.3 us
  other arithmetic: 19.9 us -> 16.8 us
    gather x6 -> x2, local copies, waits for them, and re-layouts: 6.24 us -> 1.32 us  [gather_from(): return jnp.take(jnp.stack(out), order, axis=0)]
    dot_general x2, matrix products: 3.63 us -> 7.98 us  [layer(): jnp.dot(gathered, w_out[0], preferred_element_type=f32).astype(bf16)]
    transpose x2 -> x0, other arithmetic: 3.55 us -> none  [layer(): gathered = by_zy.transpose(1, 0, 2, 3).reshape(-1, query_cols)]
    another operation x0 -> x4, other arithmetic: none -> 3.4 us  [layer(): by_zy = jnp.stack([by_z] + [along_y(by_z, k) for k in range(1, n_y)])]
  transfers between devices with their start and end apart: 49 -> 49, of which waited for: 28 -> 31; matrix products, arithmetic and copies ran while one was open for 13% -> 12% of each run, Pallas kernels for 0% -> 0%
where the time goes in v2:
time: 210 us; the launch traced here: 209 us
  waiting for transfers between devices  72 us (34%)
  starting transfers between devices  71.8 us (34%)
  local copies, waits for them, and re-layouts  26 us (12%)
  matrix products  21.3 us (10%)
  other arithmetic  16.8 us (8%)
    ppermute x48, waiting for transfers between devices, shifted(): return lax.ppermute(x, axis, [(i, fn(i, n)) for i in range(n)])  71.6 us
    ppermute x48, starting transfers between devices, shifted(): return lax.ppermute(x, axis, [(i, fn(i, n)) for i in range(n)])  70.4 us
    dot_general x2, matrix products, layer(): jnp.dot(gathered, w_out[0], preferred_element_type=f32).astype(bf16)  7.98 us
    dot_general x2, matrix products, layer(): rest = jnp.dot(xg, w_query[0, :, cut:], preferred_element_type=f32)  4.58 us
  transfers between devices with their start and end apart: 49, of which 31 were waited for; matrix products, arithmetic and copies ran while one was open for 12% of the time, Pallas kernels for 0%

profile of v2, /device:TPU:0, one launch (start us, length us, event | category | flops | bytes accessed | tf_op | source)
XLA Modules:
  0.0 209.3 jit_solution(2395854119028659979)
XLA Ops:
  47.1 3.5 %collective-permute-start.13 = (bf16[24,1280]{1,0:T(8,128)(2,1)S(1)}, bf16[24,1280]{1,0:T(8,128)(2,1)S(1)}, u32[]{:S(2)}, u32[]{:S(2)}) collective-permute-start(bf16[24,1280]{1,0:T(8,128)(2,1)S(1)} %get-tuple-element.50), channel_id=1, source_target_pairs={{0,8},{1,9},{2,10},{3,11},{4,12},{5,13},{6,14},{7,15},{8,0},{9,1},... | collective-permute-start | bytes 184328 | tf_op jit(solution)/shard_map/ppermute | solution.py:18
  52.0 2.6 %collective-permute-start.8 = (f32[24,1282]{1,0:T(8,128)S(1)}, f32[24,1282]{1,0:T(8,128)S(1)}, u32[]{:S(2)}, u32[]{:S(2)}) collective-permute-start(f32[24,1282]{1,0:T(8,128)S(1)} %get-tuple-element.39), channel_id=1, source_target_pairs={{0,3},{1,0},{2,1},{3,2},{4,7},{5,4},{6,5},{7,6},{8,11},{9,8},{10,9... | collective-permute-start | bytes 369224 | tf_op jit(solution)/shard_map/ppermute | solution.py:18
  67.5 3.1 %collective-permute-done.16 = bf16[24,2048]{1,0:T(8,128)(2,1)S(1)} collective-permute-done((bf16[24,2048]{1,0:T(8,128)(2,1)S(1)}, bf16[24,2048]{1,0:T(8,128)(2,1)S(1)}, u32[]{:S(2)}, u32[]{:S(2)}) %collective-permute-start.16) | collective-permute-done | bytes 98336 | tf_op jit(solution)/shard_map/ppermute | solution.py:18
  78.4 4.0 %collective-permute-done.19 = bf16[4,24,2048]{2,1,0:T(8,128)(2,1)S(1)} collective-permute-done((bf16[4,24,2048]{2,1,0:T(8,128)(2,1)}, bf16[4,24,2048]{2,1,0:T(8,128)(2,1)S(1)}, u32[]{:S(2)}, u32[]{:S(2)}) %collective-permute-start.19) | collective-permute-done | bytes 393248 | tf_op jit(solution)/shard_map/ppermute | solution.py:18
  82.4 4.1 %collective-permute-done.18 = bf16[4,24,2048]{2,1,0:T(8,128)(2,1)S(1)} collective-permute-done((bf16[4,24,2048]{2,1,0:T(8,128)(2,1)}, bf16[4,24,2048]{2,1,0:T(8,128)(2,1)S(1)}, u32[]{:S(2)}, u32[]{:S(2)}) %collective-permute-start.18) | collective-permute-done | bytes 393248 | tf_op jit(solution)/shard_map/ppermute | solution.py:18
  86.7 4.0 %fusion.12 = bf16[384,1024]{1,0:T(8,128)(2,1)S(1)} fusion(bf16[384,2048]{1,0:T(8,128)(2,1)S(1)} %bitcast.274, bf16[1,2048,1024]{2,1,0:T(8,128)(2,1)} %param.14), kind=kOutput, calls=%fused_computation.29 | convolution fusion | flops 1611005952 | bytes 6553600 | tf_op jit(solution)/shard_map/dot_general | solution.py:165
  96.5 7.2 %collective-permute-done.21 = bf16[96,1024]{1,0:T(8,128)(2,1)S(1)} collective-permute-done((bf16[96,1024]{1,0:T(8,128)(2,1)S(1)}, bf16[96,1024]{1,0:T(8,128)(2,1)S(1)}, u32[]{:S(2)}, u32[]{:S(2)}) %collective-permute-start.21) | collective-permute-done | bytes 196640 | tf_op jit(solution)/shard_map/ppermute | solution.py:18
  109.0 4.2 %collective-permute-done.26 = bf16[96,1024]{1,0:T(8,128)(2,1)S(1)} collective-permute-done((bf16[96,1024]{1,0:T(8,128)(2,1)S(1)}, bf16[96,1024]{1,0:T(8,128)(2,1)S(1)}, u32[]{:S(2)}, u32[]{:S(2)}) %collective-permute-start.26) | collective-permute-done | bytes 196640 | tf_op jit(solution)/shard_map/ppermute | solution.py:18
  123.1 2.9 %convolution_convert_fusion = bf16[384,1280]{1,0:T(8,128)(2,1)S(1)} fusion(bf16[1,1024,2048]{2,1,0:T(8,128)(2,1)} %param.12, bf16[384,1024]{1,0:T(8,128)(2,1)S(1)} %collective-permute-done.27, f32[1024]{0:T(1024)S(1)} %bitcast.317), kind=kOutput, calls=%fused_computation.13 | convolution fusion | flops 1008304128 | bytes 4395008 | tf_op jit(solution)/shard_map/dot_general | solution.py:127
  127.7 2.5 %collective-permute-start.36 = (bf16[4,24,1280]{2,1,0:T(8,128)(2,1)}, bf16[4,24,1280]{2,1,0:T(8,128)(2,1)}, u32[]{:S(2)}, u32[]{:S(2)}) collective-permute-start(bf16[4,24,1280]{2,1,0:T(8,128)(2,1)} %get-tuple-element.24), channel_id=1, source_target_pairs={{0,3},{1,0},{2,1},{3,2},{4,7},{5,4},{6,5},{7,6},{8,11},{9,8},{10,9... | collective-permute-start | bytes 737288 | tf_op jit(solution)/shard_map/ppermute | solution.py:18
  136.7 2.8 %collective-permute-start.30 = (bf16[4,24,1282]{2,1,0:T(8,128)(2,1)S(1)}, bf16[4,24,1282]{2,1,0:T(8,128)(2,1)S(1)}, u32[]{:S(2)}, u32[]{:S(2)}) collective-permute-start(bf16[4,24,1282]{2,1,0:T(8,128)(2,1)S(1)} %get-tuple-element.18), channel_id=1, source_target_pairs={{0,12},{1,13},{2,14},{3,15},{4,0},{5,1},{6,2},{7,3},{8,4},{9,5},{1... | collective-permute-start | bytes 738440 | tf_op jit(solution)/shard_map/ppermute | solution.py:18
  139.4 2.6 %collective-permute-done.34 = bf16[4,24,1280]{2,1,0:T(8,128)(2,1)} collective-permute-done((bf16[4,24,1280]{2,1,0:T(8,128)(2,1)}, bf16[4,24,1280]{2,1,0:T(8,128)(2,1)}, u32[]{:S(2)}, u32[]{:S(2)}) %collective-permute-start.34) | collective-permute-done | bytes 245792 | tf_op jit(solution)/shard_map/ppermute | solution.py:18
  144.6 3.2 %collective-permute-start.39 = (bf16[24,1280]{1,0:T(8,128)(2,1)S(1)}, bf16[24,1280]{1,0:T(8,128)(2,1)S(1)}, u32[]{:S(2)}, u32[]{:S(2)}) collective-permute-start(bf16[24,1280]{1,0:T(8,128)(2,1)S(1)} %get-tuple-element.46), channel_id=1, source_target_pairs={{0,12},{1,13},{2,14},{3,15},{4,0},{5,1},{6,2},{7,3},{8,4},{9,5},{1... | collective-permute-start | bytes 184328 | tf_op jit(solution)/shard_map/ppermute | solution.py:18
  149.1 3.4 %collective-permute-done.30 = bf16[4,24,1282]{2,1,0:T(8,128)(2,1)S(1)} collective-permute-done((bf16[4,24,1282]{2,1,0:T(8,128)(2,1)S(1)}, bf16[4,24,1282]{2,1,0:T(8,128)(2,1)S(1)}, u32[]{:S(2)}, u32[]{:S(2)}) %collective-permute-start.30) | collective-permute-done | bytes 246176 | tf_op jit(solution)/shard_map/ppermute | solution.py:18
  153.6 2.6 %collective-permute-start.33 = (f32[24,1282]{1,0:T(8,128)S(1)}, f32[24,1282]{1,0:T(8,128)S(1)}, u32[]{:S(2)}, u32[]{:S(2)}) collective-permute-start(f32[24,1282]{1,0:T(8,128)S(1)} %get-tuple-element.36), channel_id=1, source_target_pairs={{0,3},{1,0},{2,1},{3,2},{4,7},{5,4},{6,5},{7,6},{8,11},{9,8},{10,9... | collective-permute-start | bytes 369224 | tf_op jit(solution)/shard_map/ppermute | solution.py:18
  157.5 3.0 %collective-permute-done.31 = f32[24,1282]{1,0:T(8,128)S(1)} collective-permute-done((f32[24,1282]{1,0:T(8,128)S(1)}, f32[24,1282]{1,0:T(8,128)S(1)}, u32[]{:S(2)}, u32[]{:S(2)}) %collective-permute-start.31) | collective-permute-done | bytes 123104 | tf_op jit(solution)/shard_map/ppermute | solution.py:18
  164.5 3.4 %collective-permute-start.42 = (bf16[24,2048]{1,0:T(8,128)(2,1)S(1)}, bf16[24,2048]{1,0:T(8,128)(2,1)S(1)}, u32[]{:S(2)}, u32[]{:S(2)}) collective-permute-start(bf16[24,2048]{1,0:T(8,128)(2,1)S(1)} %reshape.646), channel_id=1, source_target_pairs={{0,12},{1,13},{2,14},{3,15},{4,0},{5,1},{6,2},{7,3},{8,4},{9,5},{1... | collective-permute-start | bytes 294920 | tf_op jit(solution)/shard_map/ppermute | solution.py:18
  171.2 3.0 %collective-permute-done.41 = bf16[24,2048]{1,0:T(8,128)(2,1)S(1)} collective-permute-done((bf16[24,2048]{1,0:T(8,128)(2,1)S(1)}, bf16[24,2048]{1,0:T(8,128)(2,1)S(1)}, u32[]{:S(2)}, u32[]{:S(2)}) %collective-permute-start.41) | collective-permute-done | bytes 98336 | tf_op jit(solution)/shard_map/ppermute | solution.py:18
  177.8 2.6 %collective-permute-start.45 = (bf16[4,24,2048]{2,1,0:T(8,128)(2,1)}, bf16[4,24,2048]{2,1,0:T(8,128)(2,1)}, u32[]{:S(2)}, u32[]{:S(2)}) collective-permute-start(bf16[4,24,2048]{2,1,0:T(8,128)(2,1)} %get-tuple-element.42), channel_id=1, source_target_pairs={{0,3},{1,0},{2,1},{3,2},{4,7},{5,4},{6,5},{7,6},{8,11},{9,8},{10,9... | collective-permute-start | bytes 1179656 | tf_op jit(solution)/shard_map/ppermute | solution.py:18
  182.9 3.3 %collective-permute-done.44 = bf16[4,24,2048]{2,1,0:T(8,128)(2,1)} collective-permute-done((bf16[4,24,2048]{2,1,0:T(8,128)(2,1)}, bf16[4,24,2048]{2,1,0:T(8,128)(2,1)}, u32[]{:S(2)}, u32[]{:S(2)}) %collective-permute-start.44) | collective-permute-done | bytes 393248 | tf_op jit(solution)/shard_map/ppermute | solution.py:18
  186.2 4.1 %collective-permute-done.43 = bf16[4,24,2048]{2,1,0:T(8,128)(2,1)} collective-permute-done((bf16[4,24,2048]{2,1,0:T(8,128)(2,1)}, bf16[4,24,2048]{2,1,0:T(8,128)(2,1)}, u32[]{:S(2)}, u32[]{:S(2)}) %collective-permute-start.43) | collective-permute-done | bytes 393248 | tf_op jit(solution)/shard_map/ppermute | solution.py:18
  191.7 4.0 %fusion.15 = bf16[384,1024]{1,0:T(8,128)(2,1)S(1)} fusion(bf16[384,2048]{1,0:T(8,128)(2,1)S(1)} %bitcast.275, bf16[1,2048,1024]{2,1,0:T(8,128)(2,1)} %param.14), kind=kOutput, calls=%fused_computation.30 | convolution fusion | flops 1611005952 | bytes 6553600 | tf_op jit(solution)/shard_map/dot_general | solution.py:165
  198.1 3.2 %collective-permute-start.48 = (bf16[3,32,1024]{2,1,0:T(8,128)(2,1)S(1)}, bf16[3,32,1024]{2,1,0:T(8,128)(2,1)S(1)}, u32[]{:S(2)}, u32[]{:S(2)}) collective-permute-start(bf16[3,32,1024]{2,1,0:T(8,128)(2,1)S(1)} %get-tuple-element.30), channel_id=1, source_target_pairs={{0,48},{16,0},{32,16},{48,32},{1,49},{17,1},{33,17},{49,33},{2,50}... | collective-permute-start | bytes 589832 | tf_op jit(solution)/shard_map/ppermute | solution.py:18
  202.0 2.9 %collective-permute-done.46 = bf16[3,32,1024]{2,1,0:T(8,128)(2,1)S(1)} collective-permute-done((bf16[3,32,1024]{2,1,0:T(8,128)(2,1)S(1)}, bf16[3,32,1024]{2,1,0:T(8,128)(2,1)S(1)}, u32[]{:S(2)}, u32[]{:S(2)}) %collective-permute-start.46) | collective-permute-done | bytes 196640 | tf_op jit(solution)/shard_map/ppermute | solution.py:18
  (268 shorter events, 125.6 us)
Async XLA Ops:
  0.6 12.0 %collective-permute-start = (bf16[3,32,1024]{2,1,0:T(8,128)(2,1)}, bf16[3,32,1024]{2,1,0:T(8,128)(2,1)S(1)}, u32[]{:S(2)}, u32[]{:S(2)}) collective-permute-start(bf16[3,32,1024]{2,1,0:T(8,128)(2,1)} %param.10), channel_id=1, source_target_pairs={{0,16},{16,32},{32,48},{48,0},{1,17},{17,33},{33,49},{49,1},{2,18}... | collective-permute-start | bytes 589832 | tf_op jit(solution)/shard_map/ppermute | solution.py:18
  2.3 10.3 %collective-permute-start.2 = (bf16[3,32,1024]{2,1,0:T(8,128)(2,1)}, bf16[3,32,1024]{2,1,0:T(8,128)(2,1)S(1)}, u32[]{:S(2)}, u32[]{:S(2)}) collective-permute-start(bf16[3,32,1024]{2,1,0:T(8,128)(2,1)} %param.10), channel_id=1, source_target_pairs={{0,48},{16,0},{32,16},{48,32},{1,49},{17,1},{33,17},{49,33},{2,50}... | collective-permute-start | bytes 589832 | tf_op jit(solution)/shard_map/ppermute | solution.py:18
  26.5 11.6 %collective-permute-start.9 = (bf16[4,24,1280]{2,1,0:T(8,128)(2,1)}, bf16[4,24,1280]{2,1,0:T(8,128)(2,1)}, u32[]{:S(2)}, u32[]{:S(2)}) collective-permute-start(bf16[4,24,1280]{2,1,0:T(8,128)(2,1)} %get-tuple-element.26), channel_id=1, source_target_pairs={{0,1},{1,2},{2,3},{3,0},{4,5},{5,6},{6,7},{7,4},{8,9},{9,10},{10,1... | collective-permute-start | bytes 737288 | tf_op jit(solution)/shard_map/ppermute | solution.py:18
  28.1 11.8 %collective-permute-start.11 = (bf16[4,24,1280]{2,1,0:T(8,128)(2,1)}, bf16[4,24,1280]{2,1,0:T(8,128)(2,1)}, u32[]{:S(2)}, u32[]{:S(2)}) collective-permute-start(bf16[4,24,1280]{2,1,0:T(8,128)(2,1)} %get-tuple-element.27), channel_id=1, source_target_pairs={{0,3},{1,0},{2,1},{3,2},{4,7},{5,4},{6,5},{7,6},{8,11},{9,8},{10,9... | collective-permute-start | bytes 737288 | tf_op jit(solution)/shard_map/ppermute | solution.py:18
  29.8 11.6 %collective-permute-start.10 = (bf16[4,24,1280]{2,1,0:T(8,128)(2,1)}, bf16[4,24,1280]{2,1,0:T(8,128)(2,1)}, u32[]{:S(2)}, u32[]{:S(2)}) collective-permute-start(bf16[4,24,1280]{2,1,0:T(8,128)(2,1)} %get-tuple-element.28), channel_id=1, source_target_pairs={{0,2},{1,3},{2,0},{3,1},{4,6},{5,7},{6,4},{7,5},{8,10},{9,11},{10,... | collective-permute-start | bytes 737288 | tf_op jit(solution)/shard_map/ppermute | solution.py:18
  33.9 13.2 %collective-permute-start.3 = (bf16[4,24,1282]{2,1,0:T(8,128)(2,1)S(1)}, bf16[4,24,1282]{2,1,0:T(8,128)(2,1)S(1)}, u32[]{:S(2)}, u32[]{:S(2)}) collective-permute-start(bf16[4,24,1282]{2,1,0:T(8,128)(2,1)S(1)} %get-tuple-element.20), channel_id=1, source_target_pairs={{0,4},{1,5},{2,6},{3,7},{4,8},{5,9},{6,10},{7,11},{8,12},{9,13},{1... | collective-permute-start | bytes 738440 | tf_op jit(solution)/shard_map/ppermute | solution.py:18
  35.9 14.6 %collective-permute-start.5 = (bf16[4,24,1282]{2,1,0:T(8,128)(2,1)S(1)}, bf16[4,24,1282]{2,1,0:T(8,128)(2,1)S(1)}, u32[]{:S(2)}, u32[]{:S(2)}) collective-permute-start(bf16[4,24,1282]{2,1,0:T(8,128)(2,1)S(1)} %get-tuple-element.21), channel_id=1, source_target_pairs={{0,12},{1,13},{2,14},{3,15},{4,0},{5,1},{6,2},{7,3},{8,4},{9,5},{1... | collective-permute-start | bytes 738440 | tf_op jit(solution)/shard_map/ppermute | solution.py:18
  38.1 13.0 %collective-permute-start.4 = (bf16[4,24,1282]{2,1,0:T(8,128)(2,1)S(1)}, bf16[4,24,1282]{2,1,0:T(8,128)(2,1)S(1)}, u32[]{:S(2)}, u32[]{:S(2)}) collective-permute-start(bf16[4,24,1282]{2,1,0:T(8,128)(2,1)S(1)} %get-tuple-element.22), channel_id=1, source_target_pairs={{0,8},{1,9},{2,10},{3,11},{4,12},{5,13},{6,14},{7,15},{8,0},{9,1},... | collective-permute-start | bytes 738440 | tf_op jit(solution)/shard_map/ppermute | solution.py:18
  42.9 11.7 %collective-permute-start.12 = (bf16[24,1280]{1,0:T(8,128)(2,1)S(1)}, bf16[24,1280]{1,0:T(8,128)(2,1)S(1)}, u32[]{:S(2)}, u32[]{:S(2)}) collective-permute-start(bf16[24,1280]{1,0:T(8,128)(2,1)S(1)} %get-tuple-element.48), channel_id=1, source_target_pairs={{0,4},{1,5},{2,6},{3,7},{4,8},{5,9},{6,10},{7,11},{8,12},{9,13},{1... | collective-permute-start | bytes 184328 | tf_op jit(solution)/shard_map/ppermute | solution.py:18
  44.9 10.2 %collective-permute-start.14 = (bf16[24,1280]{1,0:T(8,128)(2,1)S(1)}, bf16[24,1280]{1,0:T(8,128)(2,1)S(1)}, u32[]{:S(2)}, u32[]{:S(2)}) collective-permute-start(bf16[24,1280]{1,0:T(8,128)(2,1)S(1)} %get-tuple-element.49), channel_id=1, source_target_pairs={{0,12},{1,13},{2,14},{3,15},{4,0},{5,1},{6,2},{7,3},{8,4},{9,5},{1... | collective-permute-start | bytes 184328 | tf_op jit(solution)/shard_map/ppermute | solution.py:18
  73.4 13.1 %collective-permute-start.18 = (bf16[4,24,2048]{2,1,0:T(8,128)(2,1)}, bf16[4,24,2048]{2,1,0:T(8,128)(2,1)S(1)}, u32[]{:S(2)}, u32[]{:S(2)}) collective-permute-start(bf16[4,24,2048]{2,1,0:T(8,128)(2,1)} %get-tuple-element.44), channel_id=1, source_target_pairs={{0,1},{1,2},{2,3},{3,0},{4,5},{5,6},{6,7},{7,4},{8,9},{9,10},{10,1... | collective-permute-start | bytes 1179656 | tf_op jit(solution)/shard_map/ppermute | solution.py:18
  74.8 11.7 %collective-permute-start.20 = (bf16[4,24,2048]{2,1,0:T(8,128)(2,1)}, bf16[4,24,2048]{2,1,0:T(8,128)(2,1)S(1)}, u32[]{:S(2)}, u32[]{:S(2)}) collective-permute-start(bf16[4,24,2048]{2,1,0:T(8,128)(2,1)} %get-tuple-element.44), channel_id=1, source_target_pairs={{0,3},{1,0},{2,1},{3,2},{4,7},{5,4},{6,5},{7,6},{8,11},{9,8},{10,9... | collective-permute-start | bytes 1179656 | tf_op jit(solution)/shard_map/ppermute | solution.py:18
  93.0 10.7 %collective-permute-start.21 = (bf16[96,1024]{1,0:T(8,128)(2,1)S(1)}, bf16[96,1024]{1,0:T(8,128)(2,1)S(1)}, u32[]{:S(2)}, u32[]{:S(2)}) collective-permute-start(bf16[96,1024]{1,0:T(8,128)(2,1)S(1)} %get-tuple-element.32), channel_id=1, source_target_pairs={{0,16},{16,32},{32,48},{48,0},{1,17},{17,33},{33,49},{49,1},{2,18}... | collective-permute-start | bytes 589832 | tf_op jit(solution)/shard_map/ppermute | solution.py:18
  127.0 15.0 %collective-permute-start.34 = (bf16[4,24,1280]{2,1,0:T(8,128)(2,1)}, bf16[4,24,1280]{2,1,0:T(8,128)(2,1)}, u32[]{:S(2)}, u32[]{:S(2)}) collective-permute-start(bf16[4,24,1280]{2,1,0:T(8,128)(2,1)} %get-tuple-element.23), channel_id=1, source_target_pairs={{0,1},{1,2},{2,3},{3,0},{4,5},{5,6},{6,7},{7,4},{8,9},{9,10},{10,1... | collective-permute-start | bytes 737288 | tf_op jit(solution)/shard_map/ppermute | solution.py:18
  127.7 15.4 %collective-permute-start.36 = (bf16[4,24,1280]{2,1,0:T(8,128)(2,1)}, bf16[4,24,1280]{2,1,0:T(8,128)(2,1)}, u32[]{:S(2)}, u32[]{:S(2)}) collective-permute-start(bf16[4,24,1280]{2,1,0:T(8,128)(2,1)} %get-tuple-element.24), channel_id=1, source_target_pairs={{0,3},{1,0},{2,1},{3,2},{4,7},{5,4},{6,5},{7,6},{8,11},{9,8},{10,9... | collective-permute-start | bytes 737288 | tf_op jit(solution)/shard_map/ppermute | solution.py:18
  130.2 12.9 %collective-permute-start.35 = (bf16[4,24,1280]{2,1,0:T(8,128)(2,1)}, bf16[4,24,1280]{2,1,0:T(8,128)(2,1)}, u32[]{:S(2)}, u32[]{:S(2)}) collective-permute-start(bf16[4,24,1280]{2,1,0:T(8,128)(2,1)} %get-tuple-element.25), channel_id=1, source_target_pairs={{0,2},{1,3},{2,0},{3,1},{4,6},{5,7},{6,4},{7,5},{8,10},{9,11},{10,... | collective-permute-start | bytes 737288 | tf_op jit(solution)/shard_map/ppermute | solution.py:18
  136.1 11.7 %collective-permute-start.28 = (bf16[4,24,1282]{2,1,0:T(8,128)(2,1)S(1)}, bf16[4,24,1282]{2,1,0:T(8,128)(2,1)S(1)}, u32[]{:S(2)}, u32[]{:S(2)}) collective-permute-start(bf16[4,24,1282]{2,1,0:T(8,128)(2,1)S(1)} %get-tuple-element.17), channel_id=1, source_target_pairs={{0,4},{1,5},{2,6},{3,7},{4,8},{5,9},{6,10},{7,11},{8,12},{9,13},{1... | collective-permute-start | bytes 738440 | tf_op jit(solution)/shard_map/ppermute | solution.py:18
  136.7 15.8 %collective-permute-start.30 = (bf16[4,24,1282]{2,1,0:T(8,128)(2,1)S(1)}, bf16[4,24,1282]{2,1,0:T(8,128)(2,1)S(1)}, u32[]{:S(2)}, u32[]{:S(2)}) collective-permute-start(bf16[4,24,1282]{2,1,0:T(8,128)(2,1)S(1)} %get-tuple-element.18), channel_id=1, source_target_pairs={{0,12},{1,13},{2,14},{3,15},{4,0},{5,1},{6,2},{7,3},{8,4},{9,5},{1... | collective-permute-start | bytes 738440 | tf_op jit(solution)/shard_map/ppermute | solution.py:18
  142.0 10.8 %collective-permute-start.29 = (bf16[4,24,1282]{2,1,0:T(8,128)(2,1)S(1)}, bf16[4,24,1282]{2,1,0:T(8,128)(2,1)S(1)}, u32[]{:S(2)}, u32[]{:S(2)}) collective-permute-start(bf16[4,24,1282]{2,1,0:T(8,128)(2,1)S(1)} %get-tuple-element.19), channel_id=1, source_target_pairs={{0,8},{1,9},{2,10},{3,11},{4,12},{5,13},{6,14},{7,15},{8,0},{9,1},... | collective-permute-start | bytes 738440 | tf_op jit(solution)/shard_map/ppermute | solution.py:18
  144.5 11.7 %collective-permute-start.37 = (bf16[24,1280]{1,0:T(8,128)(2,1)S(1)}, bf16[24,1280]{1,0:T(8,128)(2,1)S(1)}, u32[]{:S(2)}, u32[]{:S(2)}) collective-permute-start(bf16[24,1280]{1,0:T(8,128)(2,1)S(1)} %get-tuple-element.45), channel_id=1, source_target_pairs={{0,4},{1,5},{2,6},{3,7},{4,8},{5,9},{6,10},{7,11},{8,12},{9,13},{1... | collective-permute-start | bytes 184328 | tf_op jit(solution)/shard_map/ppermute | solution.py:18
  144.6 12.8 %collective-permute-start.39 = (bf16[24,1280]{1,0:T(8,128)(2,1)S(1)}, bf16[24,1280]{1,0:T(8,128)(2,1)S(1)}, u32[]{:S(2)}, u32[]{:S(2)}) collective-permute-start(bf16[24,1280]{1,0:T(8,128)(2,1)S(1)} %get-tuple-element.46), channel_id=1, source_target_pairs={{0,12},{1,13},{2,14},{3,15},{4,0},{5,1},{6,2},{7,3},{8,4},{9,5},{1... | collective-permute-start | bytes 184328 | tf_op jit(solution)/shard_map/ppermute | solution.py:18
  175.8 10.3 %collective-permute-start.44 = (bf16[4,24,2048]{2,1,0:T(8,128)(2,1)}, bf16[4,24,2048]{2,1,0:T(8,128)(2,1)}, u32[]{:S(2)}, u32[]{:S(2)}) collective-permute-start(bf16[4,24,2048]{2,1,0:T(8,128)(2,1)} %get-tuple-element.42), channel_id=1, source_target_pairs={{0,2},{1,3},{2,0},{3,1},{4,6},{5,7},{6,4},{7,5},{8,10},{9,11},{10,... | collective-permute-start | bytes 1179656 | tf_op jit(solution)/shard_map/ppermute | solution.py:18
  177.2 13.0 %collective-permute-start.43 = (bf16[4,24,2048]{2,1,0:T(8,128)(2,1)}, bf16[4,24,2048]{2,1,0:T(8,128)(2,1)}, u32[]{:S(2)}, u32[]{:S(2)}) collective-permute-start(bf16[4,24,2048]{2,1,0:T(8,128)(2,1)} %get-tuple-element.42), channel_id=1, source_target_pairs={{0,1},{1,2},{2,3},{3,0},{4,5},{5,6},{6,7},{7,4},{8,9},{9,10},{10,1... | collective-permute-start | bytes 1179656 | tf_op jit(solution)/shard_map/ppermute | solution.py:18
  177.8 12.4 %collective-permute-start.45 = (bf16[4,24,2048]{2,1,0:T(8,128)(2,1)}, bf16[4,24,2048]{2,1,0:T(8,128)(2,1)}, u32[]{:S(2)}, u32[]{:S(2)}) collective-permute-start(bf16[4,24,2048]{2,1,0:T(8,128)(2,1)} %get-tuple-element.42), channel_id=1, source_target_pairs={{0,3},{1,0},{2,1},{3,2},{4,7},{5,4},{6,5},{7,6},{8,11},{9,8},{10,9... | collective-permute-start | bytes 1179656 | tf_op jit(solution)/shard_map/ppermute | solution.py:18
  (50 other events, 384.9 us)

commit v3 on v2

--- a/solution.py
+++ b/solution.py
@@ -182,9 +182,17 @@
         rec_new = jnp.take(x_new, own_index, axis=0).reshape(rounds, rows_local, width_local)
         return x_new, rec_new, ext_new
 
-    rows_all = gather_from(hidden, tensor, n_tensor, along_tensor)
-    rows_all = rows_all.transpose(1, 0, 2, 3).reshape(-1, width_local)
-    x = jnp.take(rows_all, sort_index, axis=0)
+    arrived = jnp.stack([hidden] + [along_tensor(hidden, k) for k in range(1, n_tensor)])
+    arrived = arrived.reshape(-1, width_local)
+    src_t = inverse // req_local
+    shift_t = (tensor - src_t) % n_tensor
+    within = (inverse % req_local) * DRAFT_BLOCK
+    arrival_index = (
+        ((shift_t[:, None, None] * rounds + rr[None, :, None]) * rows_local)
+        + within[:, None, None]
+        + jj[None, None, :]
+    ).reshape(-1)
+    x = jnp.take(arrived, arrival_index, axis=0)
     record = None
     ext = None
     for step in range(n_segment):

time: 210 us -> 207 us (0.986)
  matrix products: 21.3 us -> 19.1 us
    dot_general x2, matrix products: 7.98 us -> 5.81 us  [layer(): jnp.dot(gathered, w_out[0], preferred_element_type=f32).astype(bf16)]
where the time goes in v3:
time: 207 us; the launch traced here: 206 us
  starting transfers between devices  72.3 us (35%)
  waiting for transfers between devices  72.1 us (35%)
  local copies, waits for them, and re-layouts  24.6 us (12%)
  matrix products  19.1 us (9%)
  other arithmetic  16.5 us (8%)
    ppermute x48, waiting for transfers between devices, shifted(): return lax.ppermute(x, axis, [(i, fn(i, n)) for i in range(n)])  71.7 us
    ppermute x48, starting transfers between devices, shifted(): return lax.ppermute(x, axis, [(i, fn(i, n)) for i in range(n)])  71 us
    dot_general x2, matrix products, layer(): jnp.dot(gathered, w_out[0], preferred_element_type=f32).astype(bf16)  5.81 us
    dot_general x2, matrix products, layer(): rest = jnp.dot(xg, w_query[0, :, cut:], preferred_element_type=f32)  4.59 us
    dot_general x2, matrix products, layer(): jnp.dot(xg, w_query[0, :, :cut], preferred_element_type=f32).astype(bf16)  4.18 us
  transfers between devices with their start and end apart: 49, of which 31 were waited for; matrix products, arithmetic and copies ran while one was open for 12% of the time, Pallas kernels for 0%

profile of v3, /device:TPU:0, one launch (start us, length us, event | category | flops | bytes accessed | tf_op | source)
XLA Modules:
  0.0 206.2 jit_solution(3154340152932014157)
XLA Ops:
  46.2 3.5 %collective-permute-start.13 = (bf16[24,1280]{1,0:T(8,128)(2,1)S(1)}, bf16[24,1280]{1,0:T(8,128)(2,1)S(1)}, u32[]{:S(2)}, u32[]{:S(2)}) collective-permute-start(bf16[24,1280]{1,0:T(8,128)(2,1)S(1)} %get-tuple-element.50), channel_id=1, source_target_pairs={{0,8},{1,9},{2,10},{3,11},{4,12},{5,13},{6,14},{7,15},{8,0},{9,1},... | collective-permute-start | bytes 184328 | tf_op jit(solution)/shard_map/ppermute | solution.py:18
  51.1 2.6 %collective-permute-start.8 = (f32[24,1282]{1,0:T(8,128)S(1)}, f32[24,1282]{1,0:T(8,128)S(1)}, u32[]{:S(2)}, u32[]{:S(2)}) collective-permute-start(f32[24,1282]{1,0:T(8,128)S(1)} %get-tuple-element.39), channel_id=1, source_target_pairs={{0,3},{1,0},{2,1},{3,2},{4,7},{5,4},{6,5},{7,6},{8,11},{9,8},{10,9... | collective-permute-start | bytes 369224 | tf_op jit(solution)/shard_map/ppermute | solution.py:18
  57.7 2.5 %collective-permute-done.7 = f32[24,1282]{1,0:T(8,128)S(1)} collective-permute-done((f32[24,1282]{1,0:T(8,128)S(1)}, f32[24,1282]{1,0:T(8,128)S(1)}, u32[]{:S(2)}, u32[]{:S(2)}) %collective-permute-start.7) | collective-permute-done | bytes 123104 | tf_op jit(solution)/shard_map/ppermute | solution.py:18
  66.7 3.1 %collective-permute-done.16 = bf16[24,2048]{1,0:T(8,128)(2,1)S(1)} collective-permute-done((bf16[24,2048]{1,0:T(8,128)(2,1)S(1)}, bf16[24,2048]{1,0:T(8,128)(2,1)S(1)}, u32[]{:S(2)}, u32[]{:S(2)}) %collective-permute-start.16) | collective-permute-done | bytes 98336 | tf_op jit(solution)/shard_map/ppermute | solution.py:18
  75.8 4.9 %collective-permute-done.19 = bf16[4,24,2048]{2,1,0:T(8,128)(2,1)S(1)} collective-permute-done((bf16[4,24,2048]{2,1,0:T(8,128)(2,1)S(1)}, bf16[4,24,2048]{2,1,0:T(8,128)(2,1)S(1)}, u32[]{:S(2)}, u32[]{:S(2)}) %collective-permute-start.19) | collective-permute-done | bytes 393248 | tf_op jit(solution)/shard_map/ppermute | solution.py:18
  80.7 4.1 %collective-permute-done.18 = bf16[4,24,2048]{2,1,0:T(8,128)(2,1)S(1)} collective-permute-done((bf16[4,24,2048]{2,1,0:T(8,128)(2,1)S(1)}, bf16[4,24,2048]{2,1,0:T(8,128)(2,1)S(1)}, u32[]{:S(2)}, u32[]{:S(2)}) %collective-permute-start.18) | collective-permute-done | bytes 393248 | tf_op jit(solution)/shard_map/ppermute | solution.py:18
  92.7 6.5 %collective-permute-done.21 = bf16[96,1024]{1,0:T(8,128)(2,1)S(1)} collective-permute-done((bf16[96,1024]{1,0:T(8,128)(2,1)S(1)}, bf16[96,1024]{1,0:T(8,128)(2,1)S(1)}, u32[]{:S(2)}, u32[]{:S(2)}) %collective-permute-start.21) | collective-permute-done | bytes 196640 | tf_op jit(solution)/shard_map/ppermute | solution.py:18
  105.3 4.4 %collective-permute-done.26 = bf16[96,1024]{1,0:T(8,128)(2,1)S(1)} collective-permute-done((bf16[96,1024]{1,0:T(8,128)(2,1)S(1)}, bf16[96,1024]{1,0:T(8,128)(2,1)S(1)}, u32[]{:S(2)}, u32[]{:S(2)}) %collective-permute-start.26) | collective-permute-done | bytes 196640 | tf_op jit(solution)/shard_map/ppermute | solution.py:18
  119.4 2.9 %convolution_convert_fusion = bf16[384,1280]{1,0:T(8,128)(2,1)S(1)} fusion(bf16[1,1024,2048]{2,1,0:T(8,128)(2,1)} %param.12, bf16[384,1024]{1,0:T(8,128)(2,1)S(1)} %collective-permute-done.27, f32[1024]{0:T(1024)S(1)} %bitcast.315), kind=kOutput, calls=%fused_computation.12 | convolution fusion | flops 1008304128 | bytes 4395008 | tf_op jit(solution)/shard_map/dot_general | solution.py:127
  123.6 3.0 %collective-permute-start.36 = (bf16[4,24,1280]{2,1,0:T(8,128)(2,1)}, bf16[4,24,1280]{2,1,0:T(8,128)(2,1)}, u32[]{:S(2)}, u32[]{:S(2)}) collective-permute-start(bf16[4,24,1280]{2,1,0:T(8,128)(2,1)} %get-tuple-element.24), channel_id=1, source_target_pairs={{0,3},{1,0},{2,1},{3,2},{4,7},{5,4},{6,5},{7,6},{8,11},{9,8},{10,9... | collective-permute-start | bytes 737288 | tf_op jit(solution)/shard_map/ppermute | solution.py:18
  132.6 3.0 %collective-permute-start.30 = (bf16[4,24,1282]{2,1,0:T(8,128)(2,1)S(1)}, bf16[4,24,1282]{2,1,0:T(8,128)(2,1)S(1)}, u32[]{:S(2)}, u32[]{:S(2)}) collective-permute-start(bf16[4,24,1282]{2,1,0:T(8,128)(2,1)S(1)} %get-tuple-element.18), channel_id=1, source_target_pairs={{0,12},{1,13},{2,14},{3,15},{4,0},{5,1},{6,2},{7,3},{8,4},{9,5},{1... | collective-permute-start | bytes 738440 | tf_op jit(solution)/shard_map/ppermute | solution.py:18
  135.6 2.8 %collective-permute-done.34 = bf16[4,24,1280]{2,1,0:T(8,128)(2,1)} collective-permute-done((bf16[4,24,1280]{2,1,0:T(8,128)(2,1)}, bf16[4,24,1280]{2,1,0:T(8,128)(2,1)}, u32[]{:S(2)}, u32[]{:S(2)}) %collective-permute-start.34) | collective-permute-done | bytes 245792 | tf_op jit(solution)/shard_map/ppermute | solution.py:18
  141.0 3.2 %collective-permute-start.39 = (bf16[24,1280]{1,0:T(8,128)(2,1)S(1)}, bf16[24,1280]{1,0:T(8,128)(2,1)S(1)}, u32[]{:S(2)}, u32[]{:S(2)}) collective-permute-start(bf16[24,1280]{1,0:T(8,128)(2,1)S(1)} %get-tuple-element.46), channel_id=1, source_target_pairs={{0,12},{1,13},{2,14},{3,15},{4,0},{5,1},{6,2},{7,3},{8,4},{9,5},{1... | collective-permute-start | bytes 184328 | tf_op jit(solution)/shard_map/ppermute | solution.py:18
  145.7 3.2 %collective-permute-done.30 = bf16[4,24,1282]{2,1,0:T(8,128)(2,1)S(1)} collective-permute-done((bf16[4,24,1282]{2,1,0:T(8,128)(2,1)S(1)}, bf16[4,24,1282]{2,1,0:T(8,128)(2,1)S(1)}, u32[]{:S(2)}, u32[]{:S(2)}) %collective-permute-start.30) | collective-permute-done | bytes 246176 | tf_op jit(solution)/shard_map/ppermute | solution.py:18
  149.4 3.2 %collective-permute-start.33 = (f32[24,1282]{1,0:T(8,128)S(1)}, f32[24,1282]{1,0:T(8,128)S(1)}, u32[]{:S(2)}, u32[]{:S(2)}) collective-permute-start(f32[24,1282]{1,0:T(8,128)S(1)} %get-tuple-element.36), channel_id=1, source_target_pairs={{0,3},{1,0},{2,1},{3,2},{4,7},{5,4},{6,5},{7,6},{8,11},{9,8},{10,9... | collective-permute-start | bytes 369224 | tf_op jit(solution)/shard_map/ppermute | solution.py:18
  153.9 3.1 %collective-permute-done.31 = f32[24,1282]{1,0:T(8,128)S(1)} collective-permute-done((f32[24,1282]{1,0:T(8,128)S(1)}, f32[24,1282]{1,0:T(8,128)S(1)}, u32[]{:S(2)}, u32[]{:S(2)}) %collective-permute-start.31) | collective-permute-done | bytes 123104 | tf_op jit(solution)/shard_map/ppermute | solution.py:18
  160.9 3.4 %collective-permute-start.42 = (bf16[24,2048]{1,0:T(8,128)(2,1)S(1)}, bf16[24,2048]{1,0:T(8,128)(2,1)S(1)}, u32[]{:S(2)}, u32[]{:S(2)}) collective-permute-start(bf16[24,2048]{1,0:T(8,128)(2,1)S(1)} %reshape.694), channel_id=1, source_target_pairs={{0,12},{1,13},{2,14},{3,15},{4,0},{5,1},{6,2},{7,3},{8,4},{9,5},{1... | collective-permute-start | bytes 294920 | tf_op jit(solution)/shard_map/ppermute | solution.py:18
  167.6 3.0 %collective-permute-done.41 = bf16[24,2048]{1,0:T(8,128)(2,1)S(1)} collective-permute-done((bf16[24,2048]{1,0:T(8,128)(2,1)S(1)}, bf16[24,2048]{1,0:T(8,128)(2,1)S(1)}, u32[]{:S(2)}, u32[]{:S(2)}) %collective-permute-start.41) | collective-permute-done | bytes 98336 | tf_op jit(solution)/shard_map/ppermute | solution.py:18
  174.2 2.6 %collective-permute-start.45 = (bf16[4,24,2048]{2,1,0:T(8,128)(2,1)}, bf16[4,24,2048]{2,1,0:T(8,128)(2,1)}, u32[]{:S(2)}, u32[]{:S(2)}) collective-permute-start(bf16[4,24,2048]{2,1,0:T(8,128)(2,1)} %get-tuple-element.42), channel_id=1, source_target_pairs={{0,3},{1,0},{2,1},{3,2},{4,7},{5,4},{6,5},{7,6},{8,11},{9,8},{10,9... | collective-permute-start | bytes 1179656 | tf_op jit(solution)/shard_map/ppermute | solution.py:18
  179.2 3.7 %collective-permute-done.44 = bf16[4,24,2048]{2,1,0:T(8,128)(2,1)} collective-permute-done((bf16[4,24,2048]{2,1,0:T(8,128)(2,1)}, bf16[4,24,2048]{2,1,0:T(8,128)(2,1)}, u32[]{:S(2)}, u32[]{:S(2)}) %collective-permute-start.44) | collective-permute-done | bytes 393248 | tf_op jit(solution)/shard_map/ppermute | solution.py:18
  183.0 4.1 %collective-permute-done.43 = bf16[4,24,2048]{2,1,0:T(8,128)(2,1)} collective-permute-done((bf16[4,24,2048]{2,1,0:T(8,128)(2,1)}, bf16[4,24,2048]{2,1,0:T(8,128)(2,1)}, u32[]{:S(2)}, u32[]{:S(2)}) %collective-permute-start.43) | collective-permute-done | bytes 393248 | tf_op jit(solution)/shard_map/ppermute | solution.py:18
  188.5 4.0 %fusion.15 = bf16[384,1024]{1,0:T(8,128)(2,1)S(1)} fusion(bf16[384,2048]{1,0:T(8,128)(2,1)S(1)} %bitcast.273, bf16[1,2048,1024]{2,1,0:T(8,128)(2,1)} %param.14), kind=kOutput, calls=%fused_computation.29 | convolution fusion | flops 1611005952 | bytes 6553600 | tf_op jit(solution)/shard_map/dot_general | solution.py:165
  194.9 3.2 %collective-permute-start.48 = (bf16[3,32,1024]{2,1,0:T(8,128)(2,1)S(1)}, bf16[3,32,1024]{2,1,0:T(8,128)(2,1)S(1)}, u32[]{:S(2)}, u32[]{:S(2)}) collective-permute-start(bf16[3,32,1024]{2,1,0:T(8,128)(2,1)S(1)} %get-tuple-element.30), channel_id=1, source_target_pairs={{0,48},{16,0},{32,16},{48,32},{1,49},{17,1},{33,17},{49,33},{2,50}... | collective-permute-start | bytes 589832 | tf_op jit(solution)/shard_map/ppermute | solution.py:18
  198.8 3.9 %collective-permute-done.46 = bf16[3,32,1024]{2,1,0:T(8,128)(2,1)S(1)} collective-permute-done((bf16[3,32,1024]{2,1,0:T(8,128)(2,1)S(1)}, bf16[3,32,1024]{2,1,0:T(8,128)(2,1)S(1)}, u32[]{:S(2)}, u32[]{:S(2)}) %collective-permute-start.46) | collective-permute-done | bytes 196640 | tf_op jit(solution)/shard_map/ppermute | solution.py:18
  (263 shorter events, 120.9 us)
Async XLA Ops:
  0.6 12.7 %collective-permute-start = (bf16[3,32,1024]{2,1,0:T(8,128)(2,1)}, bf16[3,32,1024]{2,1,0:T(8,128)(2,1)S(1)}, u32[]{:S(2)}, u32[]{:S(2)}) collective-permute-start(bf16[3,32,1024]{2,1,0:T(8,128)(2,1)} %param.10), channel_id=1, source_target_pairs={{0,16},{16,32},{32,48},{48,0},{1,17},{17,33},{33,49},{49,1},{2,18}... | collective-permute-start | bytes 589832 | tf_op jit(solution)/shard_map/ppermute | solution.py:18
  2.3 11.1 %collective-permute-start.2 = (bf16[3,32,1024]{2,1,0:T(8,128)(2,1)}, bf16[3,32,1024]{2,1,0:T(8,128)(2,1)S(1)}, u32[]{:S(2)}, u32[]{:S(2)}) collective-permute-start(bf16[3,32,1024]{2,1,0:T(8,128)(2,1)} %param.10), channel_id=1, source_target_pairs={{0,48},{16,0},{32,16},{48,32},{1,49},{17,1},{33,17},{49,33},{2,50}... | collective-permute-start | bytes 589832 | tf_op jit(solution)/shard_map/ppermute | solution.py:18
  4.0 10.1 %collective-permute-start.1 = (bf16[3,32,1024]{2,1,0:T(8,128)(2,1)}, bf16[3,32,1024]{2,1,0:T(8,128)(2,1)S(1)}, u32[]{:S(2)}, u32[]{:S(2)}) collective-permute-start(bf16[3,32,1024]{2,1,0:T(8,128)(2,1)} %param.10), channel_id=1, source_target_pairs={{0,32},{16,48},{32,0},{48,16},{1,33},{17,49},{33,1},{49,17},{2,34}... | collective-permute-start | bytes 589832 | tf_op jit(solution)/shard_map/ppermute | solution.py:18
  25.6 11.6 %collective-permute-start.9 = (bf16[4,24,1280]{2,1,0:T(8,128)(2,1)}, bf16[4,24,1280]{2,1,0:T(8,128)(2,1)}, u32[]{:S(2)}, u32[]{:S(2)}) collective-permute-start(bf16[4,24,1280]{2,1,0:T(8,128)(2,1)} %get-tuple-element.26), channel_id=1, source_target_pairs={{0,1},{1,2},{2,3},{3,0},{4,5},{5,6},{6,7},{7,4},{8,9},{9,10},{10,1... | collective-permute-start | bytes 737288 | tf_op jit(solution)/shard_map/ppermute | solution.py:18
  27.2 11.8 %collective-permute-start.11 = (bf16[4,24,1280]{2,1,0:T(8,128)(2,1)}, bf16[4,24,1280]{2,1,0:T(8,128)(2,1)}, u32[]{:S(2)}, u32[]{:S(2)}) collective-permute-start(bf16[4,24,1280]{2,1,0:T(8,128)(2,1)} %get-tuple-element.27), channel_id=1, source_target_pairs={{0,3},{1,0},{2,1},{3,2},{4,7},{5,4},{6,5},{7,6},{8,11},{9,8},{10,9... | collective-permute-start | bytes 737288 | tf_op jit(solution)/shard_map/ppermute | solution.py:18
  28.9 11.6 %collective-permute-start.10 = (bf16[4,24,1280]{2,1,0:T(8,128)(2,1)}, bf16[4,24,1280]{2,1,0:T(8,128)(2,1)}, u32[]{:S(2)}, u32[]{:S(2)}) collective-permute-start(bf16[4,24,1280]{2,1,0:T(8,128)(2,1)} %get-tuple-element.28), channel_id=1, source_target_pairs={{0,2},{1,3},{2,0},{3,1},{4,6},{5,7},{6,4},{7,5},{8,10},{9,11},{10,... | collective-permute-start | bytes 737288 | tf_op jit(solution)/shard_map/ppermute | solution.py:18
  33.0 13.2 %collective-permute-start.3 = (bf16[4,24,1282]{2,1,0:T(8,128)(2,1)S(1)}, bf16[4,24,1282]{2,1,0:T(8,128)(2,1)S(1)}, u32[]{:S(2)}, u32[]{:S(2)}) collective-permute-start(bf16[4,24,1282]{2,1,0:T(8,128)(2,1)S(1)} %get-tuple-element.20), channel_id=1, source_target_pairs={{0,4},{1,5},{2,6},{3,7},{4,8},{5,9},{6,10},{7,11},{8,12},{9,13},{1... | collective-permute-start | bytes 738440 | tf_op jit(solution)/shard_map/ppermute | solution.py:18
  35.0 14.6 %collective-permute-start.5 = (bf16[4,24,1282]{2,1,0:T(8,128)(2,1)S(1)}, bf16[4,24,1282]{2,1,0:T(8,128)(2,1)S(1)}, u32[]{:S(2)}, u32[]{:S(2)}) collective-permute-start(bf16[4,24,1282]{2,1,0:T(8,128)(2,1)S(1)} %get-tuple-element.21), channel_id=1, source_target_pairs={{0,12},{1,13},{2,14},{3,15},{4,0},{5,1},{6,2},{7,3},{8,4},{9,5},{1... | collective-permute-start | bytes 738440 | tf_op jit(solution)/shard_map/ppermute | solution.py:18
  37.2 13.0 %collective-permute-start.4 = (bf16[4,24,1282]{2,1,0:T(8,128)(2,1)S(1)}, bf16[4,24,1282]{2,1,0:T(8,128)(2,1)S(1)}, u32[]{:S(2)}, u32[]{:S(2)}) collective-permute-start(bf16[4,24,1282]{2,1,0:T(8,128)(2,1)S(1)} %get-tuple-element.22), channel_id=1, source_target_pairs={{0,8},{1,9},{2,10},{3,11},{4,12},{5,13},{6,14},{7,15},{8,0},{9,1},... | collective-permute-start | bytes 738440 | tf_op jit(solution)/shard_map/ppermute | solution.py:18
  42.0 11.7 %collective-permute-start.12 = (bf16[24,1280]{1,0:T(8,128)(2,1)S(1)}, bf16[24,1280]{1,0:T(8,128)(2,1)S(1)}, u32[]{:S(2)}, u32[]{:S(2)}) collective-permute-start(bf16[24,1280]{1,0:T(8,128)(2,1)S(1)} %get-tuple-element.48), channel_id=1, source_target_pairs={{0,4},{1,5},{2,6},{3,7},{4,8},{5,9},{6,10},{7,11},{8,12},{9,13},{1... | collective-permute-start | bytes 184328 | tf_op jit(solution)/shard_map/ppermute | solution.py:18
  44.0 10.2 %collective-permute-start.14 = (bf16[24,1280]{1,0:T(8,128)(2,1)S(1)}, bf16[24,1280]{1,0:T(8,128)(2,1)S(1)}, u32[]{:S(2)}, u32[]{:S(2)}) collective-permute-start(bf16[24,1280]{1,0:T(8,128)(2,1)S(1)} %get-tuple-element.49), channel_id=1, source_target_pairs={{0,12},{1,13},{2,14},{3,15},{4,0},{5,1},{6,2},{7,3},{8,4},{9,5},{1... | collective-permute-start | bytes 184328 | tf_op jit(solution)/shard_map/ppermute | solution.py:18
  71.9 12.9 %collective-permute-start.18 = (bf16[4,24,2048]{2,1,0:T(8,128)(2,1)S(1)}, bf16[4,24,2048]{2,1,0:T(8,128)(2,1)S(1)}, u32[]{:S(2)}, u32[]{:S(2)}) collective-permute-start(bf16[4,24,2048]{2,1,0:T(8,128)(2,1)S(1)} %get-tuple-element.44), channel_id=1, source_target_pairs={{0,1},{1,2},{2,3},{3,0},{4,5},{5,6},{6,7},{7,4},{8,9},{9,10},{10,1... | collective-permute-start | bytes 1179656 | tf_op jit(solution)/shard_map/ppermute | solution.py:18
  73.3 11.5 %collective-permute-start.20 = (bf16[4,24,2048]{2,1,0:T(8,128)(2,1)S(1)}, bf16[4,24,2048]{2,1,0:T(8,128)(2,1)S(1)}, u32[]{:S(2)}, u32[]{:S(2)}) collective-permute-start(bf16[4,24,2048]{2,1,0:T(8,128)(2,1)S(1)} %get-tuple-element.44), channel_id=1, source_target_pairs={{0,3},{1,0},{2,1},{3,2},{4,7},{5,4},{6,5},{7,6},{8,11},{9,8},{10,9... | collective-permute-start | bytes 1179656 | tf_op jit(solution)/shard_map/ppermute | solution.py:18
  123.3 15.0 %collective-permute-start.34 = (bf16[4,24,1280]{2,1,0:T(8,128)(2,1)}, bf16[4,24,1280]{2,1,0:T(8,128)(2,1)}, u32[]{:S(2)}, u32[]{:S(2)}) collective-permute-start(bf16[4,24,1280]{2,1,0:T(8,128)(2,1)} %get-tuple-element.23), channel_id=1, source_target_pairs={{0,1},{1,2},{2,3},{3,0},{4,5},{5,6},{6,7},{7,4},{8,9},{9,10},{10,1... | collective-permute-start | bytes 737288 | tf_op jit(solution)/shard_map/ppermute | solution.py:18
  123.6 15.6 %collective-permute-start.36 = (bf16[4,24,1280]{2,1,0:T(8,128)(2,1)}, bf16[4,24,1280]{2,1,0:T(8,128)(2,1)}, u32[]{:S(2)}, u32[]{:S(2)}) collective-permute-start(bf16[4,24,1280]{2,1,0:T(8,128)(2,1)} %get-tuple-element.24), channel_id=1, source_target_pairs={{0,3},{1,0},{2,1},{3,2},{4,7},{5,4},{6,5},{7,6},{8,11},{9,8},{10,9... | collective-permute-start | bytes 737288 | tf_op jit(solution)/shard_map/ppermute | solution.py:18
  126.6 12.6 %collective-permute-start.35 = (bf16[4,24,1280]{2,1,0:T(8,128)(2,1)}, bf16[4,24,1280]{2,1,0:T(8,128)(2,1)}, u32[]{:S(2)}, u32[]{:S(2)}) collective-permute-start(bf16[4,24,1280]{2,1,0:T(8,128)(2,1)} %get-tuple-element.25), channel_id=1, source_target_pairs={{0,2},{1,3},{2,0},{3,1},{4,6},{5,7},{6,4},{7,5},{8,10},{9,11},{10,... | collective-permute-start | bytes 737288 | tf_op jit(solution)/shard_map/ppermute | solution.py:18
  132.3 11.9 %collective-permute-start.28 = (bf16[4,24,1282]{2,1,0:T(8,128)(2,1)S(1)}, bf16[4,24,1282]{2,1,0:T(8,128)(2,1)S(1)}, u32[]{:S(2)}, u32[]{:S(2)}) collective-permute-start(bf16[4,24,1282]{2,1,0:T(8,128)(2,1)S(1)} %get-tuple-element.17), channel_id=1, source_target_pairs={{0,4},{1,5},{2,6},{3,7},{4,8},{5,9},{6,10},{7,11},{8,12},{9,13},{1... | collective-permute-start | bytes 738440 | tf_op jit(solution)/shard_map/ppermute | solution.py:18
  132.6 16.2 %collective-permute-start.30 = (bf16[4,24,1282]{2,1,0:T(8,128)(2,1)S(1)}, bf16[4,24,1282]{2,1,0:T(8,128)(2,1)S(1)}, u32[]{:S(2)}, u32[]{:S(2)}) collective-permute-start(bf16[4,24,1282]{2,1,0:T(8,128)(2,1)S(1)} %get-tuple-element.18), channel_id=1, source_target_pairs={{0,12},{1,13},{2,14},{3,15},{4,0},{5,1},{6,2},{7,3},{8,4},{9,5},{1... | collective-permute-start | bytes 738440 | tf_op jit(solution)/shard_map/ppermute | solution.py:18
  138.4 10.8 %collective-permute-start.29 = (bf16[4,24,1282]{2,1,0:T(8,128)(2,1)S(1)}, bf16[4,24,1282]{2,1,0:T(8,128)(2,1)S(1)}, u32[]{:S(2)}, u32[]{:S(2)}) collective-permute-start(bf16[4,24,1282]{2,1,0:T(8,128)(2,1)S(1)} %get-tuple-element.19), channel_id=1, source_target_pairs={{0,8},{1,9},{2,10},{3,11},{4,12},{5,13},{6,14},{7,15},{8,0},{9,1},... | collective-permute-start | bytes 738440 | tf_op jit(solution)/shard_map/ppermute | solution.py:18
  140.7 12.0 %collective-permute-start.37 = (bf16[24,1280]{1,0:T(8,128)(2,1)S(1)}, bf16[24,1280]{1,0:T(8,128)(2,1)S(1)}, u32[]{:S(2)}, u32[]{:S(2)}) collective-permute-start(bf16[24,1280]{1,0:T(8,128)(2,1)S(1)} %get-tuple-element.45), channel_id=1, source_target_pairs={{0,4},{1,5},{2,6},{3,7},{4,8},{5,9},{6,10},{7,11},{8,12},{9,13},{1... | collective-permute-start | bytes 184328 | tf_op jit(solution)/shard_map/ppermute | solution.py:18
  141.0 12.8 %collective-permute-start.39 = (bf16[24,1280]{1,0:T(8,128)(2,1)S(1)}, bf16[24,1280]{1,0:T(8,128)(2,1)S(1)}, u32[]{:S(2)}, u32[]{:S(2)}) collective-permute-start(bf16[24,1280]{1,0:T(8,128)(2,1)S(1)} %get-tuple-element.46), channel_id=1, source_target_pairs={{0,12},{1,13},{2,14},{3,15},{4,0},{5,1},{6,2},{7,3},{8,4},{9,5},{1... | collective-permute-start | bytes 184328 | tf_op jit(solution)/shard_map/ppermute | solution.py:18
  172.2 10.8 %collective-permute-start.44 = (bf16[4,24,2048]{2,1,0:T(8,128)(2,1)}, bf16[4,24,2048]{2,1,0:T(8,128)(2,1)}, u32[]{:S(2)}, u32[]{:S(2)}) collective-permute-start(bf16[4,24,2048]{2,1,0:T(8,128)(2,1)} %get-tuple-element.42), channel_id=1, source_target_pairs={{0,2},{1,3},{2,0},{3,1},{4,6},{5,7},{6,4},{7,5},{8,10},{9,11},{10,... | collective-permute-start | bytes 1179656 | tf_op jit(solution)/shard_map/ppermute | solution.py:18
  173.6 13.5 %collective-permute-start.43 = (bf16[4,24,2048]{2,1,0:T(8,128)(2,1)}, bf16[4,24,2048]{2,1,0:T(8,128)(2,1)}, u32[]{:S(2)}, u32[]{:S(2)}) collective-permute-start(bf16[4,24,2048]{2,1,0:T(8,128)(2,1)} %get-tuple-element.42), channel_id=1, source_target_pairs={{0,1},{1,2},{2,3},{3,0},{4,5},{5,6},{6,7},{7,4},{8,9},{9,10},{10,1... | collective-permute-start | bytes 1179656 | tf_op jit(solution)/shard_map/ppermute | solution.py:18
  174.2 12.8 %collective-permute-start.45 = (bf16[4,24,2048]{2,1,0:T(8,128)(2,1)}, bf16[4,24,2048]{2,1,0:T(8,128)(2,1)}, u32[]{:S(2)}, u32[]{:S(2)}) collective-permute-start(bf16[4,24,2048]{2,1,0:T(8,128)(2,1)} %get-tuple-element.42), channel_id=1, source_target_pairs={{0,3},{1,0},{2,1},{3,2},{4,7},{5,4},{6,5},{7,6},{8,11},{9,8},{10,9... | collective-permute-start | bytes 1179656 | tf_op jit(solution)/shard_map/ppermute | solution.py:18
  (49 other events, 366.2 us)

commit v4 on v3

--- a/solution.py
+++ b/solution.py
@@ -32,11 +32,11 @@
     return shifted(x, "batch", lambda i, n: ((i // m + k) % (n // m)) * m + i % m)
 
 
-def spread(blocks, pos, send):
-    m = blocks.shape[0]
-    out = [lax.dynamic_index_in_dim(blocks, pos, 0, keepdims=False)]
+def spread(blocks, pos, send, axis=0):
+    m = blocks.shape[axis]
+    out = [lax.dynamic_index_in_dim(blocks, pos, axis, keepdims=False)]
     for k in range(1, m):
-        piece = lax.dynamic_index_in_dim(blocks, (pos + k) % m, 0, keepdims=False)
+        piece = lax.dynamic_index_in_dim(blocks, (pos + k) % m, axis, keepdims=False)
         out.append(send(piece, k))
     return out
 
@@ -128,9 +128,9 @@
         rest = jnp.dot(xg, w_query[0, :, cut:], preferred_element_type=f32)
         second = jnp.dot(xg, key_value_weight[0], preferred_element_type=f32)
         rest = jnp.concatenate([rest.astype(bf16), second.astype(bf16), sq_hi, sq_lo], axis=1)
-        first_y = first_half.reshape(n_z, n_y, own_rows, cut).transpose(1, 0, 2, 3)
+        first_y = first_half.reshape(n_z, n_y, own_rows, cut)
         first_z = rest.reshape(n_z, n_y, own_rows, rest.shape[1])
-        part_a = sum(r.astype(f32) for r in spread(first_y, y_pos, along_y)).astype(bf16)
+        part_a = sum(r.astype(f32) for r in spread(first_y, y_pos, along_y, 1)).astype(bf16)
         part_b = sum(r.astype(f32) for r in spread(first_z, z_pos, along_z))
         total_a = sum(r.astype(f32) for r in spread(part_a, z_pos, along_z))
         total_b = sum(spread(part_b, y_pos, along_y))

time: 207 us -> 207 us (level)
  no operation moved by 1% of the time
where the time goes in v4:
time: 207 us; the launch traced here: 206 us
  starting transfers between devices  72.3 us (35%)
  waiting for transfers between devices  72.1 us (35%)
  local copies, waits for them, and re-layouts  24.6 us (12%)
  matrix products  19.1 us (9%)
  other arithmetic  16.5 us (8%)
    ppermute x48, waiting for transfers between devices, shifted(): return lax.ppermute(x, axis, [(i, fn(i, n)) for i in range(n)])  71.7 us
    ppermute x48, starting transfers between devices, shifted(): return lax.ppermute(x, axis, [(i, fn(i, n)) for i in range(n)])  71 us
    dot_general x2, matrix products, layer(): jnp.dot(gathered, w_out[0], preferred_element_type=f32).astype(bf16)  5.81 us
    dot_general x2, matrix products, layer(): rest = jnp.dot(xg, w_query[0, :, cut:], preferred_element_type=f32)  4.59 us
    dot_general x2, matrix products, layer(): jnp.dot(xg, w_query[0, :, :cut], preferred_element_type=f32).astype(bf16)  4.18 us
  transfers between devices with their start and end apart: 49, of which 31 were waited for; matrix products, arithmetic and copies ran while one was open for 12% of the time, Pallas kernels for 0%

profile of v4, /device:TPU:0, one launch (start us, length us, event | category | flops | bytes accessed | tf_op | source)
XLA Modules:
  0.0 206.2 jit_solution(3154340152932014157)
XLA Ops:
  46.2 3.5 %collective-permute-start.13 = (bf16[24,1280]{1,0:T(8,128)(2,1)S(1)}, bf16[24,1280]{1,0:T(8,128)(2,1)S(1)}, u32[]{:S(2)}, u32[]{:S(2)}) collective-permute-start(bf16[24,1280]{1,0:T(8,128)(2,1)S(1)} %get-tuple-element.50), channel_id=1, source_target_pairs={{0,8},{1,9},{2,10},{3,11},{4,12},{5,13},{6,14},{7,15},{8,0},{9,1},... | collective-permute-start | bytes 184328 | tf_op jit(solution)/shard_map/ppermute | solution.py:18
  51.1 2.6 %collective-permute-start.8 = (f32[24,1282]{1,0:T(8,128)S(1)}, f32[24,1282]{1,0:T(8,128)S(1)}, u32[]{:S(2)}, u32[]{:S(2)}) collective-permute-start(f32[24,1282]{1,0:T(8,128)S(1)} %get-tuple-element.39), channel_id=1, source_target_pairs={{0,3},{1,0},{2,1},{3,2},{4,7},{5,4},{6,5},{7,6},{8,11},{9,8},{10,9... | collective-permute-start | bytes 369224 | tf_op jit(solution)/shard_map/ppermute | solution.py:18
  57.7 2.5 %collective-permute-done.7 = f32[24,1282]{1,0:T(8,128)S(1)} collective-permute-done((f32[24,1282]{1,0:T(8,128)S(1)}, f32[24,1282]{1,0:T(8,128)S(1)}, u32[]{:S(2)}, u32[]{:S(2)}) %collective-permute-start.7) | collective-permute-done | bytes 123104 | tf_op jit(solution)/shard_map/ppermute | solution.py:18
  66.7 3.1 %collective-permute-done.16 = bf16[24,2048]{1,0:T(8,128)(2,1)S(1)} collective-permute-done((bf16[24,2048]{1,0:T(8,128)(2,1)S(1)}, bf16[24,2048]{1,0:T(8,128)(2,1)S(1)}, u32[]{:S(2)}, u32[]{:S(2)}) %collective-permute-start.16) | collective-permute-done | bytes 98336 | tf_op jit(solution)/shard_map/ppermute | solution.py:18
  75.8 4.9 %collective-permute-done.19 = bf16[4,24,2048]{2,1,0:T(8,128)(2,1)S(1)} collective-permute-done((bf16[4,24,2048]{2,1,0:T(8,128)(2,1)S(1)}, bf16[4,24,2048]{2,1,0:T(8,128)(2,1)S(1)}, u32[]{:S(2)}, u32[]{:S(2)}) %collective-permute-start.19) | collective-permute-done | bytes 393248 | tf_op jit(solution)/shard_map/ppermute | solution.py:18
  80.7 4.1 %collective-permute-done.18 = bf16[4,24,2048]{2,1,0:T(8,128)(2,1)S(1)} collective-permute-done((bf16[4,24,2048]{2,1,0:T(8,128)(2,1)S(1)}, bf16[4,24,2048]{2,1,0:T(8,128)(2,1)S(1)}, u32[]{:S(2)}, u32[]{:S(2)}) %collective-permute-start.18) | collective-permute-done | bytes 393248 | tf_op jit(solution)/shard_map/ppermute | solution.py:18
  92.7 6.5 %collective-permute-done.21 = bf16[96,1024]{1,0:T(8,128)(2,1)S(1)} collective-permute-done((bf16[96,1024]{1,0:T(8,128)(2,1)S(1)}, bf16[96,1024]{1,0:T(8,128)(2,1)S(1)}, u32[]{:S(2)}, u32[]{:S(2)}) %collective-permute-start.21) | collective-permute-done | bytes 196640 | tf_op jit(solution)/shard_map/ppermute | solution.py:18
  105.3 4.4 %collective-permute-done.26 = bf16[96,1024]{1,0:T(8,128)(2,1)S(1)} collective-permute-done((bf16[96,1024]{1,0:T(8,128)(2,1)S(1)}, bf16[96,1024]{1,0:T(8,128)(2,1)S(1)}, u32[]{:S(2)}, u32[]{:S(2)}) %collective-permute-start.26) | collective-permute-done | bytes 196640 | tf_op jit(solution)/shard_map/ppermute | solution.py:18
  119.4 2.9 %convolution_convert_fusion = bf16[384,1280]{1,0:T(8,128)(2,1)S(1)} fusion(bf16[1,1024,2048]{2,1,0:T(8,128)(2,1)} %param.12, bf16[384,1024]{1,0:T(8,128)(2,1)S(1)} %collective-permute-done.27, f32[1024]{0:T(1024)S(1)} %bitcast.315), kind=kOutput, calls=%fused_computation.12 | convolution fusion | flops 1008304128 | bytes 4395008 | tf_op jit(solution)/shard_map/dot_general | solution.py:127
  123.6 3.0 %collective-permute-start.36 = (bf16[4,24,1280]{2,1,0:T(8,128)(2,1)}, bf16[4,24,1280]{2,1,0:T(8,128)(2,1)}, u32[]{:S(2)}, u32[]{:S(2)}) collective-permute-start(bf16[4,24,1280]{2,1,0:T(8,128)(2,1)} %get-tuple-element.24), channel_id=1, source_target_pairs={{0,3},{1,0},{2,1},{3,2},{4,7},{5,4},{6,5},{7,6},{8,11},{9,8},{10,9... | collective-permute-start | bytes 737288 | tf_op jit(solution)/shard_map/ppermute | solution.py:18
  132.6 3.0 %collective-permute-start.30 = (bf16[4,24,1282]{2,1,0:T(8,128)(2,1)S(1)}, bf16[4,24,1282]{2,1,0:T(8,128)(2,1)S(1)}, u32[]{:S(2)}, u32[]{:S(2)}) collective-permute-start(bf16[4,24,1282]{2,1,0:T(8,128)(2,1)S(1)} %get-tuple-element.18), channel_id=1, source_target_pairs={{0,12},{1,13},{2,14},{3,15},{4,0},{5,1},{6,2},{7,3},{8,4},{9,5},{1... | collective-permute-start | bytes 738440 | tf_op jit(solution)/shard_map/ppermute | solution.py:18
  135.6 2.8 %collective-permute-done.34 = bf16[4,24,1280]{2,1,0:T(8,128)(2,1)} collective-permute-done((bf16[4,24,1280]{2,1,0:T(8,128)(2,1)}, bf16[4,24,1280]{2,1,0:T(8,128)(2,1)}, u32[]{:S(2)}, u32[]{:S(2)}) %collective-permute-start.34) | collective-permute-done | bytes 245792 | tf_op jit(solution)/shard_map/ppermute | solution.py:18
  141.0 3.2 %collective-permute-start.39 = (bf16[24,1280]{1,0:T(8,128)(2,1)S(1)}, bf16[24,1280]{1,0:T(8,128)(2,1)S(1)}, u32[]{:S(2)}, u32[]{:S(2)}) collective-permute-start(bf16[24,1280]{1,0:T(8,128)(2,1)S(1)} %get-tuple-element.46), channel_id=1, source_target_pairs={{0,12},{1,13},{2,14},{3,15},{4,0},{5,1},{6,2},{7,3},{8,4},{9,5},{1... | collective-permute-start | bytes 184328 | tf_op jit(solution)/shard_map/ppermute | solution.py:18
  145.7 3.2 %collective-permute-done.30 = bf16[4,24,1282]{2,1,0:T(8,128)(2,1)S(1)} collective-permute-done((bf16[4,24,1282]{2,1,0:T(8,128)(2,1)S(1)}, bf16[4,24,1282]{2,1,0:T(8,128)(2,1)S(1)}, u32[]{:S(2)}, u32[]{:S(2)}) %collective-permute-start.30) | collective-permute-done | bytes 246176 | tf_op jit(solution)/shard_map/ppermute | solution.py:18
  149.4 3.2 %collective-permute-start.33 = (f32[24,1282]{1,0:T(8,128)S(1)}, f32[24,1282]{1,0:T(8,128)S(1)}, u32[]{:S(2)}, u32[]{:S(2)}) collective-permute-start(f32[24,1282]{1,0:T(8,128)S(1)} %get-tuple-element.36), channel_id=1, source_target_pairs={{0,3},{1,0},{2,1},{3,2},{4,7},{5,4},{6,5},{7,6},{8,11},{9,8},{10,9... | collective-permute-start | bytes 369224 | tf_op jit(solution)/shard_map/ppermute | solution.py:18
  153.9 3.1 %collective-permute-done.31 = f32[24,1282]{1,0:T(8,128)S(1)} collective-permute-done((f32[24,1282]{1,0:T(8,128)S(1)}, f32[24,1282]{1,0:T(8,128)S(1)}, u32[]{:S(2)}, u32[]{:S(2)}) %collective-permute-start.31) | collective-permute-done | bytes 123104 | tf_op jit(solution)/shard_map/ppermute | solution.py:18
  160.9 3.4 %collective-permute-start.42 = (bf16[24,2048]{1,0:T(8,128)(2,1)S(1)}, bf16[24,2048]{1,0:T(8,128)(2,1)S(1)}, u32[]{:S(2)}, u32[]{:S(2)}) collective-permute-start(bf16[24,2048]{1,0:T(8,128)(2,1)S(1)} %reshape.678), channel_id=1, source_target_pairs={{0,12},{1,13},{2,14},{3,15},{4,0},{5,1},{6,2},{7,3},{8,4},{9,5},{1... | collective-permute-start | bytes 294920 | tf_op jit(solution)/shard_map/ppermute | solution.py:18
  167.6 3.0 %collective-permute-done.41 = bf16[24,2048]{1,0:T(8,128)(2,1)S(1)} collective-permute-done((bf16[24,2048]{1,0:T(8,128)(2,1)S(1)}, bf16[24,2048]{1,0:T(8,128)(2,1)S(1)}, u32[]{:S(2)}, u32[]{:S(2)}) %collective-permute-start.41) | collective-permute-done | bytes 98336 | tf_op jit(solution)/shard_map/ppermute | solution.py:18
  174.2 2.6 %collective-permute-start.45 = (bf16[4,24,2048]{2,1,0:T(8,128)(2,1)}, bf16[4,24,2048]{2,1,0:T(8,128)(2,1)}, u32[]{:S(2)}, u32[]{:S(2)}) collective-permute-start(bf16[4,24,2048]{2,1,0:T(8,128)(2,1)} %get-tuple-element.42), channel_id=1, source_target_pairs={{0,3},{1,0},{2,1},{3,2},{4,7},{5,4},{6,5},{7,6},{8,11},{9,8},{10,9... | collective-permute-start | bytes 1179656 | tf_op jit(solution)/shard_map/ppermute | solution.py:18
  179.2 3.7 %collective-permute-done.44 = bf16[4,24,2048]{2,1,0:T(8,128)(2,1)} collective-permute-done((bf16[4,24,2048]{2,1,0:T(8,128)(2,1)}, bf16[4,24,2048]{2,1,0:T(8,128)(2,1)}, u32[]{:S(2)}, u32[]{:S(2)}) %collective-permute-start.44) | collective-permute-done | bytes 393248 | tf_op jit(solution)/shard_map/ppermute | solution.py:18
  183.0 4.1 %collective-permute-done.43 = bf16[4,24,2048]{2,1,0:T(8,128)(2,1)} collective-permute-done((bf16[4,24,2048]{2,1,0:T(8,128)(2,1)}, bf16[4,24,2048]{2,1,0:T(8,128)(2,1)}, u32[]{:S(2)}, u32[]{:S(2)}) %collective-permute-start.43) | collective-permute-done | bytes 393248 | tf_op jit(solution)/shard_map/ppermute | solution.py:18
  188.5 4.0 %fusion.15 = bf16[384,1024]{1,0:T(8,128)(2,1)S(1)} fusion(bf16[384,2048]{1,0:T(8,128)(2,1)S(1)} %bitcast.273, bf16[1,2048,1024]{2,1,0:T(8,128)(2,1)} %param.14), kind=kOutput, calls=%fused_computation.29 | convolution fusion | flops 1611005952 | bytes 6553600 | tf_op jit(solution)/shard_map/dot_general | solution.py:165
  194.9 3.2 %collective-permute-start.48 = (bf16[3,32,1024]{2,1,0:T(8,128)(2,1)S(1)}, bf16[3,32,1024]{2,1,0:T(8,128)(2,1)S(1)}, u32[]{:S(2)}, u32[]{:S(2)}) collective-permute-start(bf16[3,32,1024]{2,1,0:T(8,128)(2,1)S(1)} %get-tuple-element.30), channel_id=1, source_target_pairs={{0,48},{16,0},{32,16},{48,32},{1,49},{17,1},{33,17},{49,33},{2,50}... | collective-permute-start | bytes 589832 | tf_op jit(solution)/shard_map/ppermute | solution.py:18
  198.8 3.9 %collective-permute-done.46 = bf16[3,32,1024]{2,1,0:T(8,128)(2,1)S(1)} collective-permute-done((bf16[3,32,1024]{2,1,0:T(8,128)(2,1)S(1)}, bf16[3,32,1024]{2,1,0:T(8,128)(2,1)S(1)}, u32[]{:S(2)}, u32[]{:S(2)}) %collective-permute-start.46) | collective-permute-done | bytes 196640 | tf_op jit(solution)/shard_map/ppermute | solution.py:18
  (263 shorter events, 120.9 us)
Async XLA Ops:
  0.6 12.7 %collective-permute-start = (bf16[3,32,1024]{2,1,0:T(8,128)(2,1)}, bf16[3,32,1024]{2,1,0:T(8,128)(2,1)S(1)}, u32[]{:S(2)}, u32[]{:S(2)}) collective-permute-start(bf16[3,32,1024]{2,1,0:T(8,128)(2,1)} %param.10), channel_id=1, source_target_pairs={{0,16},{16,32},{32,48},{48,0},{1,17},{17,33},{33,49},{49,1},{2,18}... | collective-permute-start | bytes 589832 | tf_op jit(solution)/shard_map/ppermute | solution.py:18
  2.3 11.1 %collective-permute-start.2 = (bf16[3,32,1024]{2,1,0:T(8,128)(2,1)}, bf16[3,32,1024]{2,1,0:T(8,128)(2,1)S(1)}, u32[]{:S(2)}, u32[]{:S(2)}) collective-permute-start(bf16[3,32,1024]{2,1,0:T(8,128)(2,1)} %param.10), channel_id=1, source_target_pairs={{0,48},{16,0},{32,16},{48,32},{1,49},{17,1},{33,17},{49,33},{2,50}... | collective-permute-start | bytes 589832 | tf_op jit(solution)/shard_map/ppermute | solution.py:18
  4.0 10.1 %collective-permute-start.1 = (bf16[3,32,1024]{2,1,0:T(8,128)(2,1)}, bf16[3,32,1024]{2,1,0:T(8,128)(2,1)S(1)}, u32[]{:S(2)}, u32[]{:S(2)}) collective-permute-start(bf16[3,32,1024]{2,1,0:T(8,128)(2,1)} %param.10), channel_id=1, source_target_pairs={{0,32},{16,48},{32,0},{48,16},{1,33},{17,49},{33,1},{49,17},{2,34}... | collective-permute-start | bytes 589832 | tf_op jit(solution)/shard_map/ppermute | solution.py:18
  25.6 11.6 %collective-permute-start.9 = (bf16[4,24,1280]{2,1,0:T(8,128)(2,1)}, bf16[4,24,1280]{2,1,0:T(8,128)(2,1)}, u32[]{:S(2)}, u32[]{:S(2)}) collective-permute-start(bf16[4,24,1280]{2,1,0:T(8,128)(2,1)} %get-tuple-element.26), channel_id=1, source_target_pairs={{0,1},{1,2},{2,3},{3,0},{4,5},{5,6},{6,7},{7,4},{8,9},{9,10},{10,1... | collective-permute-start | bytes 737288 | tf_op jit(solution)/shard_map/ppermute | solution.py:18
  27.2 11.8 %collective-permute-start.11 = (bf16[4,24,1280]{2,1,0:T(8,128)(2,1)}, bf16[4,24,1280]{2,1,0:T(8,128)(2,1)}, u32[]{:S(2)}, u32[]{:S(2)}) collective-permute-start(bf16[4,24,1280]{2,1,0:T(8,128)(2,1)} %get-tuple-element.27), channel_id=1, source_target_pairs={{0,3},{1,0},{2,1},{3,2},{4,7},{5,4},{6,5},{7,6},{8,11},{9,8},{10,9... | collective-permute-start | bytes 737288 | tf_op jit(solution)/shard_map/ppermute | solution.py:18
  28.9 11.6 %collective-permute-start.10 = (bf16[4,24,1280]{2,1,0:T(8,128)(2,1)}, bf16[4,24,1280]{2,1,0:T(8,128)(2,1)}, u32[]{:S(2)}, u32[]{:S(2)}) collective-permute-start(bf16[4,24,1280]{2,1,0:T(8,128)(2,1)} %get-tuple-element.28), channel_id=1, source_target_pairs={{0,2},{1,3},{2,0},{3,1},{4,6},{5,7},{6,4},{7,5},{8,10},{9,11},{10,... | collective-permute-start | bytes 737288 | tf_op jit(solution)/shard_map/ppermute | solution.py:18
  33.0 13.2 %collective-permute-start.3 = (bf16[4,24,1282]{2,1,0:T(8,128)(2,1)S(1)}, bf16[4,24,1282]{2,1,0:T(8,128)(2,1)S(1)}, u32[]{:S(2)}, u32[]{:S(2)}) collective-permute-start(bf16[4,24,1282]{2,1,0:T(8,128)(2,1)S(1)} %get-tuple-element.20), channel_id=1, source_target_pairs={{0,4},{1,5},{2,6},{3,7},{4,8},{5,9},{6,10},{7,11},{8,12},{9,13},{1... | collective-permute-start | bytes 738440 | tf_op jit(solution)/shard_map/ppermute | solution.py:18
  35.0 14.6 %collective-permute-start.5 = (bf16[4,24,1282]{2,1,0:T(8,128)(2,1)S(1)}, bf16[4,24,1282]{2,1,0:T(8,128)(2,1)S(1)}, u32[]{:S(2)}, u32[]{:S(2)}) collective-permute-start(bf16[4,24,1282]{2,1,0:T(8,128)(2,1)S(1)} %get-tuple-element.21), channel_id=1, source_target_pairs={{0,12},{1,13},{2,14},{3,15},{4,0},{5,1},{6,2},{7,3},{8,4},{9,5},{1... | collective-permute-start | bytes 738440 | tf_op jit(solution)/shard_map/ppermute | solution.py:18
  37.2 13.0 %collective-permute-start.4 = (bf16[4,24,1282]{2,1,0:T(8,128)(2,1)S(1)}, bf16[4,24,1282]{2,1,0:T(8,128)(2,1)S(1)}, u32[]{:S(2)}, u32[]{:S(2)}) collective-permute-start(bf16[4,24,1282]{2,1,0:T(8,128)(2,1)S(1)} %get-tuple-element.22), channel_id=1, source_target_pairs={{0,8},{1,9},{2,10},{3,11},{4,12},{5,13},{6,14},{7,15},{8,0},{9,1},... | collective-permute-start | bytes 738440 | tf_op jit(solution)/shard_map/ppermute | solution.py:18
  42.0 11.7 %collective-permute-start.12 = (bf16[24,1280]{1,0:T(8,128)(2,1)S(1)}, bf16[24,1280]{1,0:T(8,128)(2,1)S(1)}, u32[]{:S(2)}, u32[]{:S(2)}) collective-permute-start(bf16[24,1280]{1,0:T(8,128)(2,1)S(1)} %get-tuple-element.48), channel_id=1, source_target_pairs={{0,4},{1,5},{2,6},{3,7},{4,8},{5,9},{6,10},{7,11},{8,12},{9,13},{1... | collective-permute-start | bytes 184328 | tf_op jit(solution)/shard_map/ppermute | solution.py:18
  44.0 10.2 %collective-permute-start.14 = (bf16[24,1280]{1,0:T(8,128)(2,1)S(1)}, bf16[24,1280]{1,0:T(8,128)(2,1)S(1)}, u32[]{:S(2)}, u32[]{:S(2)}) collective-permute-start(bf16[24,1280]{1,0:T(8,128)(2,1)S(1)} %get-tuple-element.49), channel_id=1, source_target_pairs={{0,12},{1,13},{2,14},{3,15},{4,0},{5,1},{6,2},{7,3},{8,4},{9,5},{1... | collective-permute-start | bytes 184328 | tf_op jit(solution)/shard_map/ppermute | solution.py:18
  71.9 12.9 %collective-permute-start.18 = (bf16[4,24,2048]{2,1,0:T(8,128)(2,1)S(1)}, bf16[4,24,2048]{2,1,0:T(8,128)(2,1)S(1)}, u32[]{:S(2)}, u32[]{:S(2)}) collective-permute-start(bf16[4,24,2048]{2,1,0:T(8,128)(2,1)S(1)} %get-tuple-element.44), channel_id=1, source_target_pairs={{0,1},{1,2},{2,3},{3,0},{4,5},{5,6},{6,7},{7,4},{8,9},{9,10},{10,1... | collective-permute-start | bytes 1179656 | tf_op jit(solution)/shard_map/ppermute | solution.py:18
  73.3 11.5 %collective-permute-start.20 = (bf16[4,24,2048]{2,1,0:T(8,128)(2,1)S(1)}, bf16[4,24,2048]{2,1,0:T(8,128)(2,1)S(1)}, u32[]{:S(2)}, u32[]{:S(2)}) collective-permute-start(bf16[4,24,2048]{2,1,0:T(8,128)(2,1)S(1)} %get-tuple-element.44), channel_id=1, source_target_pairs={{0,3},{1,0},{2,1},{3,2},{4,7},{5,4},{6,5},{7,6},{8,11},{9,8},{10,9... | collective-permute-start | bytes 1179656 | tf_op jit(solution)/shard_map/ppermute | solution.py:18
  123.3 15.0 %collective-permute-start.34 = (bf16[4,24,1280]{2,1,0:T(8,128)(2,1)}, bf16[4,24,1280]{2,1,0:T(8,128)(2,1)}, u32[]{:S(2)}, u32[]{:S(2)}) collective-permute-start(bf16[4,24,1280]{2,1,0:T(8,128)(2,1)} %get-tuple-element.23), channel_id=1, source_target_pairs={{0,1},{1,2},{2,3},{3,0},{4,5},{5,6},{6,7},{7,4},{8,9},{9,10},{10,1... | collective-permute-start | bytes 737288 | tf_op jit(solution)/shard_map/ppermute | solution.py:18
  123.6 15.6 %collective-permute-start.36 = (bf16[4,24,1280]{2,1,0:T(8,128)(2,1)}, bf16[4,24,1280]{2,1,0:T(8,128)(2,1)}, u32[]{:S(2)}, u32[]{:S(2)}) collective-permute-start(bf16[4,24,1280]{2,1,0:T(8,128)(2,1)} %get-tuple-element.24), channel_id=1, source_target_pairs={{0,3},{1,0},{2,1},{3,2},{4,7},{5,4},{6,5},{7,6},{8,11},{9,8},{10,9... | collective-permute-start | bytes 737288 | tf_op jit(solution)/shard_map/ppermute | solution.py:18
  126.6 12.6 %collective-permute-start.35 = (bf16[4,24,1280]{2,1,0:T(8,128)(2,1)}, bf16[4,24,1280]{2,1,0:T(8,128)(2,1)}, u32[]{:S(2)}, u32[]{:S(2)}) collective-permute-start(bf16[4,24,1280]{2,1,0:T(8,128)(2,1)} %get-tuple-element.25), channel_id=1, source_target_pairs={{0,2},{1,3},{2,0},{3,1},{4,6},{5,7},{6,4},{7,5},{8,10},{9,11},{10,... | collective-permute-start | bytes 737288 | tf_op jit(solution)/shard_map/ppermute | solution.py:18
  132.3 11.9 %collective-permute-start.28 = (bf16[4,24,1282]{2,1,0:T(8,128)(2,1)S(1)}, bf16[4,24,1282]{2,1,0:T(8,128)(2,1)S(1)}, u32[]{:S(2)}, u32[]{:S(2)}) collective-permute-start(bf16[4,24,1282]{2,1,0:T(8,128)(2,1)S(1)} %get-tuple-element.17), channel_id=1, source_target_pairs={{0,4},{1,5},{2,6},{3,7},{4,8},{5,9},{6,10},{7,11},{8,12},{9,13},{1... | collective-permute-start | bytes 738440 | tf_op jit(solution)/shard_map/ppermute | solution.py:18
  132.6 16.2 %collective-permute-start.30 = (bf16[4,24,1282]{2,1,0:T(8,128)(2,1)S(1)}, bf16[4,24,1282]{2,1,0:T(8,128)(2,1)S(1)}, u32[]{:S(2)}, u32[]{:S(2)}) collective-permute-start(bf16[4,24,1282]{2,1,0:T(8,128)(2,1)S(1)} %get-tuple-element.18), channel_id=1, source_target_pairs={{0,12},{1,13},{2,14},{3,15},{4,0},{5,1},{6,2},{7,3},{8,4},{9,5},{1... | collective-permute-start | bytes 738440 | tf_op jit(solution)/shard_map/ppermute | solution.py:18
  138.4 10.8 %collective-permute-start.29 = (bf16[4,24,1282]{2,1,0:T(8,128)(2,1)S(1)}, bf16[4,24,1282]{2,1,0:T(8,128)(2,1)S(1)}, u32[]{:S(2)}, u32[]{:S(2)}) collective-permute-start(bf16[4,24,1282]{2,1,0:T(8,128)(2,1)S(1)} %get-tuple-element.19), channel_id=1, source_target_pairs={{0,8},{1,9},{2,10},{3,11},{4,12},{5,13},{6,14},{7,15},{8,0},{9,1},... | collective-permute-start | bytes 738440 | tf_op jit(solution)/shard_map/ppermute | solution.py:18
  140.7 12.0 %collective-permute-start.37 = (bf16[24,1280]{1,0:T(8,128)(2,1)S(1)}, bf16[24,1280]{1,0:T(8,128)(2,1)S(1)}, u32[]{:S(2)}, u32[]{:S(2)}) collective-permute-start(bf16[24,1280]{1,0:T(8,128)(2,1)S(1)} %get-tuple-element.45), channel_id=1, source_target_pairs={{0,4},{1,5},{2,6},{3,7},{4,8},{5,9},{6,10},{7,11},{8,12},{9,13},{1... | collective-permute-start | bytes 184328 | tf_op jit(solution)/shard_map/ppermute | solution.py:18
  141.0 12.8 %collective-permute-start.39 = (bf16[24,1280]{1,0:T(8,128)(2,1)S(1)}, bf16[24,1280]{1,0:T(8,128)(2,1)S(1)}, u32[]{:S(2)}, u32[]{:S(2)}) collective-permute-start(bf16[24,1280]{1,0:T(8,128)(2,1)S(1)} %get-tuple-element.46), channel_id=1, source_target_pairs={{0,12},{1,13},{2,14},{3,15},{4,0},{5,1},{6,2},{7,3},{8,4},{9,5},{1... | collective-permute-start | bytes 184328 | tf_op jit(solution)/shard_map/ppermute | solution.py:18
  172.2 10.8 %collective-permute-start.44 = (bf16[4,24,2048]{2,1,0:T(8,128)(2,1)}, bf16[4,24,2048]{2,1,0:T(8,128)(2,1)}, u32[]{:S(2)}, u32[]{:S(2)}) collective-permute-start(bf16[4,24,2048]{2,1,0:T(8,128)(2,1)} %get-tuple-element.42), channel_id=1, source_target_pairs={{0,2},{1,3},{2,0},{3,1},{4,6},{5,7},{6,4},{7,5},{8,10},{9,11},{10,... | collective-permute-start | bytes 1179656 | tf_op jit(solution)/shard_map/ppermute | solution.py:18
  173.6 13.5 %collective-permute-start.43 = (bf16[4,24,2048]{2,1,0:T(8,128)(2,1)}, bf16[4,24,2048]{2,1,0:T(8,128)(2,1)}, u32[]{:S(2)}, u32[]{:S(2)}) collective-permute-start(bf16[4,24,2048]{2,1,0:T(8,128)(2,1)} %get-tuple-element.42), channel_id=1, source_target_pairs={{0,1},{1,2},{2,3},{3,0},{4,5},{5,6},{6,7},{7,4},{8,9},{9,10},{10,1... | collective-permute-start | bytes 1179656 | tf_op jit(solution)/shard_map/ppermute | solution.py:18
  174.2 12.8 %collective-permute-start.45 = (bf16[4,24,2048]{2,1,0:T(8,128)(2,1)}, bf16[4,24,2048]{2,1,0:T(8,128)(2,1)}, u32[]{:S(2)}, u32[]{:S(2)}) collective-permute-start(bf16[4,24,2048]{2,1,0:T(8,128)(2,1)} %get-tuple-element.42), channel_id=1, source_target_pairs={{0,3},{1,0},{2,1},{3,2},{4,7},{5,4},{6,5},{7,6},{8,11},{9,8},{10,9... | collective-permute-start | bytes 1179656 | tf_op jit(solution)/shard_map/ppermute | solution.py:18
  (49 other events, 366.2 us)

commit v5 on v3

--- a/solution.py
+++ b/solution.py
@@ -51,6 +51,15 @@
     devices = range(lax.axis_size(axis))
     route = [(i - distance, i) for i in devices if i - distance in devices]
     return lax.ppermute(block, axis, route)
+
+
+def handed_on(x, step):
+    n = lax.axis_size("tensor")
+    outs = []
+    for k in range(n):
+        pairs = [(step * n + t, (step + 1) * n + (t + k) % n) for t in range(n)]
+        outs.append(lax.ppermute(x, ("segment", "tensor"), pairs))
+    return jnp.stack(outs)
 
 
 def shards(
@@ -117,7 +126,7 @@
         shift_z = (z_pos - b // n_y) % n_z
         return (shift_y * n_z + shift_z) * own_rows + s % own_rows
 
-    def layer(x_sorted, last):
+    def layer(x_sorted):
         xf = x_sorted.astype(f32)
         sq = jnp.sum(xf * xf, axis=1, keepdims=True)
         sq_hi = sq.astype(bf16)
@@ -164,26 +173,13 @@
         gathered = by_zy.reshape(-1, query_cols)
         partial = jnp.dot(gathered, w_out[0], preferred_element_type=f32).astype(bf16)
         ext_new = jnp.where(keep[:, None, :, None], fresh, jnp.zeros_like(fresh))
-        if last:
-            natural = jnp.take(partial, arrived_at(back_index), axis=0)
-            pieces = natural.reshape(rounds, n_tensor, rows_local, width_local).transpose(1, 0, 2, 3)
-            mine = sum(r.astype(f32) for r in spread(pieces, tensor, along_tensor))
-            x_own = jnp.take(xf, own_index, axis=0).reshape(rounds, rows_local, width_local)
-            return None, (x_own + mine).astype(bf16), ext_new
-        quarter = partial.shape[0] // n_tensor
-        in_order = jnp.take(partial, arrived_at(jnp.arange(partial.shape[0])), axis=0)
-        pieces = in_order.reshape(n_tensor, quarter, width_local)
+        natural = jnp.take(partial, arrived_at(back_index), axis=0)
+        pieces = natural.reshape(rounds, n_tensor, rows_local, width_local).transpose(1, 0, 2, 3)
         mine = sum(r.astype(f32) for r in spread(pieces, tensor, along_tensor))
-        x_mine = lax.dynamic_index_in_dim(
-            xf.reshape(n_tensor, quarter, width_local), tensor, 0, keepdims=False
-        )
-        x_mine = (x_mine + mine).astype(bf16)
-        x_new = gather_from(x_mine, tensor, n_tensor, along_tensor).reshape(-1, width_local)
-        rec_new = jnp.take(x_new, own_index, axis=0).reshape(rounds, rows_local, width_local)
-        return x_new, rec_new, ext_new
+        x_own = jnp.take(xf, own_index, axis=0).reshape(rounds, rows_local, width_local)
+        return (x_own + mine).astype(bf16), ext_new
 
     arrived = jnp.stack([hidden] + [along_tensor(hidden, k) for k in range(1, n_tensor)])
-    arrived = arrived.reshape(-1, width_local)
     src_t = inverse // req_local
     shift_t = (tensor - src_t) % n_tensor
     within = (inverse % req_local) * DRAFT_BLOCK
@@ -192,11 +188,11 @@
         + within[:, None, None]
         + jj[None, None, :]
     ).reshape(-1)
-    x = jnp.take(arrived, arrival_index, axis=0)
     record = None
     ext = None
     for step in range(n_segment):
-        x_new, rec_new, ext_new = layer(x, step + 1 == n_segment)
+        x = jnp.take(arrived.reshape(-1, width_local), arrival_index, axis=0)
+        rec_new, ext_new = layer(x)
         if step == 0:
             record, ext = rec_new, ext_new
         else:
@@ -204,7 +200,7 @@
             record = jnp.where(active, rec_new, record)
             ext = jnp.where(active, ext_new, ext)
         if step + 1 < n_segment:
-            x = passed_along(x_new, "segment", 1)
+            arrived = handed_on(rec_new, step)
     return (record[None], ext[None])
 
 

time: 207 us -> 224 us (1.082)
  waiting for transfers between devices: 72.1 us -> 90.4 us
  starting transfers between devices: 72.3 us -> 65.3 us
  other arithmetic: 16.5 us -> 19.2 us
    ppermute x48 -> x45, waiting for transfers between devices: 71.7 us -> 87.7 us  [shifted(): return lax.ppermute(x, axis, [(i, fn(i, n)) for i in range(n)])]
    ppermute x48 -> x45, starting transfers between devices: 71 us -> 59 us  [shifted(): return lax.ppermute(x, axis, [(i, fn(i, n)) for i in range(n)])]
    ppermute x1 -> x4, starting transfers between devices: 1.34 us -> 6.3 us  [handed_on(): outs.append(lax.ppermute(x, ('segment', 'tensor'), pairs))]
    ppermute x1 -> x4, waiting for transfers between devices: 0.39 us -> 2.68 us  [handed_on(): outs.append(lax.ppermute(x, ('segment', 'tensor'), pairs))]
    gather x4 -> x2, local copies, waits for them, and re-layouts: 6.2 us -> 4.14 us  [shards(): x = jnp.take(arrived.reshape(-1, width_local), arrival_index, axis=0)]
  transfers between devices with their start and end apart: 49 -> 49, of which waited for: 31 -> 32; matrix products, arithmetic and copies ran while one was open for 12% -> 10% of each run, Pallas kernels for 0% -> 0%
where the time goes in v5:
time: 224 us; the launch traced here: 222 us
  waiting for transfers between devices  90.4 us (40%)
  starting transfers between devices  65.3 us (29%)
  local copies, waits for them, and re-layouts  25.1 us (11%)
  matrix products  20.5 us (9%)
  other arithmetic  19.2 us (9%)
    ppermute x45, waiting for transfers between devices, shifted(): return lax.ppermute(x, axis, [(i, fn(i, n)) for i in range(n)])  87.7 us
    ppermute x45, starting transfers between devices, shifted(): return lax.ppermute(x, axis, [(i, fn(i, n)) for i in range(n)])  59 us
    dot_general x2, matrix products, layer(): jnp.dot(gathered, w_out[0], preferred_element_type=f32).astype(bf16)  7.98 us
    ppermute x4, starting transfers between devices, handed_on(): outs.append(lax.ppermute(x, ('segment', 'tensor'), pairs))  6.3 us
    dot_general x2, matrix products, layer(): rest = jnp.dot(xg, w_query[0, :, cut:], preferred_element_type=f32)  5.46 us
    another operation x4, other arithmetic, layer(): by_zy = jnp.stack([by_z] + [along_y(by_z, k) for k in range(1, n_y)])  4.77 us
  transfers between devices with their start and end apart: 49, of which 32 were waited for; matrix products, arithmetic and copies ran while one was open for 10% of the time, Pallas kernels for 0%

profile of v5, /device:TPU:0, one launch (start us, length us, event | category | flops | bytes accessed | tf_op | source)
XLA Modules:
  0.0 222.2 jit_solution(9010749871589036260)
XLA Ops:
  0.7 2.9 %collective-permute-start.2 = (bf16[3,32,1024]{2,1,0:T(8,128)(2,1)}, bf16[3,32,1024]{2,1,0:T(8,128)(2,1)S(1)}, u32[]{:S(2)}, u32[]{:S(2)}) collective-permute-start(bf16[3,32,1024]{2,1,0:T(8,128)(2,1)} %param.12), channel_id=1, source_target_pairs={{0,48},{16,0},{32,16},{48,32},{1,49},{17,1},{33,17},{49,33},{2,50}... | collective-permute-start | bytes 589832 | tf_op jit(solution)/shard_map/ppermute | solution.py:18
  18.5 3.2 %fusion.20 = bf16[384,768]{1,0:T(8,128)(2,1)} fusion(bf16[1,1024,2048]{2,1,0:T(8,128)(2,1)} %param.14, f32[1024]{0:T(1024)S(1)} %bitcast.303, bf16[384,1024]{1,0:T(8,128)(2,1)S(1)} %gather_fusion.2, pred[384]{0:T(512)(128)(4,1)S(1)} %get-tuple-element.66), kind=kOutput, calls=%fused_computation.32 | convolution fusion | flops 605847552 | bytes 2953600 | tf_op jit(solution)/shard_map/dot_general | solution.py:137
  26.4 3.0 %collective-permute-start.11 = (bf16[4,24,1280]{2,1,0:T(8,128)(2,1)}, bf16[4,24,1280]{2,1,0:T(8,128)(2,1)}, u32[]{:S(2)}, u32[]{:S(2)}) collective-permute-start(bf16[4,24,1280]{2,1,0:T(8,128)(2,1)} %get-tuple-element.28), channel_id=1, source_target_pairs={{0,3},{1,0},{2,1},{3,2},{4,7},{5,4},{6,5},{7,6},{8,11},{9,8},{10,9... | collective-permute-start | bytes 737288 | tf_op jit(solution)/shard_map/ppermute | solution.py:18
  33.3 4.1 %collective-permute-start.5 = (bf16[4,24,1282]{2,1,0:T(8,128)(2,1)S(1)}, bf16[4,24,1282]{2,1,0:T(8,128)(2,1)S(1)}, u32[]{:S(2)}, u32[]{:S(2)}) collective-permute-start(bf16[4,24,1282]{2,1,0:T(8,128)(2,1)S(1)} %get-tuple-element.22), channel_id=1, source_target_pairs={{0,12},{1,13},{2,14},{3,15},{4,0},{5,1},{6,2},{7,3},{8,4},{9,5},{1... | collective-permute-start | bytes 738440 | tf_op jit(solution)/shard_map/ppermute | solution.py:18
  37.4 3.0 %collective-permute-done.11 = bf16[4,24,1280]{2,1,0:T(8,128)(2,1)} collective-permute-done((bf16[4,24,1280]{2,1,0:T(8,128)(2,1)}, bf16[4,24,1280]{2,1,0:T(8,128)(2,1)}, u32[]{:S(2)}, u32[]{:S(2)}) %collective-permute-start.11) | collective-permute-done | bytes 245792 | tf_op jit(solution)/shard_map/ppermute | solution.py:18
  45.5 4.1 %collective-permute-start.14 = (bf16[24,1280]{1,0:T(8,128)(2,1)S(1)}, bf16[24,1280]{1,0:T(8,128)(2,1)S(1)}, u32[]{:S(2)}, u32[]{:S(2)}) collective-permute-start(bf16[24,1280]{1,0:T(8,128)(2,1)S(1)} %get-tuple-element.50), channel_id=1, source_target_pairs={{0,12},{1,13},{2,14},{3,15},{4,0},{5,1},{6,2},{7,3},{8,4},{9,5},{1... | collective-permute-start | bytes 184328 | tf_op jit(solution)/shard_map/ppermute | solution.py:18
  52.1 3.6 %collective-permute-start.8 = (f32[24,1282]{1,0:T(8,128)S(1)}, f32[24,1282]{1,0:T(8,128)S(1)}, u32[]{:S(2)}, u32[]{:S(2)}) collective-permute-start(f32[24,1282]{1,0:T(8,128)S(1)} %get-tuple-element.40), channel_id=1, source_target_pairs={{0,3},{1,0},{2,1},{3,2},{4,7},{5,4},{6,5},{7,6},{8,11},{9,8},{10,9... | collective-permute-start | bytes 369224 | tf_op jit(solution)/shard_map/ppermute | solution.py:18
  57.0 3.6 %collective-permute-done.8 = f32[24,1282]{1,0:T(8,128)S(1)} collective-permute-done((f32[24,1282]{1,0:T(8,128)S(1)}, f32[24,1282]{1,0:T(8,128)S(1)}, u32[]{:S(2)}, u32[]{:S(2)}) %collective-permute-start.8) | collective-permute-done | bytes 123104 | tf_op jit(solution)/shard_map/ppermute | solution.py:18
  70.3 2.8 %collective-permute-done.16 = bf16[24,2048]{1,0:T(8,128)(2,1)S(1)} collective-permute-done((bf16[24,2048]{1,0:T(8,128)(2,1)S(1)}, bf16[24,2048]{1,0:T(8,128)(2,1)S(1)}, u32[]{:S(2)}, u32[]{:S(2)}) %collective-permute-start.16) | collective-permute-done | bytes 98336 | tf_op jit(solution)/shard_map/ppermute | solution.py:18
  78.8 6.9 %collective-permute-done.20 = bf16[4,24,2048]{2,1,0:T(8,128)(2,1)} collective-permute-done((bf16[4,24,2048]{2,1,0:T(8,128)(2,1)}, bf16[4,24,2048]{2,1,0:T(8,128)(2,1)}, u32[]{:S(2)}, u32[]{:S(2)}) %collective-permute-start.20) | collective-permute-done | bytes 393248 | tf_op jit(solution)/shard_map/ppermute | solution.py:18
  85.7 2.6 %collective-permute-done.19 = bf16[4,24,2048]{2,1,0:T(8,128)(2,1)} collective-permute-done((bf16[4,24,2048]{2,1,0:T(8,128)(2,1)}, bf16[4,24,2048]{2,1,0:T(8,128)(2,1)}, u32[]{:S(2)}, u32[]{:S(2)}) %collective-permute-start.19) | collective-permute-done | bytes 393248 | tf_op jit(solution)/shard_map/ppermute | solution.py:18
  88.3 4.1 %collective-permute-done.18 = bf16[4,24,2048]{2,1,0:T(8,128)(2,1)} collective-permute-done((bf16[4,24,2048]{2,1,0:T(8,128)(2,1)}, bf16[4,24,2048]{2,1,0:T(8,128)(2,1)}, u32[]{:S(2)}, u32[]{:S(2)}) %collective-permute-start.18) | collective-permute-done | bytes 393248 | tf_op jit(solution)/shard_map/ppermute | solution.py:18
  93.8 4.0 %fusion.12 = bf16[384,1024]{1,0:T(8,128)(2,1)S(1)} fusion(bf16[384,2048]{1,0:T(8,128)(2,1)S(1)} %bitcast.266, bf16[1,2048,1024]{2,1,0:T(8,128)(2,1)} %param.16), kind=kOutput, calls=%fused_computation.28 | convolution fusion | flops 1611005952 | bytes 6553600 | tf_op jit(solution)/shard_map/dot_general | solution.py:174
  102.5 4.8 %collective-permute-done.23 = bf16[3,32,1024]{2,1,0:T(8,128)(2,1)S(1)} collective-permute-done((bf16[3,32,1024]{2,1,0:T(8,128)(2,1)S(1)}, bf16[3,32,1024]{2,1,0:T(8,128)(2,1)S(1)}, u32[]{:S(2)}, u32[]{:S(2)}) %collective-permute-start.23) | collective-permute-done | bytes 196640 | tf_op jit(solution)/shard_map/ppermute | solution.py:18
  113.0 2.4 %collective-permute-start.26 = (bf16[3,32,1024]{2,1,0:T(8,128)(2,1)S(1)}, bf16[3,32,1024]{2,1,0:T(8,128)(2,1)S(1)}, u32[]{:S(2)}, u32[]{:S(2)}) collective-permute-start(bf16[3,32,1024]{2,1,0:T(8,128)(2,1)S(1)} %fusion.57), channel_id=1, source_target_pairs={{0,96},{16,112},{32,64},{48,80},{1,97},{17,113},{33,65},{49,81},{2... | collective-permute-start | bytes 589832 | tf_op jit(solution)/shard_map/ppermute | solution.py:61
  131.5 3.1 %collective-permute-start.35 = (bf16[4,24,1280]{2,1,0:T(8,128)(2,1)}, bf16[4,24,1280]{2,1,0:T(8,128)(2,1)}, u32[]{:S(2)}, u32[]{:S(2)}) collective-permute-start(bf16[4,24,1280]{2,1,0:T(8,128)(2,1)} %get-tuple-element.26), channel_id=1, source_target_pairs={{0,2},{1,3},{2,0},{3,1},{4,6},{5,7},{6,4},{7,5},{8,10},{9,11},{10,... | collective-permute-start | bytes 737288 | tf_op jit(solution)/shard_map/ppermute | solution.py:18
  141.6 5.8 %collective-permute-done.34 = bf16[4,24,1280]{2,1,0:T(8,128)(2,1)} collective-permute-done((bf16[4,24,1280]{2,1,0:T(8,128)(2,1)}, bf16[4,24,1280]{2,1,0:T(8,128)(2,1)}, u32[]{:S(2)}, u32[]{:S(2)}) %collective-permute-start.34) | collective-permute-done | bytes 245792 | tf_op jit(solution)/shard_map/ppermute | solution.py:18
  160.0 4.7 %collective-permute-done.33 = f32[24,1282]{1,0:T(8,128)S(1)} collective-permute-done((f32[24,1282]{1,0:T(8,128)S(1)}, f32[24,1282]{1,0:T(8,128)S(1)}, u32[]{:S(2)}, u32[]{:S(2)}) %collective-permute-start.33) | collective-permute-done | bytes 123104 | tf_op jit(solution)/shard_map/ppermute | solution.py:18
  184.7 7.2 %collective-permute-done.45 = bf16[4,24,2048]{2,1,0:T(8,128)(2,1)} collective-permute-done((bf16[4,24,2048]{2,1,0:T(8,128)(2,1)}, bf16[4,24,2048]{2,1,0:T(8,128)(2,1)}, u32[]{:S(2)}, u32[]{:S(2)}) %collective-permute-start.45) | collective-permute-done | bytes 393248 | tf_op jit(solution)/shard_map/ppermute | solution.py:18
  193.9 6.3 %collective-permute-done.43 = bf16[4,24,2048]{2,1,0:T(8,128)(2,1)} collective-permute-done((bf16[4,24,2048]{2,1,0:T(8,128)(2,1)}, bf16[4,24,2048]{2,1,0:T(8,128)(2,1)}, u32[]{:S(2)}, u32[]{:S(2)}) %collective-permute-start.43) | collective-permute-done | bytes 393248 | tf_op jit(solution)/shard_map/ppermute | solution.py:18
  201.6 4.0 %fusion.15 = bf16[384,1024]{1,0:T(8,128)(2,1)S(1)} fusion(bf16[384,2048]{1,0:T(8,128)(2,1)S(1)} %bitcast.267, bf16[1,2048,1024]{2,1,0:T(8,128)(2,1)} %param.16), kind=kOutput, calls=%fused_computation.29 | convolution fusion | flops 1611005952 | bytes 6553600 | tf_op jit(solution)/shard_map/dot_general | solution.py:174
  212.0 3.8 %collective-permute-done.48 = bf16[3,32,1024]{2,1,0:T(8,128)(2,1)S(1)} collective-permute-done((bf16[3,32,1024]{2,1,0:T(8,128)(2,1)S(1)}, bf16[3,32,1024]{2,1,0:T(8,128)(2,1)S(1)}, u32[]{:S(2)}, u32[]{:S(2)}) %collective-permute-start.48) | collective-permute-done | bytes 196640 | tf_op jit(solution)/shard_map/ppermute | solution.py:18
  215.8 2.6 %collective-permute-done.47 = bf16[3,32,1024]{2,1,0:T(8,128)(2,1)S(1)} collective-permute-done((bf16[3,32,1024]{2,1,0:T(8,128)(2,1)S(1)}, bf16[3,32,1024]{2,1,0:T(8,128)(2,1)S(1)}, u32[]{:S(2)}, u32[]{:S(2)}) %collective-permute-start.47) | collective-permute-done | bytes 196640 | tf_op jit(solution)/shard_map/ppermute | solution.py:18
  218.4 3.0 %collective-permute-done.46 = bf16[3,32,1024]{2,1,0:T(8,128)(2,1)S(1)} collective-permute-done((bf16[3,32,1024]{2,1,0:T(8,128)(2,1)S(1)}, bf16[3,32,1024]{2,1,0:T(8,128)(2,1)S(1)}, u32[]{:S(2)}, u32[]{:S(2)}) %collective-permute-start.46) | collective-permute-done | bytes 196640 | tf_op jit(solution)/shard_map/ppermute | solution.py:18
  (257 shorter events, 124.8 us)
Async XLA Ops:
  0.7 14.4 %collective-permute-start.2 = (bf16[3,32,1024]{2,1,0:T(8,128)(2,1)}, bf16[3,32,1024]{2,1,0:T(8,128)(2,1)S(1)}, u32[]{:S(2)}, u32[]{:S(2)}) collective-permute-start(bf16[3,32,1024]{2,1,0:T(8,128)(2,1)} %param.12), channel_id=1, source_target_pairs={{0,48},{16,0},{32,16},{48,32},{1,49},{17,1},{33,17},{49,33},{2,50}... | collective-permute-start | bytes 589832 | tf_op jit(solution)/shard_map/ppermute | solution.py:18
  3.6 11.4 %collective-permute-start.1 = (bf16[3,32,1024]{2,1,0:T(8,128)(2,1)}, bf16[3,32,1024]{2,1,0:T(8,128)(2,1)S(1)}, u32[]{:S(2)}, u32[]{:S(2)}) collective-permute-start(bf16[3,32,1024]{2,1,0:T(8,128)(2,1)} %param.12), channel_id=1, source_target_pairs={{0,32},{16,48},{32,0},{48,16},{1,33},{17,49},{33,1},{49,17},{2,34}... | collective-permute-start | bytes 589832 | tf_op jit(solution)/shard_map/ppermute | solution.py:18
  4.4 11.5 %collective-permute-start = (bf16[3,32,1024]{2,1,0:T(8,128)(2,1)}, bf16[3,32,1024]{2,1,0:T(8,128)(2,1)S(1)}, u32[]{:S(2)}, u32[]{:S(2)}) collective-permute-start(bf16[3,32,1024]{2,1,0:T(8,128)(2,1)} %param.12), channel_id=1, source_target_pairs={{0,16},{16,32},{32,48},{48,0},{1,17},{17,33},{33,49},{49,1},{2,18}... | collective-permute-start | bytes 589832 | tf_op jit(solution)/shard_map/ppermute | solution.py:18
  26.4 14.0 %collective-permute-start.11 = (bf16[4,24,1280]{2,1,0:T(8,128)(2,1)}, bf16[4,24,1280]{2,1,0:T(8,128)(2,1)}, u32[]{:S(2)}, u32[]{:S(2)}) collective-permute-start(bf16[4,24,1280]{2,1,0:T(8,128)(2,1)} %get-tuple-element.28), channel_id=1, source_target_pairs={{0,3},{1,0},{2,1},{3,2},{4,7},{5,4},{6,5},{7,6},{8,11},{9,8},{10,9... | collective-permute-start | bytes 737288 | tf_op jit(solution)/shard_map/ppermute | solution.py:18
  29.4 12.9 %collective-permute-start.10 = (bf16[4,24,1280]{2,1,0:T(8,128)(2,1)}, bf16[4,24,1280]{2,1,0:T(8,128)(2,1)}, u32[]{:S(2)}, u32[]{:S(2)}) collective-permute-start(bf16[4,24,1280]{2,1,0:T(8,128)(2,1)} %get-tuple-element.29), channel_id=1, source_target_pairs={{0,2},{1,3},{2,0},{3,1},{4,6},{5,7},{6,4},{7,5},{8,10},{9,11},{10,... | collective-permute-start | bytes 737288 | tf_op jit(solution)/shard_map/ppermute | solution.py:18
  30.0 14.1 %collective-permute-start.9 = (bf16[4,24,1280]{2,1,0:T(8,128)(2,1)}, bf16[4,24,1280]{2,1,0:T(8,128)(2,1)}, u32[]{:S(2)}, u32[]{:S(2)}) collective-permute-start(bf16[4,24,1280]{2,1,0:T(8,128)(2,1)} %get-tuple-element.27), channel_id=1, source_target_pairs={{0,1},{1,2},{2,3},{3,0},{4,5},{5,6},{6,7},{7,4},{8,9},{9,10},{10,1... | collective-permute-start | bytes 737288 | tf_op jit(solution)/shard_map/ppermute | solution.py:18
  33.3 16.4 %collective-permute-start.5 = (bf16[4,24,1282]{2,1,0:T(8,128)(2,1)S(1)}, bf16[4,24,1282]{2,1,0:T(8,128)(2,1)S(1)}, u32[]{:S(2)}, u32[]{:S(2)}) collective-permute-start(bf16[4,24,1282]{2,1,0:T(8,128)(2,1)S(1)} %get-tuple-element.22), channel_id=1, source_target_pairs={{0,12},{1,13},{2,14},{3,15},{4,0},{5,1},{6,2},{7,3},{8,4},{9,5},{1... | collective-permute-start | bytes 738440 | tf_op jit(solution)/shard_map/ppermute | solution.py:18
  37.4 13.5 %collective-permute-start.4 = (bf16[4,24,1282]{2,1,0:T(8,128)(2,1)S(1)}, bf16[4,24,1282]{2,1,0:T(8,128)(2,1)S(1)}, u32[]{:S(2)}, u32[]{:S(2)}) collective-permute-start(bf16[4,24,1282]{2,1,0:T(8,128)(2,1)S(1)} %get-tuple-element.23), channel_id=1, source_target_pairs={{0,8},{1,9},{2,10},{3,11},{4,12},{5,13},{6,14},{7,15},{8,0},{9,1},... | collective-permute-start | bytes 738440 | tf_op jit(solution)/shard_map/ppermute | solution.py:18
  40.3 11.6 %collective-permute-start.3 = (bf16[4,24,1282]{2,1,0:T(8,128)(2,1)S(1)}, bf16[4,24,1282]{2,1,0:T(8,128)(2,1)S(1)}, u32[]{:S(2)}, u32[]{:S(2)}) collective-permute-start(bf16[4,24,1282]{2,1,0:T(8,128)(2,1)S(1)} %get-tuple-element.21), channel_id=1, source_target_pairs={{0,4},{1,5},{2,6},{3,7},{4,8},{5,9},{6,10},{7,11},{8,12},{9,13},{1... | collective-permute-start | bytes 738440 | tf_op jit(solution)/shard_map/ppermute | solution.py:18
  45.5 11.4 %collective-permute-start.14 = (bf16[24,1280]{1,0:T(8,128)(2,1)S(1)}, bf16[24,1280]{1,0:T(8,128)(2,1)S(1)}, u32[]{:S(2)}, u32[]{:S(2)}) collective-permute-start(bf16[24,1280]{1,0:T(8,128)(2,1)S(1)} %get-tuple-element.50), channel_id=1, source_target_pairs={{0,12},{1,13},{2,14},{3,15},{4,0},{5,1},{6,2},{7,3},{8,4},{9,5},{1... | collective-permute-start | bytes 184328 | tf_op jit(solution)/shard_map/ppermute | solution.py:18
  75.1 10.6 %collective-permute-start.20 = (bf16[4,24,2048]{2,1,0:T(8,128)(2,1)}, bf16[4,24,2048]{2,1,0:T(8,128)(2,1)}, u32[]{:S(2)}, u32[]{:S(2)}) collective-permute-start(bf16[4,24,2048]{2,1,0:T(8,128)(2,1)} %get-tuple-element.45), channel_id=1, source_target_pairs={{0,3},{1,0},{2,1},{3,2},{4,7},{5,4},{6,5},{7,6},{8,11},{9,8},{10,9... | collective-permute-start | bytes 1179656 | tf_op jit(solution)/shard_map/ppermute | solution.py:18
  75.7 12.6 %collective-permute-start.19 = (bf16[4,24,2048]{2,1,0:T(8,128)(2,1)}, bf16[4,24,2048]{2,1,0:T(8,128)(2,1)}, u32[]{:S(2)}, u32[]{:S(2)}) collective-permute-start(bf16[4,24,2048]{2,1,0:T(8,128)(2,1)} %get-tuple-element.45), channel_id=1, source_target_pairs={{0,2},{1,3},{2,0},{3,1},{4,6},{5,7},{6,4},{7,5},{8,10},{9,11},{10,... | collective-permute-start | bytes 1179656 | tf_op jit(solution)/shard_map/ppermute | solution.py:18
  77.0 15.3 %collective-permute-start.18 = (bf16[4,24,2048]{2,1,0:T(8,128)(2,1)}, bf16[4,24,2048]{2,1,0:T(8,128)(2,1)}, u32[]{:S(2)}, u32[]{:S(2)}) collective-permute-start(bf16[4,24,2048]{2,1,0:T(8,128)(2,1)} %get-tuple-element.45), channel_id=1, source_target_pairs={{0,1},{1,2},{2,3},{3,0},{4,5},{5,6},{6,7},{7,4},{8,9},{9,10},{10,1... | collective-permute-start | bytes 1179656 | tf_op jit(solution)/shard_map/ppermute | solution.py:18
  131.5 9.8 %collective-permute-start.36 = (bf16[4,24,1280]{2,1,0:T(8,128)(2,1)}, bf16[4,24,1280]{2,1,0:T(8,128)(2,1)}, u32[]{:S(2)}, u32[]{:S(2)}) collective-permute-start(bf16[4,24,1280]{2,1,0:T(8,128)(2,1)} %get-tuple-element.25), channel_id=1, source_target_pairs={{0,3},{1,0},{2,1},{3,2},{4,7},{5,4},{6,5},{7,6},{8,11},{9,8},{10,9... | collective-permute-start | bytes 737288 | tf_op jit(solution)/shard_map/ppermute | solution.py:18
  131.5 10.1 %collective-permute-start.35 = (bf16[4,24,1280]{2,1,0:T(8,128)(2,1)}, bf16[4,24,1280]{2,1,0:T(8,128)(2,1)}, u32[]{:S(2)}, u32[]{:S(2)}) collective-permute-start(bf16[4,24,1280]{2,1,0:T(8,128)(2,1)} %get-tuple-element.26), channel_id=1, source_target_pairs={{0,2},{1,3},{2,0},{3,1},{4,6},{5,7},{6,4},{7,5},{8,10},{9,11},{10,... | collective-permute-start | bytes 737288 | tf_op jit(solution)/shard_map/ppermute | solution.py:18
  134.6 12.8 %collective-permute-start.34 = (bf16[4,24,1280]{2,1,0:T(8,128)(2,1)}, bf16[4,24,1280]{2,1,0:T(8,128)(2,1)}, u32[]{:S(2)}, u32[]{:S(2)}) collective-permute-start(bf16[4,24,1280]{2,1,0:T(8,128)(2,1)} %get-tuple-element.24), channel_id=1, source_target_pairs={{0,1},{1,2},{2,3},{3,0},{4,5},{5,6},{6,7},{7,4},{8,9},{9,10},{10,1... | collective-permute-start | bytes 737288 | tf_op jit(solution)/shard_map/ppermute | solution.py:18
  138.2 14.8 %collective-permute-start.30 = (bf16[4,24,1282]{2,1,0:T(8,128)(2,1)S(1)}, bf16[4,24,1282]{2,1,0:T(8,128)(2,1)S(1)}, u32[]{:S(2)}, u32[]{:S(2)}) collective-permute-start(bf16[4,24,1282]{2,1,0:T(8,128)(2,1)S(1)} %get-tuple-element.19), channel_id=1, source_target_pairs={{0,12},{1,13},{2,14},{3,15},{4,0},{5,1},{6,2},{7,3},{8,4},{9,5},{1... | collective-permute-start | bytes 738440 | tf_op jit(solution)/shard_map/ppermute | solution.py:18
  139.8 14.3 %collective-permute-start.29 = (bf16[4,24,1282]{2,1,0:T(8,128)(2,1)S(1)}, bf16[4,24,1282]{2,1,0:T(8,128)(2,1)S(1)}, u32[]{:S(2)}, u32[]{:S(2)}) collective-permute-start(bf16[4,24,1282]{2,1,0:T(8,128)(2,1)S(1)} %get-tuple-element.20), channel_id=1, source_target_pairs={{0,8},{1,9},{2,10},{3,11},{4,12},{5,13},{6,14},{7,15},{8,0},{9,1},... | collective-permute-start | bytes 738440 | tf_op jit(solution)/shard_map/ppermute | solution.py:18
  141.3 15.2 %collective-permute-start.28 = (bf16[4,24,1282]{2,1,0:T(8,128)(2,1)S(1)}, bf16[4,24,1282]{2,1,0:T(8,128)(2,1)S(1)}, u32[]{:S(2)}, u32[]{:S(2)}) collective-permute-start(bf16[4,24,1282]{2,1,0:T(8,128)(2,1)S(1)} %get-tuple-element.18), channel_id=1, source_target_pairs={{0,4},{1,5},{2,6},{3,7},{4,8},{5,9},{6,10},{7,11},{8,12},{9,13},{1... | collective-permute-start | bytes 738440 | tf_op jit(solution)/shard_map/ppermute | solution.py:18
  148.9 10.0 %collective-permute-start.39 = (bf16[24,1280]{1,0:T(8,128)(2,1)S(1)}, bf16[24,1280]{1,0:T(8,128)(2,1)S(1)}, u32[]{:S(2)}, u32[]{:S(2)}) collective-permute-start(bf16[24,1280]{1,0:T(8,128)(2,1)S(1)} %get-tuple-element.47), channel_id=1, source_target_pairs={{0,12},{1,13},{2,14},{3,15},{4,0},{5,1},{6,2},{7,3},{8,4},{9,5},{1... | collective-permute-start | bytes 184328 | tf_op jit(solution)/shard_map/ppermute | solution.py:18
  179.6 12.3 %collective-permute-start.45 = (bf16[4,24,2048]{2,1,0:T(8,128)(2,1)}, bf16[4,24,2048]{2,1,0:T(8,128)(2,1)}, u32[]{:S(2)}, u32[]{:S(2)}) collective-permute-start(bf16[4,24,2048]{2,1,0:T(8,128)(2,1)} %get-tuple-element.43), channel_id=1, source_target_pairs={{0,3},{1,0},{2,1},{3,2},{4,7},{5,4},{6,5},{7,6},{8,11},{9,8},{10,9... | collective-permute-start | bytes 1179656 | tf_op jit(solution)/shard_map/ppermute | solution.py:18
  180.1 13.9 %collective-permute-start.44 = (bf16[4,24,2048]{2,1,0:T(8,128)(2,1)}, bf16[4,24,2048]{2,1,0:T(8,128)(2,1)}, u32[]{:S(2)}, u32[]{:S(2)}) collective-permute-start(bf16[4,24,2048]{2,1,0:T(8,128)(2,1)} %get-tuple-element.43), channel_id=1, source_target_pairs={{0,2},{1,3},{2,0},{3,1},{4,6},{5,7},{6,4},{7,5},{8,10},{9,11},{10,... | collective-permute-start | bytes 1179656 | tf_op jit(solution)/shard_map/ppermute | solution.py:18
  180.4 19.8 %collective-permute-start.43 = (bf16[4,24,2048]{2,1,0:T(8,128)(2,1)}, bf16[4,24,2048]{2,1,0:T(8,128)(2,1)}, u32[]{:S(2)}, u32[]{:S(2)}) collective-permute-start(bf16[4,24,2048]{2,1,0:T(8,128)(2,1)} %get-tuple-element.43), channel_id=1, source_target_pairs={{0,1},{1,2},{2,3},{3,0},{4,5},{5,6},{6,7},{7,4},{8,9},{9,10},{10,1... | collective-permute-start | bytes 1179656 | tf_op jit(solution)/shard_map/ppermute | solution.py:18
  211.1 10.3 %collective-permute-start.46 = (bf16[3,32,1024]{2,1,0:T(8,128)(2,1)S(1)}, bf16[3,32,1024]{2,1,0:T(8,128)(2,1)S(1)}, u32[]{:S(2)}, u32[]{:S(2)}) collective-permute-start(bf16[3,32,1024]{2,1,0:T(8,128)(2,1)S(1)} %get-tuple-element.30), channel_id=1, source_target_pairs={{0,16},{16,32},{32,48},{48,0},{1,17},{17,33},{33,49},{49,1},{2,18}... | collective-permute-start | bytes 589832 | tf_op jit(solution)/shard_map/ppermute | solution.py:18
  (50 other events, 381.6 us)

commit v6 on v3

--- a/solution.py
+++ b/solution.py
@@ -131,9 +131,9 @@
         first_y = first_half.reshape(n_z, n_y, own_rows, cut).transpose(1, 0, 2, 3)
         first_z = rest.reshape(n_z, n_y, own_rows, rest.shape[1])
         part_a = sum(r.astype(f32) for r in spread(first_y, y_pos, along_y)).astype(bf16)
-        part_b = sum(r.astype(f32) for r in spread(first_z, z_pos, along_z))
+        part_b = sum(r.astype(f32) for r in spread(first_z, z_pos, along_z)).astype(bf16)
         total_a = sum(r.astype(f32) for r in spread(part_a, z_pos, along_z))
-        total_b = sum(spread(part_b, y_pos, along_y))
+        total_b = sum(r.astype(f32) for r in spread(part_b, y_pos, along_y))
         total = jnp.concatenate([total_a, total_b], axis=1)
         total_sq = total[:, query_cols + kv_cols] + total[:, query_cols + kv_cols + 1]
         inv = lax.rsqrt(total_sq / MODEL_WIDTH + 1e-05)[:, None]

time: 207 us -> 205 us (level)
  waiting for transfers between devices: 72.1 us -> 69.4 us
    ppermute x48, waiting for transfers between devices: 71.7 us -> 69 us  [shifted(): return lax.ppermute(x, axis, [(i, fn(i, n)) for i in range(n)])]
  transfers between devices with their start and end apart: 49 -> 49, of which waited for: 31 -> 29; matrix products, arithmetic and copies ran while one was open for 12% -> 12% of each run, Pallas kernels for 0% -> 0%
where the time goes in v6:
time: 205 us; the launch traced here: 204 us
  starting transfers between devices  73 us (36%)
  waiting for transfers between devices  69.4 us (34%)
  local copies, waits for them, and re-layouts  24.6 us (12%)
  matrix products  19.1 us (9%)
  other arithmetic  16.5 us (8%)
    ppermute x48, starting transfers between devices, shifted(): return lax.ppermute(x, axis, [(i, fn(i, n)) for i in range(n)])  71.7 us
    ppermute x48, waiting for transfers between devices, shifted(): return lax.ppermute(x, axis, [(i, fn(i, n)) for i in range(n)])  69 us
    dot_general x2, matrix products, layer(): jnp.dot(gathered, w_out[0], preferred_element_type=f32).astype(bf16)  5.81 us
    dot_general x2, matrix products, layer(): rest = jnp.dot(xg, w_query[0, :, cut:], preferred_element_type=f32)  4.59 us
    dot_general x2, matrix products, layer(): jnp.dot(xg, w_query[0, :, :cut], preferred_element_type=f32).astype(bf16)  4.18 us
    concatenate x2, local copies, waits for them, and re-layouts, layer(): jnp.concatenate([rest.astype(bf16), second.astype(bf16), sq_hi, sq_lo], a...  4.14 us
  transfers between devices with their start and end apart: 49, of which 29 were waited for; matrix products, arithmetic and copies ran while one was open for 12% of the time, Pallas kernels for 0%

profile of v6, /device:TPU:0, one launch (start us, length us, event | category | flops | bytes accessed | tf_op | source)
XLA Modules:
  0.0 204.1 jit_solution(4258052352211531364)
XLA Ops:
  46.2 3.5 %collective-permute-start.13 = (bf16[24,1280]{1,0:T(8,128)(2,1)S(1)}, bf16[24,1280]{1,0:T(8,128)(2,1)S(1)}, u32[]{:S(2)}, u32[]{:S(2)}) collective-permute-start(bf16[24,1280]{1,0:T(8,128)(2,1)S(1)} %get-tuple-element.50), channel_id=1, source_target_pairs={{0,8},{1,9},{2,10},{3,11},{4,12},{5,13},{6,14},{7,15},{8,0},{9,1},... | collective-permute-start | bytes 184328 | tf_op jit(solution)/shard_map/ppermute | solution.py:18
  56.2 3.2 %collective-permute-done.7 = bf16[24,1282]{1,0:T(8,128)(2,1)S(1)} collective-permute-done((bf16[24,1282]{1,0:T(8,128)(2,1)S(1)}, bf16[24,1282]{1,0:T(8,128)(2,1)S(1)}, u32[]{:S(2)}, u32[]{:S(2)}) %collective-permute-start.7) | collective-permute-done | bytes 61568 | tf_op jit(solution)/shard_map/ppermute | solution.py:18
  65.9 3.1 %collective-permute-done.16 = bf16[24,2048]{1,0:T(8,128)(2,1)S(1)} collective-permute-done((bf16[24,2048]{1,0:T(8,128)(2,1)S(1)}, bf16[24,2048]{1,0:T(8,128)(2,1)S(1)}, u32[]{:S(2)}, u32[]{:S(2)}) %collective-permute-start.16) | collective-permute-done | bytes 98336 | tf_op jit(solution)/shard_map/ppermute | solution.py:18
  71.8 2.6 %collective-permute-start.20 = (bf16[4,24,2048]{2,1,0:T(8,128)(2,1)S(1)}, bf16[4,24,2048]{2,1,0:T(8,128)(2,1)S(1)}, u32[]{:S(2)}, u32[]{:S(2)}) collective-permute-start(bf16[4,24,2048]{2,1,0:T(8,128)(2,1)S(1)} %get-tuple-element.38), channel_id=1, source_target_pairs={{0,3},{1,0},{2,1},{3,2},{4,7},{5,4},{6,5},{7,6},{8,11},{9,8},{10,9... | collective-permute-start | bytes 1179656 | tf_op jit(solution)/shard_map/ppermute | solution.py:18
  75.0 4.8 %collective-permute-done.19 = bf16[4,24,2048]{2,1,0:T(8,128)(2,1)S(1)} collective-permute-done((bf16[4,24,2048]{2,1,0:T(8,128)(2,1)S(1)}, bf16[4,24,2048]{2,1,0:T(8,128)(2,1)S(1)}, u32[]{:S(2)}, u32[]{:S(2)}) %collective-permute-start.19) | collective-permute-done | bytes 393248 | tf_op jit(solution)/shard_map/ppermute | solution.py:18
  79.9 4.1 %collective-permute-done.18 = bf16[4,24,2048]{2,1,0:T(8,128)(2,1)S(1)} collective-permute-done((bf16[4,24,2048]{2,1,0:T(8,128)(2,1)S(1)}, bf16[4,24,2048]{2,1,0:T(8,128)(2,1)S(1)}, u32[]{:S(2)}, u32[]{:S(2)}) %collective-permute-start.18) | collective-permute-done | bytes 393248 | tf_op jit(solution)/shard_map/ppermute | solution.py:18
  91.8 9.2 %collective-permute-done.21 = bf16[96,1024]{1,0:T(8,128)(2,1)S(1)} collective-permute-done((bf16[96,1024]{1,0:T(8,128)(2,1)S(1)}, bf16[96,1024]{1,0:T(8,128)(2,1)S(1)}, u32[]{:S(2)}, u32[]{:S(2)}) %collective-permute-start.21) | collective-permute-done | bytes 196640 | tf_op jit(solution)/shard_map/ppermute | solution.py:18
  106.9 3.0 %collective-permute-done.25 = bf16[96,1024]{1,0:T(8,128)(2,1)S(1)} collective-permute-done((bf16[96,1024]{1,0:T(8,128)(2,1)S(1)}, bf16[96,1024]{1,0:T(8,128)(2,1)S(1)}, u32[]{:S(2)}, u32[]{:S(2)}) %collective-permute-start.25) | collective-permute-done | bytes 196640 | tf_op jit(solution)/shard_map/ppermute | solution.py:18
  118.0 2.9 %convolution_convert_fusion = bf16[384,1280]{1,0:T(8,128)(2,1)S(1)} fusion(bf16[1,1024,2048]{2,1,0:T(8,128)(2,1)} %param.12, bf16[384,1024]{1,0:T(8,128)(2,1)S(1)} %collective-permute-done.27, f32[1024]{0:T(1024)S(1)} %bitcast.309), kind=kOutput, calls=%fused_computation.12 | convolution fusion | flops 1008304128 | bytes 4395008 | tf_op jit(solution)/shard_map/dot_general | solution.py:127
  122.2 2.9 %collective-permute-start.36 = (bf16[4,24,1280]{2,1,0:T(8,128)(2,1)}, bf16[4,24,1280]{2,1,0:T(8,128)(2,1)}, u32[]{:S(2)}, u32[]{:S(2)}) collective-permute-start(bf16[4,24,1280]{2,1,0:T(8,128)(2,1)} %get-tuple-element.24), channel_id=1, source_target_pairs={{0,3},{1,0},{2,1},{3,2},{4,7},{5,4},{6,5},{7,6},{8,11},{9,8},{10,9... | collective-permute-start | bytes 737288 | tf_op jit(solution)/shard_map/ppermute | solution.py:18
  131.2 3.0 %collective-permute-start.30 = (bf16[4,24,1282]{2,1,0:T(8,128)(2,1)S(1)}, bf16[4,24,1282]{2,1,0:T(8,128)(2,1)S(1)}, u32[]{:S(2)}, u32[]{:S(2)}) collective-permute-start(bf16[4,24,1282]{2,1,0:T(8,128)(2,1)S(1)} %get-tuple-element.18), channel_id=1, source_target_pairs={{0,12},{1,13},{2,14},{3,15},{4,0},{5,1},{6,2},{7,3},{8,4},{9,5},{1... | collective-permute-start | bytes 738440 | tf_op jit(solution)/shard_map/ppermute | solution.py:18
  134.2 2.8 %collective-permute-done.34 = bf16[4,24,1280]{2,1,0:T(8,128)(2,1)} collective-permute-done((bf16[4,24,1280]{2,1,0:T(8,128)(2,1)}, bf16[4,24,1280]{2,1,0:T(8,128)(2,1)}, u32[]{:S(2)}, u32[]{:S(2)}) %collective-permute-start.34) | collective-permute-done | bytes 245792 | tf_op jit(solution)/shard_map/ppermute | solution.py:18
  140.1 3.2 %collective-permute-start.39 = (bf16[24,1280]{1,0:T(8,128)(2,1)S(1)}, bf16[24,1280]{1,0:T(8,128)(2,1)S(1)}, u32[]{:S(2)}, u32[]{:S(2)}) collective-permute-start(bf16[24,1280]{1,0:T(8,128)(2,1)S(1)} %get-tuple-element.46), channel_id=1, source_target_pairs={{0,12},{1,13},{2,14},{3,15},{4,0},{5,1},{6,2},{7,3},{8,4},{9,5},{1... | collective-permute-start | bytes 184328 | tf_op jit(solution)/shard_map/ppermute | solution.py:18
  144.3 3.2 %collective-permute-done.30 = bf16[4,24,1282]{2,1,0:T(8,128)(2,1)S(1)} collective-permute-done((bf16[4,24,1282]{2,1,0:T(8,128)(2,1)S(1)}, bf16[4,24,1282]{2,1,0:T(8,128)(2,1)S(1)}, u32[]{:S(2)}, u32[]{:S(2)}) %collective-permute-start.30) | collective-permute-done | bytes 246176 | tf_op jit(solution)/shard_map/ppermute | solution.py:18
  148.0 3.2 %collective-permute-start.33 = (bf16[24,1282]{1,0:T(8,128)(2,1)S(1)}, bf16[24,1282]{1,0:T(8,128)(2,1)S(1)}, u32[]{:S(2)}, u32[]{:S(2)}) collective-permute-start(bf16[24,1282]{1,0:T(8,128)(2,1)S(1)} %get-tuple-element.40), channel_id=1, source_target_pairs={{0,3},{1,0},{2,1},{3,2},{4,7},{5,4},{6,5},{7,6},{8,11},{9,8},{10,9... | collective-permute-start | bytes 184616 | tf_op jit(solution)/shard_map/ppermute | solution.py:18
  154.0 3.0 %collective-permute-done.32 = bf16[24,1282]{1,0:T(8,128)(2,1)S(1)} collective-permute-done((bf16[24,1282]{1,0:T(8,128)(2,1)S(1)}, bf16[24,1282]{1,0:T(8,128)(2,1)S(1)}, u32[]{:S(2)}, u32[]{:S(2)}) %collective-permute-start.32) | collective-permute-done | bytes 61568 | tf_op jit(solution)/shard_map/ppermute | solution.py:18
  158.8 3.4 %collective-permute-start.42 = (bf16[24,2048]{1,0:T(8,128)(2,1)S(1)}, bf16[24,2048]{1,0:T(8,128)(2,1)S(1)}, u32[]{:S(2)}, u32[]{:S(2)}) collective-permute-start(bf16[24,2048]{1,0:T(8,128)(2,1)S(1)} %reshape.698), channel_id=1, source_target_pairs={{0,12},{1,13},{2,14},{3,15},{4,0},{5,1},{6,2},{7,3},{8,4},{9,5},{1... | collective-permute-start | bytes 294920 | tf_op jit(solution)/shard_map/ppermute | solution.py:18
  165.4 3.0 %collective-permute-done.41 = bf16[24,2048]{1,0:T(8,128)(2,1)S(1)} collective-permute-done((bf16[24,2048]{1,0:T(8,128)(2,1)S(1)}, bf16[24,2048]{1,0:T(8,128)(2,1)S(1)}, u32[]{:S(2)}, u32[]{:S(2)}) %collective-permute-start.41) | collective-permute-done | bytes 98336 | tf_op jit(solution)/shard_map/ppermute | solution.py:18
  171.7 3.2 %collective-permute-start.45 = (bf16[4,24,2048]{2,1,0:T(8,128)(2,1)}, bf16[4,24,2048]{2,1,0:T(8,128)(2,1)}, u32[]{:S(2)}, u32[]{:S(2)}) collective-permute-start(bf16[4,24,2048]{2,1,0:T(8,128)(2,1)} %get-tuple-element.36), channel_id=1, source_target_pairs={{0,3},{1,0},{2,1},{3,2},{4,7},{5,4},{6,5},{7,6},{8,11},{9,8},{10,9... | collective-permute-start | bytes 1179656 | tf_op jit(solution)/shard_map/ppermute | solution.py:18
  177.4 3.5 %collective-permute-done.44 = bf16[4,24,2048]{2,1,0:T(8,128)(2,1)} collective-permute-done((bf16[4,24,2048]{2,1,0:T(8,128)(2,1)}, bf16[4,24,2048]{2,1,0:T(8,128)(2,1)}, u32[]{:S(2)}, u32[]{:S(2)}) %collective-permute-start.44) | collective-permute-done | bytes 393248 | tf_op jit(solution)/shard_map/ppermute | solution.py:18
  180.9 4.1 %collective-permute-done.43 = bf16[4,24,2048]{2,1,0:T(8,128)(2,1)} collective-permute-done((bf16[4,24,2048]{2,1,0:T(8,128)(2,1)}, bf16[4,24,2048]{2,1,0:T(8,128)(2,1)}, u32[]{:S(2)}, u32[]{:S(2)}) %collective-permute-start.43) | collective-permute-done | bytes 393248 | tf_op jit(solution)/shard_map/ppermute | solution.py:18
  186.4 4.0 %fusion.15 = bf16[384,1024]{1,0:T(8,128)(2,1)S(1)} fusion(bf16[384,2048]{1,0:T(8,128)(2,1)S(1)} %bitcast.267, bf16[1,2048,1024]{2,1,0:T(8,128)(2,1)} %param.14), kind=kOutput, calls=%fused_computation.29 | convolution fusion | flops 1611005952 | bytes 6553600 | tf_op jit(solution)/shard_map/dot_general | solution.py:165
  192.8 3.2 %collective-permute-start.48 = (bf16[3,32,1024]{2,1,0:T(8,128)(2,1)S(1)}, bf16[3,32,1024]{2,1,0:T(8,128)(2,1)S(1)}, u32[]{:S(2)}, u32[]{:S(2)}) collective-permute-start(bf16[3,32,1024]{2,1,0:T(8,128)(2,1)S(1)} %get-tuple-element.30), channel_id=1, source_target_pairs={{0,48},{16,0},{32,16},{48,32},{1,49},{17,1},{33,17},{49,33},{2,50}... | collective-permute-start | bytes 589832 | tf_op jit(solution)/shard_map/ppermute | solution.py:18
  196.7 4.1 %collective-permute-done.46 = bf16[3,32,1024]{2,1,0:T(8,128)(2,1)S(1)} collective-permute-done((bf16[3,32,1024]{2,1,0:T(8,128)(2,1)S(1)}, bf16[3,32,1024]{2,1,0:T(8,128)(2,1)S(1)}, u32[]{:S(2)}, u32[]{:S(2)}) %collective-permute-start.46) | collective-permute-done | bytes 196640 | tf_op jit(solution)/shard_map/ppermute | solution.py:18
  (263 shorter events, 116.2 us)
Async XLA Ops:
  0.6 12.7 %collective-permute-start = (bf16[3,32,1024]{2,1,0:T(8,128)(2,1)}, bf16[3,32,1024]{2,1,0:T(8,128)(2,1)S(1)}, u32[]{:S(2)}, u32[]{:S(2)}) collective-permute-start(bf16[3,32,1024]{2,1,0:T(8,128)(2,1)} %param.10), channel_id=1, source_target_pairs={{0,16},{16,32},{32,48},{48,0},{1,17},{17,33},{33,49},{49,1},{2,18}... | collective-permute-start | bytes 589832 | tf_op jit(solution)/shard_map/ppermute | solution.py:18
  2.3 11.1 %collective-permute-start.2 = (bf16[3,32,1024]{2,1,0:T(8,128)(2,1)}, bf16[3,32,1024]{2,1,0:T(8,128)(2,1)S(1)}, u32[]{:S(2)}, u32[]{:S(2)}) collective-permute-start(bf16[3,32,1024]{2,1,0:T(8,128)(2,1)} %param.10), channel_id=1, source_target_pairs={{0,48},{16,0},{32,16},{48,32},{1,49},{17,1},{33,17},{49,33},{2,50}... | collective-permute-start | bytes 589832 | tf_op jit(solution)/shard_map/ppermute | solution.py:18
  25.6 11.6 %collective-permute-start.9 = (bf16[4,24,1280]{2,1,0:T(8,128)(2,1)}, bf16[4,24,1280]{2,1,0:T(8,128)(2,1)}, u32[]{:S(2)}, u32[]{:S(2)}) collective-permute-start(bf16[4,24,1280]{2,1,0:T(8,128)(2,1)} %get-tuple-element.26), channel_id=1, source_target_pairs={{0,1},{1,2},{2,3},{3,0},{4,5},{5,6},{6,7},{7,4},{8,9},{9,10},{10,1... | collective-permute-start | bytes 737288 | tf_op jit(solution)/shard_map/ppermute | solution.py:18
  27.2 11.8 %collective-permute-start.11 = (bf16[4,24,1280]{2,1,0:T(8,128)(2,1)}, bf16[4,24,1280]{2,1,0:T(8,128)(2,1)}, u32[]{:S(2)}, u32[]{:S(2)}) collective-permute-start(bf16[4,24,1280]{2,1,0:T(8,128)(2,1)} %get-tuple-element.27), channel_id=1, source_target_pairs={{0,3},{1,0},{2,1},{3,2},{4,7},{5,4},{6,5},{7,6},{8,11},{9,8},{10,9... | collective-permute-start | bytes 737288 | tf_op jit(solution)/shard_map/ppermute | solution.py:18
  28.9 11.6 %collective-permute-start.10 = (bf16[4,24,1280]{2,1,0:T(8,128)(2,1)}, bf16[4,24,1280]{2,1,0:T(8,128)(2,1)}, u32[]{:S(2)}, u32[]{:S(2)}) collective-permute-start(bf16[4,24,1280]{2,1,0:T(8,128)(2,1)} %get-tuple-element.28), channel_id=1, source_target_pairs={{0,2},{1,3},{2,0},{3,1},{4,6},{5,7},{6,4},{7,5},{8,10},{9,11},{10,... | collective-permute-start | bytes 737288 | tf_op jit(solution)/shard_map/ppermute | solution.py:18
  33.0 13.2 %collective-permute-start.3 = (bf16[4,24,1282]{2,1,0:T(8,128)(2,1)S(1)}, bf16[4,24,1282]{2,1,0:T(8,128)(2,1)S(1)}, u32[]{:S(2)}, u32[]{:S(2)}) collective-permute-start(bf16[4,24,1282]{2,1,0:T(8,128)(2,1)S(1)} %get-tuple-element.20), channel_id=1, source_target_pairs={{0,4},{1,5},{2,6},{3,7},{4,8},{5,9},{6,10},{7,11},{8,12},{9,13},{1... | collective-permute-start | bytes 738440 | tf_op jit(solution)/shard_map/ppermute | solution.py:18
  35.0 14.6 %collective-permute-start.5 = (bf16[4,24,1282]{2,1,0:T(8,128)(2,1)S(1)}, bf16[4,24,1282]{2,1,0:T(8,128)(2,1)S(1)}, u32[]{:S(2)}, u32[]{:S(2)}) collective-permute-start(bf16[4,24,1282]{2,1,0:T(8,128)(2,1)S(1)} %get-tuple-element.21), channel_id=1, source_target_pairs={{0,12},{1,13},{2,14},{3,15},{4,0},{5,1},{6,2},{7,3},{8,4},{9,5},{1... | collective-permute-start | bytes 738440 | tf_op jit(solution)/shard_map/ppermute | solution.py:18
  37.2 13.0 %collective-permute-start.4 = (bf16[4,24,1282]{2,1,0:T(8,128)(2,1)S(1)}, bf16[4,24,1282]{2,1,0:T(8,128)(2,1)S(1)}, u32[]{:S(2)}, u32[]{:S(2)}) collective-permute-start(bf16[4,24,1282]{2,1,0:T(8,128)(2,1)S(1)} %get-tuple-element.22), channel_id=1, source_target_pairs={{0,8},{1,9},{2,10},{3,11},{4,12},{5,13},{6,14},{7,15},{8,0},{9,1},... | collective-permute-start | bytes 738440 | tf_op jit(solution)/shard_map/ppermute | solution.py:18
  42.0 11.7 %collective-permute-start.12 = (bf16[24,1280]{1,0:T(8,128)(2,1)S(1)}, bf16[24,1280]{1,0:T(8,128)(2,1)S(1)}, u32[]{:S(2)}, u32[]{:S(2)}) collective-permute-start(bf16[24,1280]{1,0:T(8,128)(2,1)S(1)} %get-tuple-element.48), channel_id=1, source_target_pairs={{0,4},{1,5},{2,6},{3,7},{4,8},{5,9},{6,10},{7,11},{8,12},{9,13},{1... | collective-permute-start | bytes 184328 | tf_op jit(solution)/shard_map/ppermute | solution.py:18
  71.1 12.8 %collective-permute-start.18 = (bf16[4,24,2048]{2,1,0:T(8,128)(2,1)S(1)}, bf16[4,24,2048]{2,1,0:T(8,128)(2,1)S(1)}, u32[]{:S(2)}, u32[]{:S(2)}) collective-permute-start(bf16[4,24,2048]{2,1,0:T(8,128)(2,1)S(1)} %get-tuple-element.38), channel_id=1, source_target_pairs={{0,1},{1,2},{2,3},{3,0},{4,5},{5,6},{6,7},{7,4},{8,9},{9,10},{10,1... | collective-permute-start | bytes 1179656 | tf_op jit(solution)/shard_map/ppermute | solution.py:18
  71.8 12.2 %collective-permute-start.20 = (bf16[4,24,2048]{2,1,0:T(8,128)(2,1)S(1)}, bf16[4,24,2048]{2,1,0:T(8,128)(2,1)S(1)}, u32[]{:S(2)}, u32[]{:S(2)}) collective-permute-start(bf16[4,24,2048]{2,1,0:T(8,128)(2,1)S(1)} %get-tuple-element.38), channel_id=1, source_target_pairs={{0,3},{1,0},{2,1},{3,2},{4,7},{5,4},{6,5},{7,6},{8,11},{9,8},{10,9... | collective-permute-start | bytes 1179656 | tf_op jit(solution)/shard_map/ppermute | solution.py:18
  88.3 12.7 %collective-permute-start.21 = (bf16[96,1024]{1,0:T(8,128)(2,1)S(1)}, bf16[96,1024]{1,0:T(8,128)(2,1)S(1)}, u32[]{:S(2)}, u32[]{:S(2)}) collective-permute-start(bf16[96,1024]{1,0:T(8,128)(2,1)S(1)} %get-tuple-element.32), channel_id=1, source_target_pairs={{0,16},{16,32},{32,48},{48,0},{1,17},{17,33},{33,49},{49,1},{2,18}... | collective-permute-start | bytes 589832 | tf_op jit(solution)/shard_map/ppermute | solution.py:18
  89.4 11.7 %collective-permute-start.23 = (bf16[96,1024]{1,0:T(8,128)(2,1)S(1)}, bf16[96,1024]{1,0:T(8,128)(2,1)S(1)}, u32[]{:S(2)}, u32[]{:S(2)}) collective-permute-start(bf16[96,1024]{1,0:T(8,128)(2,1)S(1)} %get-tuple-element.33), channel_id=1, source_target_pairs={{0,48},{16,0},{32,16},{48,32},{1,49},{17,1},{33,17},{49,33},{2,50}... | collective-permute-start | bytes 589832 | tf_op jit(solution)/shard_map/ppermute | solution.py:18
  121.9 15.0 %collective-permute-start.34 = (bf16[4,24,1280]{2,1,0:T(8,128)(2,1)}, bf16[4,24,1280]{2,1,0:T(8,128)(2,1)}, u32[]{:S(2)}, u32[]{:S(2)}) collective-permute-start(bf16[4,24,1280]{2,1,0:T(8,128)(2,1)} %get-tuple-element.23), channel_id=1, source_target_pairs={{0,1},{1,2},{2,3},{3,0},{4,5},{5,6},{6,7},{7,4},{8,9},{9,10},{10,1... | collective-permute-start | bytes 737288 | tf_op jit(solution)/shard_map/ppermute | solution.py:18
  122.2 16.1 %collective-permute-start.36 = (bf16[4,24,1280]{2,1,0:T(8,128)(2,1)}, bf16[4,24,1280]{2,1,0:T(8,128)(2,1)}, u32[]{:S(2)}, u32[]{:S(2)}) collective-permute-start(bf16[4,24,1280]{2,1,0:T(8,128)(2,1)} %get-tuple-element.24), channel_id=1, source_target_pairs={{0,3},{1,0},{2,1},{3,2},{4,7},{5,4},{6,5},{7,6},{8,11},{9,8},{10,9... | collective-permute-start | bytes 737288 | tf_op jit(solution)/shard_map/ppermute | solution.py:18
  125.2 13.2 %collective-permute-start.35 = (bf16[4,24,1280]{2,1,0:T(8,128)(2,1)}, bf16[4,24,1280]{2,1,0:T(8,128)(2,1)}, u32[]{:S(2)}, u32[]{:S(2)}) collective-permute-start(bf16[4,24,1280]{2,1,0:T(8,128)(2,1)} %get-tuple-element.25), channel_id=1, source_target_pairs={{0,2},{1,3},{2,0},{3,1},{4,6},{5,7},{6,4},{7,5},{8,10},{9,11},{10,... | collective-permute-start | bytes 737288 | tf_op jit(solution)/shard_map/ppermute | solution.py:18
  130.9 12.4 %collective-permute-start.28 = (bf16[4,24,1282]{2,1,0:T(8,128)(2,1)S(1)}, bf16[4,24,1282]{2,1,0:T(8,128)(2,1)S(1)}, u32[]{:S(2)}, u32[]{:S(2)}) collective-permute-start(bf16[4,24,1282]{2,1,0:T(8,128)(2,1)S(1)} %get-tuple-element.17), channel_id=1, source_target_pairs={{0,4},{1,5},{2,6},{3,7},{4,8},{5,9},{6,10},{7,11},{8,12},{9,13},{1... | collective-permute-start | bytes 738440 | tf_op jit(solution)/shard_map/ppermute | solution.py:18
  131.2 16.2 %collective-permute-start.30 = (bf16[4,24,1282]{2,1,0:T(8,128)(2,1)S(1)}, bf16[4,24,1282]{2,1,0:T(8,128)(2,1)S(1)}, u32[]{:S(2)}, u32[]{:S(2)}) collective-permute-start(bf16[4,24,1282]{2,1,0:T(8,128)(2,1)S(1)} %get-tuple-element.18), channel_id=1, source_target_pairs={{0,12},{1,13},{2,14},{3,15},{4,0},{5,1},{6,2},{7,3},{8,4},{9,5},{1... | collective-permute-start | bytes 738440 | tf_op jit(solution)/shard_map/ppermute | solution.py:18
  137.0 10.8 %collective-permute-start.29 = (bf16[4,24,1282]{2,1,0:T(8,128)(2,1)S(1)}, bf16[4,24,1282]{2,1,0:T(8,128)(2,1)S(1)}, u32[]{:S(2)}, u32[]{:S(2)}) collective-permute-start(bf16[4,24,1282]{2,1,0:T(8,128)(2,1)S(1)} %get-tuple-element.19), channel_id=1, source_target_pairs={{0,8},{1,9},{2,10},{3,11},{4,12},{5,13},{6,14},{7,15},{8,0},{9,1},... | collective-permute-start | bytes 738440 | tf_op jit(solution)/shard_map/ppermute | solution.py:18
  139.8 11.4 %collective-permute-start.37 = (bf16[24,1280]{1,0:T(8,128)(2,1)S(1)}, bf16[24,1280]{1,0:T(8,128)(2,1)S(1)}, u32[]{:S(2)}, u32[]{:S(2)}) collective-permute-start(bf16[24,1280]{1,0:T(8,128)(2,1)S(1)} %get-tuple-element.45), channel_id=1, source_target_pairs={{0,4},{1,5},{2,6},{3,7},{4,8},{5,9},{6,10},{7,11},{8,12},{9,13},{1... | collective-permute-start | bytes 184328 | tf_op jit(solution)/shard_map/ppermute | solution.py:18
  140.1 12.9 %collective-permute-start.39 = (bf16[24,1280]{1,0:T(8,128)(2,1)S(1)}, bf16[24,1280]{1,0:T(8,128)(2,1)S(1)}, u32[]{:S(2)}, u32[]{:S(2)}) collective-permute-start(bf16[24,1280]{1,0:T(8,128)(2,1)S(1)} %get-tuple-element.46), channel_id=1, source_target_pairs={{0,12},{1,13},{2,14},{3,15},{4,0},{5,1},{6,2},{7,3},{8,4},{9,5},{1... | collective-permute-start | bytes 184328 | tf_op jit(solution)/shard_map/ppermute | solution.py:18
  170.0 10.8 %collective-permute-start.44 = (bf16[4,24,2048]{2,1,0:T(8,128)(2,1)}, bf16[4,24,2048]{2,1,0:T(8,128)(2,1)}, u32[]{:S(2)}, u32[]{:S(2)}) collective-permute-start(bf16[4,24,2048]{2,1,0:T(8,128)(2,1)} %get-tuple-element.36), channel_id=1, source_target_pairs={{0,2},{1,3},{2,0},{3,1},{4,6},{5,7},{6,4},{7,5},{8,10},{9,11},{10,... | collective-permute-start | bytes 1179656 | tf_op jit(solution)/shard_map/ppermute | solution.py:18
  171.7 13.2 %collective-permute-start.43 = (bf16[4,24,2048]{2,1,0:T(8,128)(2,1)}, bf16[4,24,2048]{2,1,0:T(8,128)(2,1)}, u32[]{:S(2)}, u32[]{:S(2)}) collective-permute-start(bf16[4,24,2048]{2,1,0:T(8,128)(2,1)} %get-tuple-element.36), channel_id=1, source_target_pairs={{0,1},{1,2},{2,3},{3,0},{4,5},{5,6},{6,7},{7,4},{8,9},{9,10},{10,1... | collective-permute-start | bytes 1179656 | tf_op jit(solution)/shard_map/ppermute | solution.py:18
  171.7 13.2 %collective-permute-start.45 = (bf16[4,24,2048]{2,1,0:T(8,128)(2,1)}, bf16[4,24,2048]{2,1,0:T(8,128)(2,1)}, u32[]{:S(2)}, u32[]{:S(2)}) collective-permute-start(bf16[4,24,2048]{2,1,0:T(8,128)(2,1)} %get-tuple-element.36), channel_id=1, source_target_pairs={{0,3},{1,0},{2,1},{3,2},{4,7},{5,4},{6,5},{7,6},{8,11},{9,8},{10,9... | collective-permute-start | bytes 1179656 | tf_op jit(solution)/shard_map/ppermute | solution.py:18
  (49 other events, 362.9 us)

commit v7 on v6

--- a/solution.py
+++ b/solution.py
@@ -165,8 +165,11 @@
         partial = jnp.dot(gathered, w_out[0], preferred_element_type=f32).astype(bf16)
         ext_new = jnp.where(keep[:, None, :, None], fresh, jnp.zeros_like(fresh))
         if last:
-            natural = jnp.take(partial, arrived_at(back_index), axis=0)
-            pieces = natural.reshape(rounds, n_tensor, rows_local, width_local).transpose(1, 0, 2, 3)
+            by_group = arrived_at(back_index).reshape(rounds, n_tensor, rows_local)
+            by_group = by_group.transpose(1, 0, 2).reshape(-1)
+            pieces = jnp.take(partial, by_group, axis=0).reshape(
+                n_tensor, rounds, rows_local, width_local
+            )
             mine = sum(r.astype(f32) for r in spread(pieces, tensor, along_tensor))
             x_own = jnp.take(xf, own_index, axis=0).reshape(rounds, rows_local, width_local)
             return None, (x_own + mine).astype(bf16), ext_new

time: 205 us -> 208 us (1.015)
  matrix products: 19.1 us -> 21.2 us
    dot_general x2, matrix products: 5.81 us -> 7.98 us  [layer(): jnp.dot(gathered, w_out[0], preferred_element_type=f32).astype(bf16)]
  transfers between devices with their start and end apart: 49 -> 49, of which waited for: 29 -> 29; matrix products, arithmetic and copies ran while one was open for 12% -> 11% of each run, Pallas kernels for 0% -> 0%
where the time goes in v7:
time: 208 us; the launch traced here: 207 us
  starting transfers between devices  72.7 us (35%)
  waiting for transfers between devices  70.6 us (34%)
  local copies, waits for them, and re-layouts  24.7 us (12%)
  matrix products  21.2 us (10%)
  other arithmetic  16.4 us (8%)
    ppermute x48, starting transfers between devices, shifted(): return lax.ppermute(x, axis, [(i, fn(i, n)) for i in range(n)])  71.3 us
    ppermute x48, waiting for transfers between devices, shifted(): return lax.ppermute(x, axis, [(i, fn(i, n)) for i in range(n)])  70.2 us
    dot_general x2, matrix products, layer(): jnp.dot(gathered, w_out[0], preferred_element_type=f32).astype(bf16)  7.98 us
    dot_general x2, matrix products, layer(): rest = jnp.dot(xg, w_query[0, :, cut:], preferred_element_type=f32)  4.58 us
    dot_general x2, matrix products, layer(): jnp.dot(xg, w_query[0, :, :cut], preferred_element_type=f32).astype(bf16)  4.18 us
  transfers between devices with their start and end apart: 49, of which 29 were waited for; matrix products, arithmetic and copies ran while one was open for 11% of the time, Pallas kernels for 0%

profile of v7, /device:TPU:0, one launch (start us, length us, event | category | flops | bytes accessed | tf_op | source)
XLA Modules:
  0.0 207.1 jit_solution(3364521794761790023)
XLA Ops:
  46.1 3.5 %collective-permute-start.13 = (bf16[24,1280]{1,0:T(8,128)(2,1)S(1)}, bf16[24,1280]{1,0:T(8,128)(2,1)S(1)}, u32[]{:S(2)}, u32[]{:S(2)}) collective-permute-start(bf16[24,1280]{1,0:T(8,128)(2,1)S(1)} %get-tuple-element.48), channel_id=1, source_target_pairs={{0,8},{1,9},{2,10},{3,11},{4,12},{5,13},{6,14},{7,15},{8,0},{9,1},... | collective-permute-start | bytes 184328 | tf_op jit(solution)/shard_map/ppermute | solution.py:18
  56.2 3.2 %collective-permute-done.7 = bf16[24,1282]{1,0:T(8,128)(2,1)S(1)} collective-permute-done((bf16[24,1282]{1,0:T(8,128)(2,1)S(1)}, bf16[24,1282]{1,0:T(8,128)(2,1)S(1)}, u32[]{:S(2)}, u32[]{:S(2)}) %collective-permute-start.7) | collective-permute-done | bytes 61568 | tf_op jit(solution)/shard_map/ppermute | solution.py:18
  65.9 3.1 %collective-permute-done.16 = bf16[24,2048]{1,0:T(8,128)(2,1)S(1)} collective-permute-done((bf16[24,2048]{1,0:T(8,128)(2,1)S(1)}, bf16[24,2048]{1,0:T(8,128)(2,1)S(1)}, u32[]{:S(2)}, u32[]{:S(2)}) %collective-permute-start.16) | collective-permute-done | bytes 98336 | tf_op jit(solution)/shard_map/ppermute | solution.py:18
  75.7 5.0 %collective-permute-done.19 = bf16[4,24,2048]{2,1,0:T(8,128)(2,1)S(1)} collective-permute-done((bf16[4,24,2048]{2,1,0:T(8,128)(2,1)}, bf16[4,24,2048]{2,1,0:T(8,128)(2,1)S(1)}, u32[]{:S(2)}, u32[]{:S(2)}) %collective-permute-start.19) | collective-permute-done | bytes 393248 | tf_op jit(solution)/shard_map/ppermute | solution.py:18
  80.7 4.1 %collective-permute-done.18 = bf16[4,24,2048]{2,1,0:T(8,128)(2,1)S(1)} collective-permute-done((bf16[4,24,2048]{2,1,0:T(8,128)(2,1)}, bf16[4,24,2048]{2,1,0:T(8,128)(2,1)S(1)}, u32[]{:S(2)}, u32[]{:S(2)}) %collective-permute-start.18) | collective-permute-done | bytes 393248 | tf_op jit(solution)/shard_map/ppermute | solution.py:18
  85.0 4.0 %fusion.12 = bf16[384,1024]{1,0:T(8,128)(2,1)S(1)} fusion(bf16[384,2048]{1,0:T(8,128)(2,1)S(1)} %bitcast.266, bf16[1,2048,1024]{2,1,0:T(8,128)(2,1)} %param.14), kind=kOutput, calls=%fused_computation.28 | convolution fusion | flops 1611005952 | bytes 6553600 | tf_op jit(solution)/shard_map/dot_general | solution.py:165
  94.8 9.2 %collective-permute-done.21 = bf16[96,1024]{1,0:T(8,128)(2,1)S(1)} collective-permute-done((bf16[96,1024]{1,0:T(8,128)(2,1)S(1)}, bf16[96,1024]{1,0:T(8,128)(2,1)S(1)}, u32[]{:S(2)}, u32[]{:S(2)}) %collective-permute-start.21) | collective-permute-done | bytes 196640 | tf_op jit(solution)/shard_map/ppermute | solution.py:18
  109.9 3.0 %collective-permute-done.25 = bf16[96,1024]{1,0:T(8,128)(2,1)S(1)} collective-permute-done((bf16[96,1024]{1,0:T(8,128)(2,1)S(1)}, bf16[96,1024]{1,0:T(8,128)(2,1)S(1)}, u32[]{:S(2)}, u32[]{:S(2)}) %collective-permute-start.25) | collective-permute-done | bytes 196640 | tf_op jit(solution)/shard_map/ppermute | solution.py:18
  121.0 2.9 %convolution_convert_fusion = bf16[384,1280]{1,0:T(8,128)(2,1)S(1)} fusion(bf16[1,1024,2048]{2,1,0:T(8,128)(2,1)} %param.12, bf16[384,1024]{1,0:T(8,128)(2,1)S(1)} %collective-permute-done.27, f32[1024]{0:T(1024)S(1)} %bitcast.309), kind=kOutput, calls=%fused_computation.12 | convolution fusion | flops 1008304128 | bytes 4395008 | tf_op jit(solution)/shard_map/dot_general | solution.py:127
  125.2 3.0 %collective-permute-start.36 = (bf16[4,24,1280]{2,1,0:T(8,128)(2,1)}, bf16[4,24,1280]{2,1,0:T(8,128)(2,1)}, u32[]{:S(2)}, u32[]{:S(2)}) collective-permute-start(bf16[4,24,1280]{2,1,0:T(8,128)(2,1)} %get-tuple-element.22), channel_id=1, source_target_pairs={{0,3},{1,0},{2,1},{3,2},{4,7},{5,4},{6,5},{7,6},{8,11},{9,8},{10,9... | collective-permute-start | bytes 737288 | tf_op jit(solution)/shard_map/ppermute | solution.py:18
  134.2 3.0 %collective-permute-start.30 = (bf16[4,24,1282]{2,1,0:T(8,128)(2,1)S(1)}, bf16[4,24,1282]{2,1,0:T(8,128)(2,1)S(1)}, u32[]{:S(2)}, u32[]{:S(2)}) collective-permute-start(bf16[4,24,1282]{2,1,0:T(8,128)(2,1)S(1)} %get-tuple-element.16), channel_id=1, source_target_pairs={{0,12},{1,13},{2,14},{3,15},{4,0},{5,1},{6,2},{7,3},{8,4},{9,5},{1... | collective-permute-start | bytes 738440 | tf_op jit(solution)/shard_map/ppermute | solution.py:18
  137.2 2.8 %collective-permute-done.34 = bf16[4,24,1280]{2,1,0:T(8,128)(2,1)} collective-permute-done((bf16[4,24,1280]{2,1,0:T(8,128)(2,1)}, bf16[4,24,1280]{2,1,0:T(8,128)(2,1)}, u32[]{:S(2)}, u32[]{:S(2)}) %collective-permute-start.34) | collective-permute-done | bytes 245792 | tf_op jit(solution)/shard_map/ppermute | solution.py:18
  142.9 3.2 %collective-permute-start.39 = (bf16[24,1280]{1,0:T(8,128)(2,1)S(1)}, bf16[24,1280]{1,0:T(8,128)(2,1)S(1)}, u32[]{:S(2)}, u32[]{:S(2)}) collective-permute-start(bf16[24,1280]{1,0:T(8,128)(2,1)S(1)} %get-tuple-element.44), channel_id=1, source_target_pairs={{0,12},{1,13},{2,14},{3,15},{4,0},{5,1},{6,2},{7,3},{8,4},{9,5},{1... | collective-permute-start | bytes 184328 | tf_op jit(solution)/shard_map/ppermute | solution.py:18
  147.1 3.4 %collective-permute-done.30 = bf16[4,24,1282]{2,1,0:T(8,128)(2,1)S(1)} collective-permute-done((bf16[4,24,1282]{2,1,0:T(8,128)(2,1)S(1)}, bf16[4,24,1282]{2,1,0:T(8,128)(2,1)S(1)}, u32[]{:S(2)}, u32[]{:S(2)}) %collective-permute-start.30) | collective-permute-done | bytes 246176 | tf_op jit(solution)/shard_map/ppermute | solution.py:18
  151.0 3.2 %collective-permute-start.33 = (bf16[24,1282]{1,0:T(8,128)(2,1)S(1)}, bf16[24,1282]{1,0:T(8,128)(2,1)S(1)}, u32[]{:S(2)}, u32[]{:S(2)}) collective-permute-start(bf16[24,1282]{1,0:T(8,128)(2,1)S(1)} %get-tuple-element.38), channel_id=1, source_target_pairs={{0,3},{1,0},{2,1},{3,2},{4,7},{5,4},{6,5},{7,6},{8,11},{9,8},{10,9... | collective-permute-start | bytes 184616 | tf_op jit(solution)/shard_map/ppermute | solution.py:18
  157.0 3.0 %collective-permute-done.32 = bf16[24,1282]{1,0:T(8,128)(2,1)S(1)} collective-permute-done((bf16[24,1282]{1,0:T(8,128)(2,1)S(1)}, bf16[24,1282]{1,0:T(8,128)(2,1)S(1)}, u32[]{:S(2)}, u32[]{:S(2)}) %collective-permute-start.32) | collective-permute-done | bytes 61568 | tf_op jit(solution)/shard_map/ppermute | solution.py:18
  161.8 3.4 %collective-permute-start.42 = (bf16[24,2048]{1,0:T(8,128)(2,1)S(1)}, bf16[24,2048]{1,0:T(8,128)(2,1)S(1)}, u32[]{:S(2)}, u32[]{:S(2)}) collective-permute-start(bf16[24,2048]{1,0:T(8,128)(2,1)S(1)} %reshape.689), channel_id=1, source_target_pairs={{0,12},{1,13},{2,14},{3,15},{4,0},{5,1},{6,2},{7,3},{8,4},{9,5},{1... | collective-permute-start | bytes 294920 | tf_op jit(solution)/shard_map/ppermute | solution.py:18
  168.4 3.0 %collective-permute-done.41 = bf16[24,2048]{1,0:T(8,128)(2,1)S(1)} collective-permute-done((bf16[24,2048]{1,0:T(8,128)(2,1)S(1)}, bf16[24,2048]{1,0:T(8,128)(2,1)S(1)}, u32[]{:S(2)}, u32[]{:S(2)}) %collective-permute-start.41) | collective-permute-done | bytes 98336 | tf_op jit(solution)/shard_map/ppermute | solution.py:18
  174.7 3.2 %collective-permute-start.45 = (bf16[4,24,2048]{2,1,0:T(8,128)(2,1)}, bf16[4,24,2048]{2,1,0:T(8,128)(2,1)}, u32[]{:S(2)}, u32[]{:S(2)}) collective-permute-start(bf16[4,24,2048]{2,1,0:T(8,128)(2,1)} %get-tuple-element.34), channel_id=1, source_target_pairs={{0,3},{1,0},{2,1},{3,2},{4,7},{5,4},{6,5},{7,6},{8,11},{9,8},{10,9... | collective-permute-start | bytes 1179656 | tf_op jit(solution)/shard_map/ppermute | solution.py:18
  180.4 3.5 %collective-permute-done.44 = bf16[4,24,2048]{2,1,0:T(8,128)(2,1)} collective-permute-done((bf16[4,24,2048]{2,1,0:T(8,128)(2,1)}, bf16[4,24,2048]{2,1,0:T(8,128)(2,1)}, u32[]{:S(2)}, u32[]{:S(2)}) %collective-permute-start.44) | collective-permute-done | bytes 393248 | tf_op jit(solution)/shard_map/ppermute | solution.py:18
  183.9 4.1 %collective-permute-done.43 = bf16[4,24,2048]{2,1,0:T(8,128)(2,1)} collective-permute-done((bf16[4,24,2048]{2,1,0:T(8,128)(2,1)}, bf16[4,24,2048]{2,1,0:T(8,128)(2,1)}, u32[]{:S(2)}, u32[]{:S(2)}) %collective-permute-start.43) | collective-permute-done | bytes 393248 | tf_op jit(solution)/shard_map/ppermute | solution.py:18
  189.4 4.0 %fusion.15 = bf16[384,1024]{1,0:T(8,128)(2,1)S(1)} fusion(bf16[384,2048]{1,0:T(8,128)(2,1)S(1)} %bitcast.267, bf16[1,2048,1024]{2,1,0:T(8,128)(2,1)} %param.14), kind=kOutput, calls=%fused_computation.29 | convolution fusion | flops 1611005952 | bytes 6553600 | tf_op jit(solution)/shard_map/dot_general | solution.py:165
  195.8 3.2 %collective-permute-start.48 = (bf16[3,32,1024]{2,1,0:T(8,128)(2,1)S(1)}, bf16[3,32,1024]{2,1,0:T(8,128)(2,1)S(1)}, u32[]{:S(2)}, u32[]{:S(2)}) collective-permute-start(bf16[3,32,1024]{2,1,0:T(8,128)(2,1)S(1)} %get-tuple-element.28), channel_id=1, source_target_pairs={{0,48},{16,0},{32,16},{48,32},{1,49},{17,1},{33,17},{49,33},{2,50}... | collective-permute-start | bytes 589832 | tf_op jit(solution)/shard_map/ppermute | solution.py:18
  199.7 4.1 %collective-permute-done.46 = bf16[3,32,1024]{2,1,0:T(8,128)(2,1)S(1)} collective-permute-done((bf16[3,32,1024]{2,1,0:T(8,128)(2,1)S(1)}, bf16[3,32,1024]{2,1,0:T(8,128)(2,1)S(1)}, u32[]{:S(2)}, u32[]{:S(2)}) %collective-permute-start.46) | collective-permute-done | bytes 196640 | tf_op jit(solution)/shard_map/ppermute | solution.py:18
  (259 shorter events, 117.5 us)
Async XLA Ops:
  0.6 12.3 %collective-permute-start = (bf16[3,32,1024]{2,1,0:T(8,128)(2,1)}, bf16[3,32,1024]{2,1,0:T(8,128)(2,1)S(1)}, u32[]{:S(2)}, u32[]{:S(2)}) collective-permute-start(bf16[3,32,1024]{2,1,0:T(8,128)(2,1)} %param.10), channel_id=1, source_target_pairs={{0,16},{16,32},{32,48},{48,0},{1,17},{17,33},{33,49},{49,1},{2,18}... | collective-permute-start | bytes 589832 | tf_op jit(solution)/shard_map/ppermute | solution.py:18
  2.3 10.7 %collective-permute-start.2 = (bf16[3,32,1024]{2,1,0:T(8,128)(2,1)}, bf16[3,32,1024]{2,1,0:T(8,128)(2,1)S(1)}, u32[]{:S(2)}, u32[]{:S(2)}) collective-permute-start(bf16[3,32,1024]{2,1,0:T(8,128)(2,1)} %param.10), channel_id=1, source_target_pairs={{0,48},{16,0},{32,16},{48,32},{1,49},{17,1},{33,17},{49,33},{2,50}... | collective-permute-start | bytes 589832 | tf_op jit(solution)/shard_map/ppermute | solution.py:18
  25.6 11.6 %collective-permute-start.9 = (bf16[4,24,1280]{2,1,0:T(8,128)(2,1)}, bf16[4,24,1280]{2,1,0:T(8,128)(2,1)}, u32[]{:S(2)}, u32[]{:S(2)}) collective-permute-start(bf16[4,24,1280]{2,1,0:T(8,128)(2,1)} %get-tuple-element.24), channel_id=1, source_target_pairs={{0,1},{1,2},{2,3},{3,0},{4,5},{5,6},{6,7},{7,4},{8,9},{9,10},{10,1... | collective-permute-start | bytes 737288 | tf_op jit(solution)/shard_map/ppermute | solution.py:18
  27.2 11.8 %collective-permute-start.11 = (bf16[4,24,1280]{2,1,0:T(8,128)(2,1)}, bf16[4,24,1280]{2,1,0:T(8,128)(2,1)}, u32[]{:S(2)}, u32[]{:S(2)}) collective-permute-start(bf16[4,24,1280]{2,1,0:T(8,128)(2,1)} %get-tuple-element.25), channel_id=1, source_target_pairs={{0,3},{1,0},{2,1},{3,2},{4,7},{5,4},{6,5},{7,6},{8,11},{9,8},{10,9... | collective-permute-start | bytes 737288 | tf_op jit(solution)/shard_map/ppermute | solution.py:18
  28.8 11.6 %collective-permute-start.10 = (bf16[4,24,1280]{2,1,0:T(8,128)(2,1)}, bf16[4,24,1280]{2,1,0:T(8,128)(2,1)}, u32[]{:S(2)}, u32[]{:S(2)}) collective-permute-start(bf16[4,24,1280]{2,1,0:T(8,128)(2,1)} %get-tuple-element.26), channel_id=1, source_target_pairs={{0,2},{1,3},{2,0},{3,1},{4,6},{5,7},{6,4},{7,5},{8,10},{9,11},{10,... | collective-permute-start | bytes 737288 | tf_op jit(solution)/shard_map/ppermute | solution.py:18
  33.0 13.2 %collective-permute-start.3 = (bf16[4,24,1282]{2,1,0:T(8,128)(2,1)S(1)}, bf16[4,24,1282]{2,1,0:T(8,128)(2,1)S(1)}, u32[]{:S(2)}, u32[]{:S(2)}) collective-permute-start(bf16[4,24,1282]{2,1,0:T(8,128)(2,1)S(1)} %get-tuple-element.18), channel_id=1, source_target_pairs={{0,4},{1,5},{2,6},{3,7},{4,8},{5,9},{6,10},{7,11},{8,12},{9,13},{1... | collective-permute-start | bytes 738440 | tf_op jit(solution)/shard_map/ppermute | solution.py:18
  35.0 14.6 %collective-permute-start.5 = (bf16[4,24,1282]{2,1,0:T(8,128)(2,1)S(1)}, bf16[4,24,1282]{2,1,0:T(8,128)(2,1)S(1)}, u32[]{:S(2)}, u32[]{:S(2)}) collective-permute-start(bf16[4,24,1282]{2,1,0:T(8,128)(2,1)S(1)} %get-tuple-element.19), channel_id=1, source_target_pairs={{0,12},{1,13},{2,14},{3,15},{4,0},{5,1},{6,2},{7,3},{8,4},{9,5},{1... | collective-permute-start | bytes 738440 | tf_op jit(solution)/shard_map/ppermute | solution.py:18
  37.2 13.0 %collective-permute-start.4 = (bf16[4,24,1282]{2,1,0:T(8,128)(2,1)S(1)}, bf16[4,24,1282]{2,1,0:T(8,128)(2,1)S(1)}, u32[]{:S(2)}, u32[]{:S(2)}) collective-permute-start(bf16[4,24,1282]{2,1,0:T(8,128)(2,1)S(1)} %get-tuple-element.20), channel_id=1, source_target_pairs={{0,8},{1,9},{2,10},{3,11},{4,12},{5,13},{6,14},{7,15},{8,0},{9,1},... | collective-permute-start | bytes 738440 | tf_op jit(solution)/shard_map/ppermute | solution.py:18
  41.9 11.7 %collective-permute-start.12 = (bf16[24,1280]{1,0:T(8,128)(2,1)S(1)}, bf16[24,1280]{1,0:T(8,128)(2,1)S(1)}, u32[]{:S(2)}, u32[]{:S(2)}) collective-permute-start(bf16[24,1280]{1,0:T(8,128)(2,1)S(1)} %get-tuple-element.46), channel_id=1, source_target_pairs={{0,4},{1,5},{2,6},{3,7},{4,8},{5,9},{6,10},{7,11},{8,12},{9,13},{1... | collective-permute-start | bytes 184328 | tf_op jit(solution)/shard_map/ppermute | solution.py:18
  71.8 13.1 %collective-permute-start.18 = (bf16[4,24,2048]{2,1,0:T(8,128)(2,1)}, bf16[4,24,2048]{2,1,0:T(8,128)(2,1)S(1)}, u32[]{:S(2)}, u32[]{:S(2)}) collective-permute-start(bf16[4,24,2048]{2,1,0:T(8,128)(2,1)} %get-tuple-element.36), channel_id=1, source_target_pairs={{0,1},{1,2},{2,3},{3,0},{4,5},{5,6},{6,7},{7,4},{8,9},{9,10},{10,1... | collective-permute-start | bytes 1179656 | tf_op jit(solution)/shard_map/ppermute | solution.py:18
  72.4 12.4 %collective-permute-start.20 = (bf16[4,24,2048]{2,1,0:T(8,128)(2,1)}, bf16[4,24,2048]{2,1,0:T(8,128)(2,1)S(1)}, u32[]{:S(2)}, u32[]{:S(2)}) collective-permute-start(bf16[4,24,2048]{2,1,0:T(8,128)(2,1)} %get-tuple-element.36), channel_id=1, source_target_pairs={{0,3},{1,0},{2,1},{3,2},{4,7},{5,4},{6,5},{7,6},{8,11},{9,8},{10,9... | collective-permute-start | bytes 1179656 | tf_op jit(solution)/shard_map/ppermute | solution.py:18
  91.3 12.7 %collective-permute-start.21 = (bf16[96,1024]{1,0:T(8,128)(2,1)S(1)}, bf16[96,1024]{1,0:T(8,128)(2,1)S(1)}, u32[]{:S(2)}, u32[]{:S(2)}) collective-permute-start(bf16[96,1024]{1,0:T(8,128)(2,1)S(1)} %get-tuple-element.30), channel_id=1, source_target_pairs={{0,16},{16,32},{32,48},{48,0},{1,17},{17,33},{33,49},{49,1},{2,18}... | collective-permute-start | bytes 589832 | tf_op jit(solution)/shard_map/ppermute | solution.py:18
  92.4 11.7 %collective-permute-start.23 = (bf16[96,1024]{1,0:T(8,128)(2,1)S(1)}, bf16[96,1024]{1,0:T(8,128)(2,1)S(1)}, u32[]{:S(2)}, u32[]{:S(2)}) collective-permute-start(bf16[96,1024]{1,0:T(8,128)(2,1)S(1)} %get-tuple-element.31), channel_id=1, source_target_pairs={{0,48},{16,0},{32,16},{48,32},{1,49},{17,1},{33,17},{49,33},{2,50}... | collective-permute-start | bytes 589832 | tf_op jit(solution)/shard_map/ppermute | solution.py:18
  124.9 15.0 %collective-permute-start.34 = (bf16[4,24,1280]{2,1,0:T(8,128)(2,1)}, bf16[4,24,1280]{2,1,0:T(8,128)(2,1)}, u32[]{:S(2)}, u32[]{:S(2)}) collective-permute-start(bf16[4,24,1280]{2,1,0:T(8,128)(2,1)} %get-tuple-element.21), channel_id=1, source_target_pairs={{0,1},{1,2},{2,3},{3,0},{4,5},{5,6},{6,7},{7,4},{8,9},{9,10},{10,1... | collective-permute-start | bytes 737288 | tf_op jit(solution)/shard_map/ppermute | solution.py:18
  125.2 16.1 %collective-permute-start.36 = (bf16[4,24,1280]{2,1,0:T(8,128)(2,1)}, bf16[4,24,1280]{2,1,0:T(8,128)(2,1)}, u32[]{:S(2)}, u32[]{:S(2)}) collective-permute-start(bf16[4,24,1280]{2,1,0:T(8,128)(2,1)} %get-tuple-element.22), channel_id=1, source_target_pairs={{0,3},{1,0},{2,1},{3,2},{4,7},{5,4},{6,5},{7,6},{8,11},{9,8},{10,9... | collective-permute-start | bytes 737288 | tf_op jit(solution)/shard_map/ppermute | solution.py:18
  128.2 13.2 %collective-permute-start.35 = (bf16[4,24,1280]{2,1,0:T(8,128)(2,1)}, bf16[4,24,1280]{2,1,0:T(8,128)(2,1)}, u32[]{:S(2)}, u32[]{:S(2)}) collective-permute-start(bf16[4,24,1280]{2,1,0:T(8,128)(2,1)} %get-tuple-element.23), channel_id=1, source_target_pairs={{0,2},{1,3},{2,0},{3,1},{4,6},{5,7},{6,4},{7,5},{8,10},{9,11},{10,... | collective-permute-start | bytes 737288 | tf_op jit(solution)/shard_map/ppermute | solution.py:18
  133.9 12.2 %collective-permute-start.28 = (bf16[4,24,1282]{2,1,0:T(8,128)(2,1)S(1)}, bf16[4,24,1282]{2,1,0:T(8,128)(2,1)S(1)}, u32[]{:S(2)}, u32[]{:S(2)}) collective-permute-start(bf16[4,24,1282]{2,1,0:T(8,128)(2,1)S(1)} %get-tuple-element.15), channel_id=1, source_target_pairs={{0,4},{1,5},{2,6},{3,7},{4,8},{5,9},{6,10},{7,11},{8,12},{9,13},{1... | collective-permute-start | bytes 738440 | tf_op jit(solution)/shard_map/ppermute | solution.py:18
  134.2 16.2 %collective-permute-start.30 = (bf16[4,24,1282]{2,1,0:T(8,128)(2,1)S(1)}, bf16[4,24,1282]{2,1,0:T(8,128)(2,1)S(1)}, u32[]{:S(2)}, u32[]{:S(2)}) collective-permute-start(bf16[4,24,1282]{2,1,0:T(8,128)(2,1)S(1)} %get-tuple-element.16), channel_id=1, source_target_pairs={{0,12},{1,13},{2,14},{3,15},{4,0},{5,1},{6,2},{7,3},{8,4},{9,5},{1... | collective-permute-start | bytes 738440 | tf_op jit(solution)/shard_map/ppermute | solution.py:18
  140.0 10.8 %collective-permute-start.29 = (bf16[4,24,1282]{2,1,0:T(8,128)(2,1)S(1)}, bf16[4,24,1282]{2,1,0:T(8,128)(2,1)S(1)}, u32[]{:S(2)}, u32[]{:S(2)}) collective-permute-start(bf16[4,24,1282]{2,1,0:T(8,128)(2,1)S(1)} %get-tuple-element.17), channel_id=1, source_target_pairs={{0,8},{1,9},{2,10},{3,11},{4,12},{5,13},{6,14},{7,15},{8,0},{9,1},... | collective-permute-start | bytes 738440 | tf_op jit(solution)/shard_map/ppermute | solution.py:18
  142.8 11.4 %collective-permute-start.37 = (bf16[24,1280]{1,0:T(8,128)(2,1)S(1)}, bf16[24,1280]{1,0:T(8,128)(2,1)S(1)}, u32[]{:S(2)}, u32[]{:S(2)}) collective-permute-start(bf16[24,1280]{1,0:T(8,128)(2,1)S(1)} %get-tuple-element.43), channel_id=1, source_target_pairs={{0,4},{1,5},{2,6},{3,7},{4,8},{5,9},{6,10},{7,11},{8,12},{9,13},{1... | collective-permute-start | bytes 184328 | tf_op jit(solution)/shard_map/ppermute | solution.py:18
  142.9 13.2 %collective-permute-start.39 = (bf16[24,1280]{1,0:T(8,128)(2,1)S(1)}, bf16[24,1280]{1,0:T(8,128)(2,1)S(1)}, u32[]{:S(2)}, u32[]{:S(2)}) collective-permute-start(bf16[24,1280]{1,0:T(8,128)(2,1)S(1)} %get-tuple-element.44), channel_id=1, source_target_pairs={{0,12},{1,13},{2,14},{3,15},{4,0},{5,1},{6,2},{7,3},{8,4},{9,5},{1... | collective-permute-start | bytes 184328 | tf_op jit(solution)/shard_map/ppermute | solution.py:18
  173.1 10.8 %collective-permute-start.44 = (bf16[4,24,2048]{2,1,0:T(8,128)(2,1)}, bf16[4,24,2048]{2,1,0:T(8,128)(2,1)}, u32[]{:S(2)}, u32[]{:S(2)}) collective-permute-start(bf16[4,24,2048]{2,1,0:T(8,128)(2,1)} %get-tuple-element.34), channel_id=1, source_target_pairs={{0,2},{1,3},{2,0},{3,1},{4,6},{5,7},{6,4},{7,5},{8,10},{9,11},{10,... | collective-permute-start | bytes 1179656 | tf_op jit(solution)/shard_map/ppermute | solution.py:18
  174.7 13.2 %collective-permute-start.43 = (bf16[4,24,2048]{2,1,0:T(8,128)(2,1)}, bf16[4,24,2048]{2,1,0:T(8,128)(2,1)}, u32[]{:S(2)}, u32[]{:S(2)}) collective-permute-start(bf16[4,24,2048]{2,1,0:T(8,128)(2,1)} %get-tuple-element.34), channel_id=1, source_target_pairs={{0,1},{1,2},{2,3},{3,0},{4,5},{5,6},{6,7},{7,4},{8,9},{9,10},{10,1... | collective-permute-start | bytes 1179656 | tf_op jit(solution)/shard_map/ppermute | solution.py:18
  174.7 13.2 %collective-permute-start.45 = (bf16[4,24,2048]{2,1,0:T(8,128)(2,1)}, bf16[4,24,2048]{2,1,0:T(8,128)(2,1)}, u32[]{:S(2)}, u32[]{:S(2)}) collective-permute-start(bf16[4,24,2048]{2,1,0:T(8,128)(2,1)} %get-tuple-element.34), channel_id=1, source_target_pairs={{0,3},{1,0},{2,1},{3,2},{4,7},{5,4},{6,5},{7,6},{8,11},{9,8},{10,9... | collective-permute-start | bytes 1179656 | tf_op jit(solution)/shard_map/ppermute | solution.py:18
  (46 other events, 344.5 us)

commit v8 on v6

--- a/solution.py
+++ b/solution.py
@@ -115,7 +115,7 @@
         b = s // own_rows
         shift_y = (y_pos - b % n_y) % n_y
         shift_z = (z_pos - b // n_y) % n_z
-        return (shift_y * n_z + shift_z) * own_rows + s % own_rows
+        return (shift_z * n_y + shift_y) * own_rows + s % own_rows
 
     def layer(x_sorted, last):
         xf = x_sorted.astype(f32)
@@ -159,8 +159,8 @@
             "shgrjl,shld->srjhgd", weights, values, preferred_element_type=f32
         )
         attended = attended.astype(bf16).reshape(own_rows, query_cols)
-        by_z = jnp.stack([attended] + [along_z(attended, k) for k in range(1, n_z)])
-        by_zy = jnp.stack([by_z] + [along_y(by_z, k) for k in range(1, n_y)])
+        by_y = jnp.stack([attended] + [along_y(attended, k) for k in range(1, n_y)])
+        by_zy = jnp.stack([by_y] + [along_z(by_y, k) for k in range(1, n_z)])
         gathered = by_zy.reshape(-1, query_cols)
         partial = jnp.dot(gathered, w_out[0], preferred_element_type=f32).astype(bf16)
         ext_new = jnp.where(keep[:, None, :, None], fresh, jnp.zeros_like(fresh))

time: 205 us -> 204 us (level)
  transfers between devices with their start and end apart: 49 -> 49, of which waited for: 29 -> 31; matrix products, arithmetic and copies ran while one was open for 12% -> 12% of each run, Pallas kernels for 0% -> 0%
where the time goes in v8:
time: 204 us; the launch traced here: 203 us
  starting transfers between devices  72.8 us (36%)
  waiting for transfers between devices  68.7 us (34%)
  local copies, waits for them, and re-layouts  24.6 us (12%)
  matrix products  19.1 us (9%)
  other arithmetic  16.5 us (8%)
    ppermute x48, starting transfers between devices, shifted(): return lax.ppermute(x, axis, [(i, fn(i, n)) for i in range(n)])  71.5 us
    ppermute x48, waiting for transfers between devices, shifted(): return lax.ppermute(x, axis, [(i, fn(i, n)) for i in range(n)])  68.3 us
    dot_general x2, matrix products, layer(): jnp.dot(gathered, w_out[0], preferred_element_type=f32).astype(bf16)  5.81 us
    dot_general x2, matrix products, layer(): rest = jnp.dot(xg, w_query[0, :, cut:], preferred_element_type=f32)  4.58 us
    dot_general x2, matrix products, layer(): jnp.dot(xg, w_query[0, :, :cut], preferred_element_type=f32).astype(bf16)  4.18 us
    concatenate x2, local copies, waits for them, and re-layouts, layer(): jnp.concatenate([rest.astype(bf16), second.astype(bf16), sq_hi, sq_lo], a...  4.14 us
  transfers between devices with their start and end apart: 49, of which 31 were waited for; matrix products, arithmetic and copies ran while one was open for 12% of the time, Pallas kernels for 0%

profile of v8, /device:TPU:0, one launch (start us, length us, event | category | flops | bytes accessed | tf_op | source)
XLA Modules:
  0.0 203.2 jit_solution(8615090234726407984)
XLA Ops:
  17.6 2.4 %fusion.20 = bf16[384,768]{1,0:T(8,128)(2,1)S(1)} fusion(bf16[1,1024,2048]{2,1,0:T(8,128)(2,1)} %param.12, f32[1024]{0:T(1024)S(1)} %bitcast.306, bf16[384,1024]{1,0:T(8,128)(2,1)S(1)} %gather_fusion.5, pred[384]{0:T(512)(128)(4,1)S(1)} %compare_and_fusion.2), kind=kOutput, calls=%fused_computation.32 | convolution fusion | flops 605847552 | bytes 2953600 | tf_op jit(solution)/shard_map/dot_general | solution.py:128
  46.2 3.5 %collective-permute-start.13 = (bf16[24,1280]{1,0:T(8,128)(2,1)S(1)}, bf16[24,1280]{1,0:T(8,128)(2,1)S(1)}, u32[]{:S(2)}, u32[]{:S(2)}) collective-permute-start(bf16[24,1280]{1,0:T(8,128)(2,1)S(1)} %get-tuple-element.50), channel_id=1, source_target_pairs={{0,8},{1,9},{2,10},{3,11},{4,12},{5,13},{6,14},{7,15},{8,0},{9,1},... | collective-permute-start | bytes 184328 | tf_op jit(solution)/shard_map/ppermute | solution.py:18
  51.1 2.6 %collective-permute-start.8 = (bf16[24,1282]{1,0:T(8,128)(2,1)S(1)}, bf16[24,1282]{1,0:T(8,128)(2,1)S(1)}, u32[]{:S(2)}, u32[]{:S(2)}) collective-permute-start(bf16[24,1282]{1,0:T(8,128)(2,1)S(1)} %get-tuple-element.43), channel_id=1, source_target_pairs={{0,3},{1,0},{2,1},{3,2},{4,7},{5,4},{6,5},{7,6},{8,11},{9,8},{10,9... | collective-permute-start | bytes 184616 | tf_op jit(solution)/shard_map/ppermute | solution.py:18
  56.2 3.2 %collective-permute-done.7 = bf16[24,1282]{1,0:T(8,128)(2,1)S(1)} collective-permute-done((bf16[24,1282]{1,0:T(8,128)(2,1)S(1)}, bf16[24,1282]{1,0:T(8,128)(2,1)S(1)}, u32[]{:S(2)}, u32[]{:S(2)}) %collective-permute-start.7) | collective-permute-done | bytes 61568 | tf_op jit(solution)/shard_map/ppermute | solution.py:18
  73.8 5.2 %collective-permute-done.19 = bf16[4,24,2048]{2,1,0:T(8,128)(2,1)S(1)} collective-permute-done((bf16[4,24,2048]{2,1,0:T(8,128)(2,1)S(1)}, bf16[4,24,2048]{2,1,0:T(8,128)(2,1)S(1)}, u32[]{:S(2)}, u32[]{:S(2)}) %collective-permute-start.19) | collective-permute-done | bytes 393248 | tf_op jit(solution)/shard_map/ppermute | solution.py:18
  79.1 4.1 %collective-permute-done.18 = bf16[4,24,2048]{2,1,0:T(8,128)(2,1)S(1)} collective-permute-done((bf16[4,24,2048]{2,1,0:T(8,128)(2,1)S(1)}, bf16[4,24,2048]{2,1,0:T(8,128)(2,1)S(1)}, u32[]{:S(2)}, u32[]{:S(2)}) %collective-permute-start.18) | collective-permute-done | bytes 393248 | tf_op jit(solution)/shard_map/ppermute | solution.py:18
  88.2 2.6 %collective-permute-start.23 = (bf16[96,1024]{1,0:T(8,128)(2,1)S(1)}, bf16[96,1024]{1,0:T(8,128)(2,1)S(1)}, u32[]{:S(2)}, u32[]{:S(2)}) collective-permute-start(bf16[96,1024]{1,0:T(8,128)(2,1)S(1)} %get-tuple-element.33), channel_id=1, source_target_pairs={{0,48},{16,0},{32,16},{48,32},{1,49},{17,1},{33,17},{49,33},{2,50}... | collective-permute-start | bytes 589832 | tf_op jit(solution)/shard_map/ppermute | solution.py:18
  91.0 3.5 %collective-permute-done.21 = bf16[96,1024]{1,0:T(8,128)(2,1)S(1)} collective-permute-done((bf16[96,1024]{1,0:T(8,128)(2,1)S(1)}, bf16[96,1024]{1,0:T(8,128)(2,1)S(1)}, u32[]{:S(2)}, u32[]{:S(2)}) %collective-permute-start.21) | collective-permute-done | bytes 196640 | tf_op jit(solution)/shard_map/ppermute | solution.py:18
  94.4 4.7 %collective-permute-done.23 = bf16[96,1024]{1,0:T(8,128)(2,1)S(1)} collective-permute-done((bf16[96,1024]{1,0:T(8,128)(2,1)S(1)}, bf16[96,1024]{1,0:T(8,128)(2,1)S(1)}, u32[]{:S(2)}, u32[]{:S(2)}) %collective-permute-start.23) | collective-permute-done | bytes 196640 | tf_op jit(solution)/shard_map/ppermute | solution.py:18
  100.2 2.8 %collective-permute-start.26 = (bf16[96,1024]{1,0:T(8,128)(2,1)S(1)}, bf16[96,1024]{1,0:T(8,128)(2,1)S(1)}, u32[]{:S(2)}, u32[]{:S(2)}) collective-permute-start(bf16[96,1024]{1,0:T(8,128)(2,1)S(1)} %fusion.59), channel_id=1, source_target_pairs={{0,48},{16,0},{32,16},{48,32},{1,49},{17,1},{33,17},{49,33},{2,50}... | collective-permute-start | bytes 589832 | tf_op jit(solution)/shard_map/ppermute | solution.py:18
  104.0 4.4 %collective-permute-done.26 = bf16[96,1024]{1,0:T(8,128)(2,1)S(1)} collective-permute-done((bf16[96,1024]{1,0:T(8,128)(2,1)S(1)}, bf16[96,1024]{1,0:T(8,128)(2,1)S(1)}, u32[]{:S(2)}, u32[]{:S(2)}) %collective-permute-start.26) | collective-permute-done | bytes 196640 | tf_op jit(solution)/shard_map/ppermute | solution.py:18
  118.1 2.9 %convolution_convert_fusion = bf16[384,1280]{1,0:T(8,128)(2,1)S(1)} fusion(bf16[1,1024,2048]{2,1,0:T(8,128)(2,1)} %param.12, bf16[384,1024]{1,0:T(8,128)(2,1)S(1)} %collective-permute-done.27, f32[1024]{0:T(1024)S(1)} %bitcast.309), kind=kOutput, calls=%fused_computation.12 | convolution fusion | flops 1008304128 | bytes 4395008 | tf_op jit(solution)/shard_map/dot_general | solution.py:127
  134.7 2.3 %collective-permute-done.34 = bf16[4,24,1280]{2,1,0:T(8,128)(2,1)} collective-permute-done((bf16[4,24,1280]{2,1,0:T(8,128)(2,1)}, bf16[4,24,1280]{2,1,0:T(8,128)(2,1)}, u32[]{:S(2)}, u32[]{:S(2)}) %collective-permute-start.34) | collective-permute-done | bytes 245792 | tf_op jit(solution)/shard_map/ppermute | solution.py:18
  140.8 2.7 %collective-permute-start.39 = (bf16[24,1280]{1,0:T(8,128)(2,1)S(1)}, bf16[24,1280]{1,0:T(8,128)(2,1)S(1)}, u32[]{:S(2)}, u32[]{:S(2)}) collective-permute-start(bf16[24,1280]{1,0:T(8,128)(2,1)S(1)} %get-tuple-element.46), channel_id=1, source_target_pairs={{0,12},{1,13},{2,14},{3,15},{4,0},{5,1},{6,2},{7,3},{8,4},{9,5},{1... | collective-permute-start | bytes 184328 | tf_op jit(solution)/shard_map/ppermute | solution.py:18
  143.5 4.2 %collective-permute-done.28 = bf16[4,24,1282]{2,1,0:T(8,128)(2,1)S(1)} collective-permute-done((bf16[4,24,1282]{2,1,0:T(8,128)(2,1)S(1)}, bf16[4,24,1282]{2,1,0:T(8,128)(2,1)S(1)}, u32[]{:S(2)}, u32[]{:S(2)}) %collective-permute-start.28) | collective-permute-done | bytes 246176 | tf_op jit(solution)/shard_map/ppermute | solution.py:18
  148.7 2.5 %collective-permute-start.33 = (bf16[24,1282]{1,0:T(8,128)(2,1)S(1)}, bf16[24,1282]{1,0:T(8,128)(2,1)S(1)}, u32[]{:S(2)}, u32[]{:S(2)}) collective-permute-start(bf16[24,1282]{1,0:T(8,128)(2,1)S(1)} %get-tuple-element.40), channel_id=1, source_target_pairs={{0,3},{1,0},{2,1},{3,2},{4,7},{5,4},{6,5},{7,6},{8,11},{9,8},{10,9... | collective-permute-start | bytes 184616 | tf_op jit(solution)/shard_map/ppermute | solution.py:18
  153.5 3.5 %collective-permute-done.32 = bf16[24,1282]{1,0:T(8,128)(2,1)S(1)} collective-permute-done((bf16[24,1282]{1,0:T(8,128)(2,1)S(1)}, bf16[24,1282]{1,0:T(8,128)(2,1)S(1)}, u32[]{:S(2)}, u32[]{:S(2)}) %collective-permute-start.32) | collective-permute-done | bytes 61568 | tf_op jit(solution)/shard_map/ppermute | solution.py:18
  167.6 3.5 %collective-permute-start.44 = (bf16[4,24,2048]{2,1,0:T(8,128)(2,1)}, bf16[4,24,2048]{2,1,0:T(8,128)(2,1)}, u32[]{:S(2)}, u32[]{:S(2)}) collective-permute-start(bf16[4,24,2048]{2,1,0:T(8,128)(2,1)} %get-tuple-element.36), channel_id=1, source_target_pairs={{0,8},{1,9},{2,10},{3,11},{4,12},{5,13},{6,14},{7,15},{8,0},{9,1},... | collective-permute-start | bytes 1179656 | tf_op jit(solution)/shard_map/ppermute | solution.py:18
  171.6 2.7 %collective-permute-start.45 = (bf16[4,24,2048]{2,1,0:T(8,128)(2,1)}, bf16[4,24,2048]{2,1,0:T(8,128)(2,1)}, u32[]{:S(2)}, u32[]{:S(2)}) collective-permute-start(bf16[4,24,2048]{2,1,0:T(8,128)(2,1)} %get-tuple-element.36), channel_id=1, source_target_pairs={{0,12},{1,13},{2,14},{3,15},{4,0},{5,1},{6,2},{7,3},{8,4},{9,5},{1... | collective-permute-start | bytes 1179656 | tf_op jit(solution)/shard_map/ppermute | solution.py:18
  176.7 2.9 %collective-permute-done.44 = bf16[4,24,2048]{2,1,0:T(8,128)(2,1)} collective-permute-done((bf16[4,24,2048]{2,1,0:T(8,128)(2,1)}, bf16[4,24,2048]{2,1,0:T(8,128)(2,1)}, u32[]{:S(2)}, u32[]{:S(2)}) %collective-permute-start.44) | collective-permute-done | bytes 393248 | tf_op jit(solution)/shard_map/ppermute | solution.py:18
  179.6 4.1 %collective-permute-done.43 = bf16[4,24,2048]{2,1,0:T(8,128)(2,1)} collective-permute-done((bf16[4,24,2048]{2,1,0:T(8,128)(2,1)}, bf16[4,24,2048]{2,1,0:T(8,128)(2,1)}, u32[]{:S(2)}, u32[]{:S(2)}) %collective-permute-start.43) | collective-permute-done | bytes 393248 | tf_op jit(solution)/shard_map/ppermute | solution.py:18
  185.5 4.0 %fusion.15 = bf16[384,1024]{1,0:T(8,128)(2,1)S(1)} fusion(bf16[384,2048]{1,0:T(8,128)(2,1)S(1)} %bitcast.267, bf16[1,2048,1024]{2,1,0:T(8,128)(2,1)} %param.14), kind=kOutput, calls=%fused_computation.29 | convolution fusion | flops 1611005952 | bytes 6553600 | tf_op jit(solution)/shard_map/dot_general | solution.py:165
  191.9 3.2 %collective-permute-start.48 = (bf16[3,32,1024]{2,1,0:T(8,128)(2,1)S(1)}, bf16[3,32,1024]{2,1,0:T(8,128)(2,1)S(1)}, u32[]{:S(2)}, u32[]{:S(2)}) collective-permute-start(bf16[3,32,1024]{2,1,0:T(8,128)(2,1)S(1)} %get-tuple-element.30), channel_id=1, source_target_pairs={{0,48},{16,0},{32,16},{48,32},{1,49},{17,1},{33,17},{49,33},{2,50}... | collective-permute-start | bytes 589832 | tf_op jit(solution)/shard_map/ppermute | solution.py:18
  195.9 3.9 %collective-permute-done.46 = bf16[3,32,1024]{2,1,0:T(8,128)(2,1)S(1)} collective-permute-done((bf16[3,32,1024]{2,1,0:T(8,128)(2,1)S(1)}, bf16[3,32,1024]{2,1,0:T(8,128)(2,1)S(1)}, u32[]{:S(2)}, u32[]{:S(2)}) %collective-permute-start.46) | collective-permute-done | bytes 196640 | tf_op jit(solution)/shard_map/ppermute | solution.py:18
  (263 shorter events, 120.4 us)
Async XLA Ops:
  0.6 12.7 %collective-permute-start = (bf16[3,32,1024]{2,1,0:T(8,128)(2,1)}, bf16[3,32,1024]{2,1,0:T(8,128)(2,1)S(1)}, u32[]{:S(2)}, u32[]{:S(2)}) collective-permute-start(bf16[3,32,1024]{2,1,0:T(8,128)(2,1)} %param.10), channel_id=1, source_target_pairs={{0,16},{16,32},{32,48},{48,0},{1,17},{17,33},{33,49},{49,1},{2,18}... | collective-permute-start | bytes 589832 | tf_op jit(solution)/shard_map/ppermute | solution.py:18
  2.3 11.1 %collective-permute-start.2 = (bf16[3,32,1024]{2,1,0:T(8,128)(2,1)}, bf16[3,32,1024]{2,1,0:T(8,128)(2,1)S(1)}, u32[]{:S(2)}, u32[]{:S(2)}) collective-permute-start(bf16[3,32,1024]{2,1,0:T(8,128)(2,1)} %param.10), channel_id=1, source_target_pairs={{0,48},{16,0},{32,16},{48,32},{1,49},{17,1},{33,17},{49,33},{2,50}... | collective-permute-start | bytes 589832 | tf_op jit(solution)/shard_map/ppermute | solution.py:18
  25.6 11.6 %collective-permute-start.9 = (bf16[4,24,1280]{2,1,0:T(8,128)(2,1)}, bf16[4,24,1280]{2,1,0:T(8,128)(2,1)}, u32[]{:S(2)}, u32[]{:S(2)}) collective-permute-start(bf16[4,24,1280]{2,1,0:T(8,128)(2,1)} %get-tuple-element.26), channel_id=1, source_target_pairs={{0,1},{1,2},{2,3},{3,0},{4,5},{5,6},{6,7},{7,4},{8,9},{9,10},{10,1... | collective-permute-start | bytes 737288 | tf_op jit(solution)/shard_map/ppermute | solution.py:18
  27.2 11.8 %collective-permute-start.11 = (bf16[4,24,1280]{2,1,0:T(8,128)(2,1)}, bf16[4,24,1280]{2,1,0:T(8,128)(2,1)}, u32[]{:S(2)}, u32[]{:S(2)}) collective-permute-start(bf16[4,24,1280]{2,1,0:T(8,128)(2,1)} %get-tuple-element.27), channel_id=1, source_target_pairs={{0,3},{1,0},{2,1},{3,2},{4,7},{5,4},{6,5},{7,6},{8,11},{9,8},{10,9... | collective-permute-start | bytes 737288 | tf_op jit(solution)/shard_map/ppermute | solution.py:18
  28.9 11.6 %collective-permute-start.10 = (bf16[4,24,1280]{2,1,0:T(8,128)(2,1)}, bf16[4,24,1280]{2,1,0:T(8,128)(2,1)}, u32[]{:S(2)}, u32[]{:S(2)}) collective-permute-start(bf16[4,24,1280]{2,1,0:T(8,128)(2,1)} %get-tuple-element.28), channel_id=1, source_target_pairs={{0,2},{1,3},{2,0},{3,1},{4,6},{5,7},{6,4},{7,5},{8,10},{9,11},{10,... | collective-permute-start | bytes 737288 | tf_op jit(solution)/shard_map/ppermute | solution.py:18
  33.0 13.2 %collective-permute-start.3 = (bf16[4,24,1282]{2,1,0:T(8,128)(2,1)S(1)}, bf16[4,24,1282]{2,1,0:T(8,128)(2,1)S(1)}, u32[]{:S(2)}, u32[]{:S(2)}) collective-permute-start(bf16[4,24,1282]{2,1,0:T(8,128)(2,1)S(1)} %get-tuple-element.20), channel_id=1, source_target_pairs={{0,4},{1,5},{2,6},{3,7},{4,8},{5,9},{6,10},{7,11},{8,12},{9,13},{1... | collective-permute-start | bytes 738440 | tf_op jit(solution)/shard_map/ppermute | solution.py:18
  35.0 14.6 %collective-permute-start.5 = (bf16[4,24,1282]{2,1,0:T(8,128)(2,1)S(1)}, bf16[4,24,1282]{2,1,0:T(8,128)(2,1)S(1)}, u32[]{:S(2)}, u32[]{:S(2)}) collective-permute-start(bf16[4,24,1282]{2,1,0:T(8,128)(2,1)S(1)} %get-tuple-element.21), channel_id=1, source_target_pairs={{0,12},{1,13},{2,14},{3,15},{4,0},{5,1},{6,2},{7,3},{8,4},{9,5},{1... | collective-permute-start | bytes 738440 | tf_op jit(solution)/shard_map/ppermute | solution.py:18
  37.2 13.0 %collective-permute-start.4 = (bf16[4,24,1282]{2,1,0:T(8,128)(2,1)S(1)}, bf16[4,24,1282]{2,1,0:T(8,128)(2,1)S(1)}, u32[]{:S(2)}, u32[]{:S(2)}) collective-permute-start(bf16[4,24,1282]{2,1,0:T(8,128)(2,1)S(1)} %get-tuple-element.22), channel_id=1, source_target_pairs={{0,8},{1,9},{2,10},{3,11},{4,12},{5,13},{6,14},{7,15},{8,0},{9,1},... | collective-permute-start | bytes 738440 | tf_op jit(solution)/shard_map/ppermute | solution.py:18
  42.0 11.7 %collective-permute-start.12 = (bf16[24,1280]{1,0:T(8,128)(2,1)S(1)}, bf16[24,1280]{1,0:T(8,128)(2,1)S(1)}, u32[]{:S(2)}, u32[]{:S(2)}) collective-permute-start(bf16[24,1280]{1,0:T(8,128)(2,1)S(1)} %get-tuple-element.48), channel_id=1, source_target_pairs={{0,4},{1,5},{2,6},{3,7},{4,8},{5,9},{6,10},{7,11},{8,12},{9,13},{1... | collective-permute-start | bytes 184328 | tf_op jit(solution)/shard_map/ppermute | solution.py:18
  44.0 10.1 %collective-permute-start.14 = (bf16[24,1280]{1,0:T(8,128)(2,1)S(1)}, bf16[24,1280]{1,0:T(8,128)(2,1)S(1)}, u32[]{:S(2)}, u32[]{:S(2)}) collective-permute-start(bf16[24,1280]{1,0:T(8,128)(2,1)S(1)} %get-tuple-element.49), channel_id=1, source_target_pairs={{0,12},{1,13},{2,14},{3,15},{4,0},{5,1},{6,2},{7,3},{8,4},{9,5},{1... | collective-permute-start | bytes 184328 | tf_op jit(solution)/shard_map/ppermute | solution.py:18
  69.8 13.3 %collective-permute-start.18 = (bf16[4,24,2048]{2,1,0:T(8,128)(2,1)S(1)}, bf16[4,24,2048]{2,1,0:T(8,128)(2,1)S(1)}, u32[]{:S(2)}, u32[]{:S(2)}) collective-permute-start(bf16[4,24,2048]{2,1,0:T(8,128)(2,1)S(1)} %get-tuple-element.38), channel_id=1, source_target_pairs={{0,4},{1,5},{2,6},{3,7},{4,8},{5,9},{6,10},{7,11},{8,12},{9,13},{1... | collective-permute-start | bytes 1179656 | tf_op jit(solution)/shard_map/ppermute | solution.py:18
  71.9 11.3 %collective-permute-start.20 = (bf16[4,24,2048]{2,1,0:T(8,128)(2,1)S(1)}, bf16[4,24,2048]{2,1,0:T(8,128)(2,1)S(1)}, u32[]{:S(2)}, u32[]{:S(2)}) collective-permute-start(bf16[4,24,2048]{2,1,0:T(8,128)(2,1)S(1)} %get-tuple-element.38), channel_id=1, source_target_pairs={{0,12},{1,13},{2,14},{3,15},{4,0},{5,1},{6,2},{7,3},{8,4},{9,5},{1... | collective-permute-start | bytes 1179656 | tf_op jit(solution)/shard_map/ppermute | solution.py:18
  88.2 11.0 %collective-permute-start.23 = (bf16[96,1024]{1,0:T(8,128)(2,1)S(1)}, bf16[96,1024]{1,0:T(8,128)(2,1)S(1)}, u32[]{:S(2)}, u32[]{:S(2)}) collective-permute-start(bf16[96,1024]{1,0:T(8,128)(2,1)S(1)} %get-tuple-element.33), channel_id=1, source_target_pairs={{0,48},{16,0},{32,16},{48,32},{1,49},{17,1},{33,17},{49,33},{2,50}... | collective-permute-start | bytes 589832 | tf_op jit(solution)/shard_map/ppermute | solution.py:18
  122.0 15.0 %collective-permute-start.34 = (bf16[4,24,1280]{2,1,0:T(8,128)(2,1)}, bf16[4,24,1280]{2,1,0:T(8,128)(2,1)}, u32[]{:S(2)}, u32[]{:S(2)}) collective-permute-start(bf16[4,24,1280]{2,1,0:T(8,128)(2,1)} %get-tuple-element.23), channel_id=1, source_target_pairs={{0,1},{1,2},{2,3},{3,0},{4,5},{5,6},{6,7},{7,4},{8,9},{9,10},{10,1... | collective-permute-start | bytes 737288 | tf_op jit(solution)/shard_map/ppermute | solution.py:18
  123.1 14.0 %collective-permute-start.36 = (bf16[4,24,1280]{2,1,0:T(8,128)(2,1)}, bf16[4,24,1280]{2,1,0:T(8,128)(2,1)}, u32[]{:S(2)}, u32[]{:S(2)}) collective-permute-start(bf16[4,24,1280]{2,1,0:T(8,128)(2,1)} %get-tuple-element.24), channel_id=1, source_target_pairs={{0,3},{1,0},{2,1},{3,2},{4,7},{5,4},{6,5},{7,6},{8,11},{9,8},{10,9... | collective-permute-start | bytes 737288 | tf_op jit(solution)/shard_map/ppermute | solution.py:18
  125.2 11.8 %collective-permute-start.35 = (bf16[4,24,1280]{2,1,0:T(8,128)(2,1)}, bf16[4,24,1280]{2,1,0:T(8,128)(2,1)}, u32[]{:S(2)}, u32[]{:S(2)}) collective-permute-start(bf16[4,24,1280]{2,1,0:T(8,128)(2,1)} %get-tuple-element.25), channel_id=1, source_target_pairs={{0,2},{1,3},{2,0},{3,1},{4,6},{5,7},{6,4},{7,5},{8,10},{9,11},{10,... | collective-permute-start | bytes 737288 | tf_op jit(solution)/shard_map/ppermute | solution.py:18
  131.4 16.3 %collective-permute-start.28 = (bf16[4,24,1282]{2,1,0:T(8,128)(2,1)S(1)}, bf16[4,24,1282]{2,1,0:T(8,128)(2,1)S(1)}, u32[]{:S(2)}, u32[]{:S(2)}) collective-permute-start(bf16[4,24,1282]{2,1,0:T(8,128)(2,1)S(1)} %get-tuple-element.17), channel_id=1, source_target_pairs={{0,4},{1,5},{2,6},{3,7},{4,8},{5,9},{6,10},{7,11},{8,12},{9,13},{1... | collective-permute-start | bytes 738440 | tf_op jit(solution)/shard_map/ppermute | solution.py:18
  133.0 14.7 %collective-permute-start.30 = (bf16[4,24,1282]{2,1,0:T(8,128)(2,1)S(1)}, bf16[4,24,1282]{2,1,0:T(8,128)(2,1)S(1)}, u32[]{:S(2)}, u32[]{:S(2)}) collective-permute-start(bf16[4,24,1282]{2,1,0:T(8,128)(2,1)S(1)} %get-tuple-element.18), channel_id=1, source_target_pairs={{0,12},{1,13},{2,14},{3,15},{4,0},{5,1},{6,2},{7,3},{8,4},{9,5},{1... | collective-permute-start | bytes 738440 | tf_op jit(solution)/shard_map/ppermute | solution.py:18
  137.0 10.7 %collective-permute-start.29 = (bf16[4,24,1282]{2,1,0:T(8,128)(2,1)S(1)}, bf16[4,24,1282]{2,1,0:T(8,128)(2,1)S(1)}, u32[]{:S(2)}, u32[]{:S(2)}) collective-permute-start(bf16[4,24,1282]{2,1,0:T(8,128)(2,1)S(1)} %get-tuple-element.19), channel_id=1, source_target_pairs={{0,8},{1,9},{2,10},{3,11},{4,12},{5,13},{6,14},{7,15},{8,0},{9,1},... | collective-permute-start | bytes 738440 | tf_op jit(solution)/shard_map/ppermute | solution.py:18
  138.5 12.7 %collective-permute-start.37 = (bf16[24,1280]{1,0:T(8,128)(2,1)S(1)}, bf16[24,1280]{1,0:T(8,128)(2,1)S(1)}, u32[]{:S(2)}, u32[]{:S(2)}) collective-permute-start(bf16[24,1280]{1,0:T(8,128)(2,1)S(1)} %get-tuple-element.45), channel_id=1, source_target_pairs={{0,4},{1,5},{2,6},{3,7},{4,8},{5,9},{6,10},{7,11},{8,12},{9,13},{1... | collective-permute-start | bytes 184328 | tf_op jit(solution)/shard_map/ppermute | solution.py:18
  140.8 12.3 %collective-permute-start.39 = (bf16[24,1280]{1,0:T(8,128)(2,1)S(1)}, bf16[24,1280]{1,0:T(8,128)(2,1)S(1)}, u32[]{:S(2)}, u32[]{:S(2)}) collective-permute-start(bf16[24,1280]{1,0:T(8,128)(2,1)S(1)} %get-tuple-element.46), channel_id=1, source_target_pairs={{0,12},{1,13},{2,14},{3,15},{4,0},{5,1},{6,2},{7,3},{8,4},{9,5},{1... | collective-permute-start | bytes 184328 | tf_op jit(solution)/shard_map/ppermute | solution.py:18
  167.6 12.1 %collective-permute-start.44 = (bf16[4,24,2048]{2,1,0:T(8,128)(2,1)}, bf16[4,24,2048]{2,1,0:T(8,128)(2,1)}, u32[]{:S(2)}, u32[]{:S(2)}) collective-permute-start(bf16[4,24,2048]{2,1,0:T(8,128)(2,1)} %get-tuple-element.36), channel_id=1, source_target_pairs={{0,8},{1,9},{2,10},{3,11},{4,12},{5,13},{6,14},{7,15},{8,0},{9,1},... | collective-permute-start | bytes 1179656 | tf_op jit(solution)/shard_map/ppermute | solution.py:18
  171.1 12.6 %collective-permute-start.43 = (bf16[4,24,2048]{2,1,0:T(8,128)(2,1)}, bf16[4,24,2048]{2,1,0:T(8,128)(2,1)}, u32[]{:S(2)}, u32[]{:S(2)}) collective-permute-start(bf16[4,24,2048]{2,1,0:T(8,128)(2,1)} %get-tuple-element.36), channel_id=1, source_target_pairs={{0,4},{1,5},{2,6},{3,7},{4,8},{5,9},{6,10},{7,11},{8,12},{9,13},{1... | collective-permute-start | bytes 1179656 | tf_op jit(solution)/shard_map/ppermute | solution.py:18
  171.6 12.5 %collective-permute-start.45 = (bf16[4,24,2048]{2,1,0:T(8,128)(2,1)}, bf16[4,24,2048]{2,1,0:T(8,128)(2,1)}, u32[]{:S(2)}, u32[]{:S(2)}) collective-permute-start(bf16[4,24,2048]{2,1,0:T(8,128)(2,1)} %get-tuple-element.36), channel_id=1, source_target_pairs={{0,12},{1,13},{2,14},{3,15},{4,0},{5,1},{6,2},{7,3},{8,4},{9,5},{1... | collective-permute-start | bytes 1179656 | tf_op jit(solution)/shard_map/ppermute | solution.py:18
  (49 other events, 346.6 us)

commit v9 on v6

--- a/solution.py
+++ b/solution.py
@@ -152,11 +152,18 @@
             preferred_element_type=f32,
         ) * scale
         s_fresh = jnp.where(valid[:, None, None], s_fresh, -1e30)
-        scores = jnp.concatenate([s_cache, s_fresh], axis=-1)
-        weights = jax.nn.softmax(scores, axis=-1).astype(bf16)
-        values = jnp.concatenate([cache_local[..., HEAD_SIZE:], fresh[..., HEAD_SIZE:]], axis=2)
+        top = jnp.maximum(
+            jnp.max(s_cache, axis=-1, keepdims=True), jnp.max(s_fresh, axis=-1, keepdims=True)
+        )
+        e_cache = jnp.exp(s_cache - top)
+        e_fresh = jnp.exp(s_fresh - top)
+        denom = jnp.sum(e_cache, axis=-1, keepdims=True) + jnp.sum(e_fresh, axis=-1, keepdims=True)
+        w_cache = (e_cache / denom).astype(bf16)
+        w_fresh = (e_fresh / denom).astype(bf16)
         attended = jnp.einsum(
-            "shgrjl,shld->srjhgd", weights, values, preferred_element_type=f32
+            "shgrjl,shld->srjhgd", w_cache, cache_local[..., HEAD_SIZE:], preferred_element_type=f32
+        ) + jnp.einsum(
+            "shgrjl,shld->srjhgd", w_fresh, fresh[..., HEAD_SIZE:], preferred_element_type=f32
         )
         attended = attended.astype(bf16).reshape(own_rows, query_cols)
         by_z = jnp.stack([attended] + [along_z(attended, k) for k in range(1, n_z)])

time: 205 us -> 206 us (level)
  transfers between devices with their start and end apart: 49 -> 49, of which waited for: 29 -> 30; matrix products, arithmetic and copies ran while one was open for 12% -> 11% of each run, Pallas kernels for 0% -> 0%
where the time goes in v9:
time: 206 us; the launch traced here: 205 us
  starting transfers between devices  73 us (35%)
  waiting for transfers between devices  71.1 us (35%)
  local copies, waits for them, and re-layouts  22.9 us (11%)
  matrix products  19.6 us (10%)
  other arithmetic  17 us (8%)
    ppermute x48, starting transfers between devices, shifted(): return lax.ppermute(x, axis, [(i, fn(i, n)) for i in range(n)])  71.6 us
    ppermute x48, waiting for transfers between devices, shifted(): return lax.ppermute(x, axis, [(i, fn(i, n)) for i in range(n)])  70.7 us
    dot_general x2, matrix products, layer(): jnp.dot(gathered, w_out[0], preferred_element_type=f32).astype(bf16)  5.81 us
    dot_general x2, matrix products, layer(): rest = jnp.dot(xg, w_query[0, :, cut:], preferred_element_type=f32)  4.59 us
    dot_general x2, matrix products, layer(): jnp.dot(xg, w_query[0, :, :cut], preferred_element_type=f32).astype(bf16)  4.18 us
    concatenate x2, local copies, waits for them, and re-layouts, layer(): jnp.concatenate([rest.astype(bf16), second.astype(bf16), sq_hi, sq_lo], a...  4.14 us
  transfers between devices with their start and end apart: 49, of which 30 were waited for; matrix products, arithmetic and copies ran while one was open for 11% of the time, Pallas kernels for 0%

profile of v9, /device:TPU:0, one launch (start us, length us, event | category | flops | bytes accessed | tf_op | source)
XLA Modules:
  0.0 205.1 jit_solution(3061353986258407089)
XLA Ops:
  46.1 3.5 %collective-permute-start.7 = (bf16[24,1280]{1,0:T(8,128)(2,1)S(1)}, bf16[24,1280]{1,0:T(8,128)(2,1)S(1)}, u32[]{:S(2)}, u32[]{:S(2)}) collective-permute-start(bf16[24,1280]{1,0:T(8,128)(2,1)S(1)} %get-tuple-element.50), channel_id=1, source_target_pairs={{0,8},{1,9},{2,10},{3,11},{4,12},{5,13},{6,14},{7,15},{8,0},{9,1},... | collective-permute-start | bytes 184328 | tf_op jit(solution)/shard_map/ppermute | solution.py:18
  56.2 3.2 %collective-permute-done.13 = bf16[24,1282]{1,0:T(8,128)(2,1)S(1)} collective-permute-done((bf16[24,1282]{1,0:T(8,128)(2,1)S(1)}, bf16[24,1282]{1,0:T(8,128)(2,1)S(1)}, u32[]{:S(2)}, u32[]{:S(2)}) %collective-permute-start.13) | collective-permute-done | bytes 61568 | tf_op jit(solution)/shard_map/ppermute | solution.py:18
  66.4 3.1 %collective-permute-done.16 = bf16[24,2048]{1,0:T(8,128)(2,1)S(1)} collective-permute-done((bf16[24,2048]{1,0:T(8,128)(2,1)S(1)}, bf16[24,2048]{1,0:T(8,128)(2,1)S(1)}, u32[]{:S(2)}, u32[]{:S(2)}) %collective-permute-start.16) | collective-permute-done | bytes 98336 | tf_op jit(solution)/shard_map/ppermute | solution.py:18
  72.3 2.6 %collective-permute-start.20 = (bf16[4,24,2048]{2,1,0:T(8,128)(2,1)S(1)}, bf16[4,24,2048]{2,1,0:T(8,128)(2,1)S(1)}, u32[]{:S(2)}, u32[]{:S(2)}) collective-permute-start(bf16[4,24,2048]{2,1,0:T(8,128)(2,1)S(1)} %get-tuple-element.38), channel_id=1, source_target_pairs={{0,3},{1,0},{2,1},{3,2},{4,7},{5,4},{6,5},{7,6},{8,11},{9,8},{10,9... | collective-permute-start | bytes 1179656 | tf_op jit(solution)/shard_map/ppermute | solution.py:18
  75.5 4.8 %collective-permute-done.19 = bf16[4,24,2048]{2,1,0:T(8,128)(2,1)S(1)} collective-permute-done((bf16[4,24,2048]{2,1,0:T(8,128)(2,1)S(1)}, bf16[4,24,2048]{2,1,0:T(8,128)(2,1)S(1)}, u32[]{:S(2)}, u32[]{:S(2)}) %collective-permute-start.19) | collective-permute-done | bytes 393248 | tf_op jit(solution)/shard_map/ppermute | solution.py:18
  80.3 4.1 %collective-permute-done.18 = bf16[4,24,2048]{2,1,0:T(8,128)(2,1)S(1)} collective-permute-done((bf16[4,24,2048]{2,1,0:T(8,128)(2,1)S(1)}, bf16[4,24,2048]{2,1,0:T(8,128)(2,1)S(1)}, u32[]{:S(2)}, u32[]{:S(2)}) %collective-permute-start.18) | collective-permute-done | bytes 393248 | tf_op jit(solution)/shard_map/ppermute | solution.py:18
  92.3 9.1 %collective-permute-done.21 = bf16[96,1024]{1,0:T(8,128)(2,1)S(1)} collective-permute-done((bf16[96,1024]{1,0:T(8,128)(2,1)S(1)}, bf16[96,1024]{1,0:T(8,128)(2,1)S(1)}, u32[]{:S(2)}, u32[]{:S(2)}) %collective-permute-start.21) | collective-permute-done | bytes 196640 | tf_op jit(solution)/shard_map/ppermute | solution.py:18
  107.3 3.1 %collective-permute-done.25 = bf16[96,1024]{1,0:T(8,128)(2,1)S(1)} collective-permute-done((bf16[96,1024]{1,0:T(8,128)(2,1)S(1)}, bf16[96,1024]{1,0:T(8,128)(2,1)S(1)}, u32[]{:S(2)}, u32[]{:S(2)}) %collective-permute-start.25) | collective-permute-done | bytes 196640 | tf_op jit(solution)/shard_map/ppermute | solution.py:18
  118.6 2.9 %convolution_convert_fusion = bf16[384,1280]{1,0:T(8,128)(2,1)S(1)} fusion(bf16[1,1024,2048]{2,1,0:T(8,128)(2,1)} %param.12, bf16[384,1024]{1,0:T(8,128)(2,1)S(1)} %collective-permute-done.27, f32[1024]{0:T(1024)S(1)} %bitcast.328), kind=kOutput, calls=%fused_computation.12 | convolution fusion | flops 1008304128 | bytes 4395008 | tf_op jit(solution)/shard_map/dot_general | solution.py:127
  123.1 2.6 %collective-permute-start.30 = (bf16[4,24,1280]{2,1,0:T(8,128)(2,1)}, bf16[4,24,1280]{2,1,0:T(8,128)(2,1)}, u32[]{:S(2)}, u32[]{:S(2)}) collective-permute-start(bf16[4,24,1280]{2,1,0:T(8,128)(2,1)} %get-tuple-element.24), channel_id=1, source_target_pairs={{0,3},{1,0},{2,1},{3,2},{4,7},{5,4},{6,5},{7,6},{8,11},{9,8},{10,9... | collective-permute-start | bytes 737288 | tf_op jit(solution)/shard_map/ppermute | solution.py:18
  132.0 2.8 %collective-permute-start.36 = (bf16[4,24,1282]{2,1,0:T(8,128)(2,1)S(1)}, bf16[4,24,1282]{2,1,0:T(8,128)(2,1)S(1)}, u32[]{:S(2)}, u32[]{:S(2)}) collective-permute-start(bf16[4,24,1282]{2,1,0:T(8,128)(2,1)S(1)} %get-tuple-element.18), channel_id=1, source_target_pairs={{0,12},{1,13},{2,14},{3,15},{4,0},{5,1},{6,2},{7,3},{8,4},{9,5},{1... | collective-permute-start | bytes 738440 | tf_op jit(solution)/shard_map/ppermute | solution.py:18
  134.8 2.7 %collective-permute-done.28 = bf16[4,24,1280]{2,1,0:T(8,128)(2,1)} collective-permute-done((bf16[4,24,1280]{2,1,0:T(8,128)(2,1)}, bf16[4,24,1280]{2,1,0:T(8,128)(2,1)}, u32[]{:S(2)}, u32[]{:S(2)}) %collective-permute-start.28) | collective-permute-done | bytes 245792 | tf_op jit(solution)/shard_map/ppermute | solution.py:18
  140.3 3.2 %collective-permute-start.33 = (bf16[24,1280]{1,0:T(8,128)(2,1)S(1)}, bf16[24,1280]{1,0:T(8,128)(2,1)S(1)}, u32[]{:S(2)}, u32[]{:S(2)}) collective-permute-start(bf16[24,1280]{1,0:T(8,128)(2,1)S(1)} %get-tuple-element.46), channel_id=1, source_target_pairs={{0,12},{1,13},{2,14},{3,15},{4,0},{5,1},{6,2},{7,3},{8,4},{9,5},{1... | collective-permute-start | bytes 184328 | tf_op jit(solution)/shard_map/ppermute | solution.py:18
  144.6 3.3 %collective-permute-done.36 = bf16[4,24,1282]{2,1,0:T(8,128)(2,1)S(1)} collective-permute-done((bf16[4,24,1282]{2,1,0:T(8,128)(2,1)S(1)}, bf16[4,24,1282]{2,1,0:T(8,128)(2,1)S(1)}, u32[]{:S(2)}, u32[]{:S(2)}) %collective-permute-start.36) | collective-permute-done | bytes 246176 | tf_op jit(solution)/shard_map/ppermute | solution.py:18
  148.5 3.2 %collective-permute-start.39 = (bf16[24,1282]{1,0:T(8,128)(2,1)S(1)}, bf16[24,1282]{1,0:T(8,128)(2,1)S(1)}, u32[]{:S(2)}, u32[]{:S(2)}) collective-permute-start(bf16[24,1282]{1,0:T(8,128)(2,1)S(1)} %get-tuple-element.40), channel_id=1, source_target_pairs={{0,3},{1,0},{2,1},{3,2},{4,7},{5,4},{6,5},{7,6},{8,11},{9,8},{10,9... | collective-permute-start | bytes 184616 | tf_op jit(solution)/shard_map/ppermute | solution.py:18
  154.5 3.0 %collective-permute-done.38 = bf16[24,1282]{1,0:T(8,128)(2,1)S(1)} collective-permute-done((bf16[24,1282]{1,0:T(8,128)(2,1)S(1)}, bf16[24,1282]{1,0:T(8,128)(2,1)S(1)}, u32[]{:S(2)}, u32[]{:S(2)}) %collective-permute-start.38) | collective-permute-done | bytes 61568 | tf_op jit(solution)/shard_map/ppermute | solution.py:18
  159.8 3.4 %collective-permute-start.42 = (bf16[24,2048]{1,0:T(8,128)(2,1)S(1)}, bf16[24,2048]{1,0:T(8,128)(2,1)S(1)}, u32[]{:S(2)}, u32[]{:S(2)}) collective-permute-start(bf16[24,2048]{1,0:T(8,128)(2,1)S(1)} %reshape.710), channel_id=1, source_target_pairs={{0,12},{1,13},{2,14},{3,15},{4,0},{5,1},{6,2},{7,3},{8,4},{9,5},{1... | collective-permute-start | bytes 294920 | tf_op jit(solution)/shard_map/ppermute | solution.py:18
  166.4 3.0 %collective-permute-done.41 = bf16[24,2048]{1,0:T(8,128)(2,1)S(1)} collective-permute-done((bf16[24,2048]{1,0:T(8,128)(2,1)S(1)}, bf16[24,2048]{1,0:T(8,128)(2,1)S(1)}, u32[]{:S(2)}, u32[]{:S(2)}) %collective-permute-start.41) | collective-permute-done | bytes 98336 | tf_op jit(solution)/shard_map/ppermute | solution.py:18
  172.7 3.2 %collective-permute-start.45 = (bf16[4,24,2048]{2,1,0:T(8,128)(2,1)}, bf16[4,24,2048]{2,1,0:T(8,128)(2,1)}, u32[]{:S(2)}, u32[]{:S(2)}) collective-permute-start(bf16[4,24,2048]{2,1,0:T(8,128)(2,1)} %get-tuple-element.36), channel_id=1, source_target_pairs={{0,3},{1,0},{2,1},{3,2},{4,7},{5,4},{6,5},{7,6},{8,11},{9,8},{10,9... | collective-permute-start | bytes 1179656 | tf_op jit(solution)/shard_map/ppermute | solution.py:18
  178.4 3.5 %collective-permute-done.44 = bf16[4,24,2048]{2,1,0:T(8,128)(2,1)} collective-permute-done((bf16[4,24,2048]{2,1,0:T(8,128)(2,1)}, bf16[4,24,2048]{2,1,0:T(8,128)(2,1)}, u32[]{:S(2)}, u32[]{:S(2)}) %collective-permute-start.44) | collective-permute-done | bytes 393248 | tf_op jit(solution)/shard_map/ppermute | solution.py:18
  181.9 4.1 %collective-permute-done.43 = bf16[4,24,2048]{2,1,0:T(8,128)(2,1)} collective-permute-done((bf16[4,24,2048]{2,1,0:T(8,128)(2,1)}, bf16[4,24,2048]{2,1,0:T(8,128)(2,1)}, u32[]{:S(2)}, u32[]{:S(2)}) %collective-permute-start.43) | collective-permute-done | bytes 393248 | tf_op jit(solution)/shard_map/ppermute | solution.py:18
  187.4 4.0 %fusion.15 = bf16[384,1024]{1,0:T(8,128)(2,1)S(1)} fusion(bf16[384,2048]{1,0:T(8,128)(2,1)S(1)} %bitcast.285, bf16[1,2048,1024]{2,1,0:T(8,128)(2,1)} %param.14), kind=kOutput, calls=%fused_computation.29 | convolution fusion | flops 1611005952 | bytes 6553600 | tf_op jit(solution)/shard_map/dot_general | solution.py:172
  193.8 3.2 %collective-permute-start.48 = (bf16[3,32,1024]{2,1,0:T(8,128)(2,1)S(1)}, bf16[3,32,1024]{2,1,0:T(8,128)(2,1)S(1)}, u32[]{:S(2)}, u32[]{:S(2)}) collective-permute-start(bf16[3,32,1024]{2,1,0:T(8,128)(2,1)S(1)} %get-tuple-element.30), channel_id=1, source_target_pairs={{0,48},{16,0},{32,16},{48,32},{1,49},{17,1},{33,17},{49,33},{2,50}... | collective-permute-start | bytes 589832 | tf_op jit(solution)/shard_map/ppermute | solution.py:18
  197.7 4.1 %collective-permute-done.46 = bf16[3,32,1024]{2,1,0:T(8,128)(2,1)S(1)} collective-permute-done((bf16[3,32,1024]{2,1,0:T(8,128)(2,1)S(1)}, bf16[3,32,1024]{2,1,0:T(8,128)(2,1)S(1)}, u32[]{:S(2)}, u32[]{:S(2)}) %collective-permute-start.46) | collective-permute-done | bytes 196640 | tf_op jit(solution)/shard_map/ppermute | solution.py:18
  (262 shorter events, 117.6 us)
Async XLA Ops:
  0.6 11.1 %collective-permute-start = (bf16[3,32,1024]{2,1,0:T(8,128)(2,1)}, bf16[3,32,1024]{2,1,0:T(8,128)(2,1)S(1)}, u32[]{:S(2)}, u32[]{:S(2)}) collective-permute-start(bf16[3,32,1024]{2,1,0:T(8,128)(2,1)} %param.10), channel_id=1, source_target_pairs={{0,16},{16,32},{32,48},{48,0},{1,17},{17,33},{33,49},{49,1},{2,18}... | collective-permute-start | bytes 589832 | tf_op jit(solution)/shard_map/ppermute | solution.py:18
  25.6 11.6 %collective-permute-start.3 = (bf16[4,24,1280]{2,1,0:T(8,128)(2,1)}, bf16[4,24,1280]{2,1,0:T(8,128)(2,1)}, u32[]{:S(2)}, u32[]{:S(2)}) collective-permute-start(bf16[4,24,1280]{2,1,0:T(8,128)(2,1)} %get-tuple-element.26), channel_id=1, source_target_pairs={{0,1},{1,2},{2,3},{3,0},{4,5},{5,6},{6,7},{7,4},{8,9},{9,10},{10,1... | collective-permute-start | bytes 737288 | tf_op jit(solution)/shard_map/ppermute | solution.py:18
  27.2 11.8 %collective-permute-start.5 = (bf16[4,24,1280]{2,1,0:T(8,128)(2,1)}, bf16[4,24,1280]{2,1,0:T(8,128)(2,1)}, u32[]{:S(2)}, u32[]{:S(2)}) collective-permute-start(bf16[4,24,1280]{2,1,0:T(8,128)(2,1)} %get-tuple-element.27), channel_id=1, source_target_pairs={{0,3},{1,0},{2,1},{3,2},{4,7},{5,4},{6,5},{7,6},{8,11},{9,8},{10,9... | collective-permute-start | bytes 737288 | tf_op jit(solution)/shard_map/ppermute | solution.py:18
  28.8 11.6 %collective-permute-start.4 = (bf16[4,24,1280]{2,1,0:T(8,128)(2,1)}, bf16[4,24,1280]{2,1,0:T(8,128)(2,1)}, u32[]{:S(2)}, u32[]{:S(2)}) collective-permute-start(bf16[4,24,1280]{2,1,0:T(8,128)(2,1)} %get-tuple-element.28), channel_id=1, source_target_pairs={{0,2},{1,3},{2,0},{3,1},{4,6},{5,7},{6,4},{7,5},{8,10},{9,11},{10,... | collective-permute-start | bytes 737288 | tf_op jit(solution)/shard_map/ppermute | solution.py:18
  33.0 13.2 %collective-permute-start.9 = (bf16[4,24,1282]{2,1,0:T(8,128)(2,1)S(1)}, bf16[4,24,1282]{2,1,0:T(8,128)(2,1)S(1)}, u32[]{:S(2)}, u32[]{:S(2)}) collective-permute-start(bf16[4,24,1282]{2,1,0:T(8,128)(2,1)S(1)} %get-tuple-element.20), channel_id=1, source_target_pairs={{0,4},{1,5},{2,6},{3,7},{4,8},{5,9},{6,10},{7,11},{8,12},{9,13},{1... | collective-permute-start | bytes 738440 | tf_op jit(solution)/shard_map/ppermute | solution.py:18
  34.9 14.6 %collective-permute-start.11 = (bf16[4,24,1282]{2,1,0:T(8,128)(2,1)S(1)}, bf16[4,24,1282]{2,1,0:T(8,128)(2,1)S(1)}, u32[]{:S(2)}, u32[]{:S(2)}) collective-permute-start(bf16[4,24,1282]{2,1,0:T(8,128)(2,1)S(1)} %get-tuple-element.21), channel_id=1, source_target_pairs={{0,12},{1,13},{2,14},{3,15},{4,0},{5,1},{6,2},{7,3},{8,4},{9,5},{1... | collective-permute-start | bytes 738440 | tf_op jit(solution)/shard_map/ppermute | solution.py:18
  37.2 13.0 %collective-permute-start.10 = (bf16[4,24,1282]{2,1,0:T(8,128)(2,1)S(1)}, bf16[4,24,1282]{2,1,0:T(8,128)(2,1)S(1)}, u32[]{:S(2)}, u32[]{:S(2)}) collective-permute-start(bf16[4,24,1282]{2,1,0:T(8,128)(2,1)S(1)} %get-tuple-element.22), channel_id=1, source_target_pairs={{0,8},{1,9},{2,10},{3,11},{4,12},{5,13},{6,14},{7,15},{8,0},{9,1},... | collective-permute-start | bytes 738440 | tf_op jit(solution)/shard_map/ppermute | solution.py:18
  41.9 11.7 %collective-permute-start.6 = (bf16[24,1280]{1,0:T(8,128)(2,1)S(1)}, bf16[24,1280]{1,0:T(8,128)(2,1)S(1)}, u32[]{:S(2)}, u32[]{:S(2)}) collective-permute-start(bf16[24,1280]{1,0:T(8,128)(2,1)S(1)} %get-tuple-element.48), channel_id=1, source_target_pairs={{0,4},{1,5},{2,6},{3,7},{4,8},{5,9},{6,10},{7,11},{8,12},{9,13},{1... | collective-permute-start | bytes 184328 | tf_op jit(solution)/shard_map/ppermute | solution.py:18
  43.9 10.2 %collective-permute-start.8 = (bf16[24,1280]{1,0:T(8,128)(2,1)S(1)}, bf16[24,1280]{1,0:T(8,128)(2,1)S(1)}, u32[]{:S(2)}, u32[]{:S(2)}) collective-permute-start(bf16[24,1280]{1,0:T(8,128)(2,1)S(1)} %get-tuple-element.49), channel_id=1, source_target_pairs={{0,12},{1,13},{2,14},{3,15},{4,0},{5,1},{6,2},{7,3},{8,4},{9,5},{1... | collective-permute-start | bytes 184328 | tf_op jit(solution)/shard_map/ppermute | solution.py:18
  71.6 12.8 %collective-permute-start.18 = (bf16[4,24,2048]{2,1,0:T(8,128)(2,1)S(1)}, bf16[4,24,2048]{2,1,0:T(8,128)(2,1)S(1)}, u32[]{:S(2)}, u32[]{:S(2)}) collective-permute-start(bf16[4,24,2048]{2,1,0:T(8,128)(2,1)S(1)} %get-tuple-element.38), channel_id=1, source_target_pairs={{0,1},{1,2},{2,3},{3,0},{4,5},{5,6},{6,7},{7,4},{8,9},{9,10},{10,1... | collective-permute-start | bytes 1179656 | tf_op jit(solution)/shard_map/ppermute | solution.py:18
  72.3 12.2 %collective-permute-start.20 = (bf16[4,24,2048]{2,1,0:T(8,128)(2,1)S(1)}, bf16[4,24,2048]{2,1,0:T(8,128)(2,1)S(1)}, u32[]{:S(2)}, u32[]{:S(2)}) collective-permute-start(bf16[4,24,2048]{2,1,0:T(8,128)(2,1)S(1)} %get-tuple-element.38), channel_id=1, source_target_pairs={{0,3},{1,0},{2,1},{3,2},{4,7},{5,4},{6,5},{7,6},{8,11},{9,8},{10,9... | collective-permute-start | bytes 1179656 | tf_op jit(solution)/shard_map/ppermute | solution.py:18
  88.8 12.6 %collective-permute-start.21 = (bf16[96,1024]{1,0:T(8,128)(2,1)S(1)}, bf16[96,1024]{1,0:T(8,128)(2,1)S(1)}, u32[]{:S(2)}, u32[]{:S(2)}) collective-permute-start(bf16[96,1024]{1,0:T(8,128)(2,1)S(1)} %get-tuple-element.32), channel_id=1, source_target_pairs={{0,16},{16,32},{32,48},{48,0},{1,17},{17,33},{33,49},{49,1},{2,18}... | collective-permute-start | bytes 589832 | tf_op jit(solution)/shard_map/ppermute | solution.py:18
  89.8 11.5 %collective-permute-start.23 = (bf16[96,1024]{1,0:T(8,128)(2,1)S(1)}, bf16[96,1024]{1,0:T(8,128)(2,1)S(1)}, u32[]{:S(2)}, u32[]{:S(2)}) collective-permute-start(bf16[96,1024]{1,0:T(8,128)(2,1)S(1)} %get-tuple-element.33), channel_id=1, source_target_pairs={{0,48},{16,0},{32,16},{48,32},{1,49},{17,1},{33,17},{49,33},{2,50}... | collective-permute-start | bytes 589832 | tf_op jit(solution)/shard_map/ppermute | solution.py:18
  122.5 15.0 %collective-permute-start.28 = (bf16[4,24,1280]{2,1,0:T(8,128)(2,1)}, bf16[4,24,1280]{2,1,0:T(8,128)(2,1)}, u32[]{:S(2)}, u32[]{:S(2)}) collective-permute-start(bf16[4,24,1280]{2,1,0:T(8,128)(2,1)} %get-tuple-element.23), channel_id=1, source_target_pairs={{0,1},{1,2},{2,3},{3,0},{4,5},{5,6},{6,7},{7,4},{8,9},{9,10},{10,1... | collective-permute-start | bytes 737288 | tf_op jit(solution)/shard_map/ppermute | solution.py:18
  123.1 15.7 %collective-permute-start.30 = (bf16[4,24,1280]{2,1,0:T(8,128)(2,1)}, bf16[4,24,1280]{2,1,0:T(8,128)(2,1)}, u32[]{:S(2)}, u32[]{:S(2)}) collective-permute-start(bf16[4,24,1280]{2,1,0:T(8,128)(2,1)} %get-tuple-element.24), channel_id=1, source_target_pairs={{0,3},{1,0},{2,1},{3,2},{4,7},{5,4},{6,5},{7,6},{8,11},{9,8},{10,9... | collective-permute-start | bytes 737288 | tf_op jit(solution)/shard_map/ppermute | solution.py:18
  125.7 13.1 %collective-permute-start.29 = (bf16[4,24,1280]{2,1,0:T(8,128)(2,1)}, bf16[4,24,1280]{2,1,0:T(8,128)(2,1)}, u32[]{:S(2)}, u32[]{:S(2)}) collective-permute-start(bf16[4,24,1280]{2,1,0:T(8,128)(2,1)} %get-tuple-element.25), channel_id=1, source_target_pairs={{0,2},{1,3},{2,0},{3,1},{4,6},{5,7},{6,4},{7,5},{8,10},{9,11},{10,... | collective-permute-start | bytes 737288 | tf_op jit(solution)/shard_map/ppermute | solution.py:18
  131.5 12.1 %collective-permute-start.34 = (bf16[4,24,1282]{2,1,0:T(8,128)(2,1)S(1)}, bf16[4,24,1282]{2,1,0:T(8,128)(2,1)S(1)}, u32[]{:S(2)}, u32[]{:S(2)}) collective-permute-start(bf16[4,24,1282]{2,1,0:T(8,128)(2,1)S(1)} %get-tuple-element.17), channel_id=1, source_target_pairs={{0,4},{1,5},{2,6},{3,7},{4,8},{5,9},{6,10},{7,11},{8,12},{9,13},{1... | collective-permute-start | bytes 738440 | tf_op jit(solution)/shard_map/ppermute | solution.py:18
  132.0 15.9 %collective-permute-start.36 = (bf16[4,24,1282]{2,1,0:T(8,128)(2,1)S(1)}, bf16[4,24,1282]{2,1,0:T(8,128)(2,1)S(1)}, u32[]{:S(2)}, u32[]{:S(2)}) collective-permute-start(bf16[4,24,1282]{2,1,0:T(8,128)(2,1)S(1)} %get-tuple-element.18), channel_id=1, source_target_pairs={{0,12},{1,13},{2,14},{3,15},{4,0},{5,1},{6,2},{7,3},{8,4},{9,5},{1... | collective-permute-start | bytes 738440 | tf_op jit(solution)/shard_map/ppermute | solution.py:18
  137.5 10.8 %collective-permute-start.35 = (bf16[4,24,1282]{2,1,0:T(8,128)(2,1)S(1)}, bf16[4,24,1282]{2,1,0:T(8,128)(2,1)S(1)}, u32[]{:S(2)}, u32[]{:S(2)}) collective-permute-start(bf16[4,24,1282]{2,1,0:T(8,128)(2,1)S(1)} %get-tuple-element.19), channel_id=1, source_target_pairs={{0,8},{1,9},{2,10},{3,11},{4,12},{5,13},{6,14},{7,15},{8,0},{9,1},... | collective-permute-start | bytes 738440 | tf_op jit(solution)/shard_map/ppermute | solution.py:18
  140.3 11.5 %collective-permute-start.31 = (bf16[24,1280]{1,0:T(8,128)(2,1)S(1)}, bf16[24,1280]{1,0:T(8,128)(2,1)S(1)}, u32[]{:S(2)}, u32[]{:S(2)}) collective-permute-start(bf16[24,1280]{1,0:T(8,128)(2,1)S(1)} %get-tuple-element.45), channel_id=1, source_target_pairs={{0,4},{1,5},{2,6},{3,7},{4,8},{5,9},{6,10},{7,11},{8,12},{9,13},{1... | collective-permute-start | bytes 184328 | tf_op jit(solution)/shard_map/ppermute | solution.py:18
  140.3 13.2 %collective-permute-start.33 = (bf16[24,1280]{1,0:T(8,128)(2,1)S(1)}, bf16[24,1280]{1,0:T(8,128)(2,1)S(1)}, u32[]{:S(2)}, u32[]{:S(2)}) collective-permute-start(bf16[24,1280]{1,0:T(8,128)(2,1)S(1)} %get-tuple-element.46), channel_id=1, source_target_pairs={{0,12},{1,13},{2,14},{3,15},{4,0},{5,1},{6,2},{7,3},{8,4},{9,5},{1... | collective-permute-start | bytes 184328 | tf_op jit(solution)/shard_map/ppermute | solution.py:18
  171.1 10.8 %collective-permute-start.44 = (bf16[4,24,2048]{2,1,0:T(8,128)(2,1)}, bf16[4,24,2048]{2,1,0:T(8,128)(2,1)}, u32[]{:S(2)}, u32[]{:S(2)}) collective-permute-start(bf16[4,24,2048]{2,1,0:T(8,128)(2,1)} %get-tuple-element.36), channel_id=1, source_target_pairs={{0,2},{1,3},{2,0},{3,1},{4,6},{5,7},{6,4},{7,5},{8,10},{9,11},{10,... | collective-permute-start | bytes 1179656 | tf_op jit(solution)/shard_map/ppermute | solution.py:18
  172.7 13.2 %collective-permute-start.43 = (bf16[4,24,2048]{2,1,0:T(8,128)(2,1)}, bf16[4,24,2048]{2,1,0:T(8,128)(2,1)}, u32[]{:S(2)}, u32[]{:S(2)}) collective-permute-start(bf16[4,24,2048]{2,1,0:T(8,128)(2,1)} %get-tuple-element.36), channel_id=1, source_target_pairs={{0,1},{1,2},{2,3},{3,0},{4,5},{5,6},{6,7},{7,4},{8,9},{9,10},{10,1... | collective-permute-start | bytes 1179656 | tf_op jit(solution)/shard_map/ppermute | solution.py:18
  172.7 13.2 %collective-permute-start.45 = (bf16[4,24,2048]{2,1,0:T(8,128)(2,1)}, bf16[4,24,2048]{2,1,0:T(8,128)(2,1)}, u32[]{:S(2)}, u32[]{:S(2)}) collective-permute-start(bf16[4,24,2048]{2,1,0:T(8,128)(2,1)} %get-tuple-element.36), channel_id=1, source_target_pairs={{0,3},{1,0},{2,1},{3,2},{4,7},{5,4},{6,5},{7,6},{8,11},{9,8},{10,9... | collective-permute-start | bytes 1179656 | tf_op jit(solution)/shard_map/ppermute | solution.py:18
  (47 other events, 352.1 us)
